TPU v7x, 32 devices: a whole 2x2x4 slice. The times are simulated.
32 devices in a mesh: wave: 4 (over y, core), lev: 4 (over z), cpl: 2 (over x).
Axes of the slice: x: 2, y: 2, z: 4, core: 2. Of those that a mesh axis runs over, the one named last changes fastest.
Arguments:
- spectral: bfloat16 [1280, 2, 4, 24, 1280], P('wave', None, None, 'lev'), may hold values from -0.125 to 0.125
- legendre: bfloat16 [1280, 16, 1280], P('wave', 'cpl'), may hold values from -0.15625 to 0.15625
- wavenumber: int32 [1280], replicated, may hold values from 0 to 1279, each once
- level_weight: float32 [24], P('lev'), may hold values from 0.1 to 1
- source_row: int32 [16], replicated, may hold values from 0 to 14
- row_weight: float32 [16], replicated, may hold values from 0.2 to 0.8
Outputs:
- ocean_flux: float32 [16, 4, 4320], P(('wave', 'cpl'), None, 'lev')
All inputs are finite; a program needn't handle non-finite values.
Results may differ from a plain program's by a relative error of at most 0.0041.
Values may be sent and summed in bfloat16 or wider, within the bound.
No kernel may reach another device: no remote copies, remote signals or barrier semaphores. Data moves between devices by JAX's collectives and lax.ppermute only.
A program may use at most 192 MiB of HBM per device.

v0:
```python
import math

import jax
import jax.numpy as jnp
from jax import lax
from jax.sharding import PartitionSpec as P

NLON = 4320


def phase_angle(phase, lon_total):
    return phase.astype(jnp.float32) * (2.0 * math.pi / lon_total)


def surface_flux(grid_vals, level_weight):
    wind_speed = jnp.sqrt(grid_vals[..., 0, :, :] ** 2 + grid_vals[..., 1, :, :] ** 2 + 0.25)
    return jnp.sum(level_weight[:, None] * wind_speed[..., None, :, :] * grid_vals, axis=-2)


def latitude_order(gathered, wave_count, cpl_count, lat_dev):
    trailing = gathered.shape[1:]
    gathered = gathered.reshape((wave_count, cpl_count, lat_dev) + trailing)
    gathered = jnp.swapaxes(gathered, 0, 1)
    return gathered.reshape((wave_count * cpl_count * lat_dev,) + trailing)


def interpolate(gathered, source, weight_hi):
    lower = jnp.take(gathered, source, axis=0)
    upper = jnp.take(gathered, source + 1, axis=0)
    return (1.0 - weight_hi[:, None, None]) * lower + weight_hi[:, None, None] * upper


def local(spectral, legendre, wavenumber, level_weight, source_row, row_weight):
    slot_count = spectral.shape[0]
    fields = spectral.shape[2]
    levels = spectral.shape[3]
    degree = spectral.shape[4]
    channels = 2 * fields * levels
    wave_count = lax.axis_size("wave")
    cpl_count = lax.axis_size("cpl")
    wave_at = lax.axis_index("wave")
    cpl_at = lax.axis_index("cpl")
    owned_waves = lax.dynamic_slice_in_dim(wavenumber, wave_at * slot_count, slot_count)
    coefficient = spectral.reshape(slot_count, channels, degree)
    in_triangle = (
        lax.broadcasted_iota(jnp.int32, (slot_count, 1, degree), 2)
        < (degree - owned_waves)[:, None, None]
    )
    coefficient = jnp.where(in_triangle, coefficient, jnp.zeros_like(coefficient))
    spec_grid = jnp.einsum(
        "skj,slj->slk", coefficient, legendre, preferred_element_type=jnp.float32
    ).astype(jnp.bfloat16)
    by_latitude = lax.all_to_all(spec_grid, "wave", split_axis=1, concat_axis=0, tiled=True)
    total_slots = by_latitude.shape[0]
    lat_dev = by_latitude.shape[1]
    rows_in = (
        by_latitude.reshape(total_slots, lat_dev, 2, fields * levels)
        .transpose(1, 3, 0, 2)
        .reshape(lat_dev * fields * levels, 2 * total_slots)
    )
    lon_block = NLON // 8
    factor = jnp.where(wavenumber == 0, 1.0, 2.0).astype(jnp.float32)[:, None]
    offsets = jnp.arange(lon_block, dtype=jnp.int32)
    base_angle = phase_angle(wavenumber[:, None] * offsets[None, :] % NLON, NLON)
    base_cos = jnp.cos(base_angle)
    base_sin = jnp.sin(base_angle)

    def one_block(first_lon):
        start_angle = phase_angle(wavenumber * first_lon % NLON, NLON)[:, None]
        start_cos = jnp.cos(start_angle)
        start_sin = jnp.sin(start_angle)
        cos_vals = start_cos * base_cos - start_sin * base_sin
        sin_vals = start_sin * base_cos + start_cos * base_sin
        fourier = (
            jnp.stack([factor * cos_vals, -factor * sin_vals], axis=1)
            .astype(jnp.bfloat16)
            .reshape(2 * total_slots, lon_block)
        )
        grid_vals = jnp.dot(rows_in, fourier, preferred_element_type=jnp.float32).reshape(
            lat_dev, fields, levels, lon_block
        )
        return surface_flux(grid_vals, level_weight)

    block_starts = jnp.arange(8, dtype=jnp.int32) * lon_block
    per_block = lax.map(one_block, block_starts)
    partial_value = per_block.transpose(1, 2, 0, 3).reshape(lat_dev, fields, NLON)
    own_first = (wave_at * cpl_count + cpl_at) * lat_dev
    source = lax.dynamic_slice_in_dim(source_row, own_first, lat_dev)
    weight_hi = lax.dynamic_slice_in_dim(row_weight, own_first, lat_dev)
    strip_width = NLON // lax.axis_size("lev")
    summed = lax.psum(partial_value, "lev")
    gathered = lax.all_gather(summed, ("wave", "cpl"), axis=0, tiled=True)
    gathered = latitude_order(gathered, wave_count, cpl_count, lat_dev)
    gathered = lax.dynamic_slice_in_dim(
        gathered, lax.axis_index("lev") * strip_width, strip_width, 2
    )
    return interpolate(gathered, source, weight_hi)


def solution(mesh):
    placed = (P("wave", None, None, "lev", None), P("wave", "cpl", None), P(), P("lev"), P(), P())
    return jax.shard_map(
        local,
        mesh=mesh,
        in_specs=placed,
        out_specs=P(("wave", "cpl"), None, "lev"),
        check_vma=False,
    )
```

profile of v0, /device:TPU:0, one launch (start us, length us, event | category | flops | bytes accessed | tf_op | source)
XLA Modules:
  0.0 437.1 jit_solution(12876540771261802303)
XLA Ops:
  6.5 0.8 dynamic-slice_subtract_fusion
  7.6 26.6 %copy.16 = bf16[320,2,4,6,1280]{4,0,3,2,1:T(8,128)(2,1)} copy(bf16[320,2,4,6,1280]{4,2,3,1,0:T(4,128)(2,1)} %param.10) | data formatting | bytes 78643200 | tf_op args[0]
  34.2 26.6 %bitcast_select_fusion = bf16[320,48,1280]{2,0,1:T(8,128)(2,1)} fusion(bf16[320,2,4,6,1280]{4,0,3,2,1:T(8,128)(2,1)} %copy.16, pred[320,1280]{1,0:T(8,128)(4,1)S(1)} %iota_compare_fusion), kind=kLoop, calls=%fused_computation.40 | loop fusion | flops 19660800 | bytes 79052800 | tf_op jit(solution)/shard_map/jit(_where)/select_n | solution.py:49
  60.8 47.0 %fusion.31 = bf16[320,8,48]{2,1,0:T(8,128)(2,1)S(1)} fusion(bf16[320,8,1280]{2,1,0:T(8,128)(2,1)} %param.11, bf16[320,48,1280]{2,0,1:T(8,128)(2,1)} %bitcast_select_fusion), kind=kOutput, calls=%fused_computation.45 | convolution fusion | flops 314695680 | bytes 46120960 | tf_op jit(solution)/shard_map/skj,slj->slk/dot_general | solution.py:50
  107.8 1.1 copy.18
  109.0 4.2 all-to-all-start
  113.3 6.3 %all-to-all-done = bf16[320,8,48]{0,2,1:T(8,128)(2,1)S(1)} async-done(((bf16[320,8,48]{0,2,1:T(8,128)(2,1)}), bf16[320,8,48]{0,2,1:T(8,128)(2,1)S(1)}, u32[]{:S(2)}, u32[]{:S(2)}) %all-to-all-start) | async-done | bytes 245792 | tf_op jit(solution)/shard_map/all_to_all | solution.py:53
  120.0 1.7 copy.20
  122.4 0.9 copy.21
  123.3 240.5 %while.14 = (s32[]{:T(128)}, f32[8,2,4,540]{3,2,1,0:T(4,128)}, f32[6]{0:T(128)S(1)}, f32[1280,1]{0,1:T(1,128)S(1)}, s32[8]{0:T(128)S(1)}, /*index=5*/s32[1280]{0...) while((s32[]{:T(128)}, f32[8,2,4,540]{3,2,1,0:T(4,128)}, ...), condition=%wide.region_2.3_spmd.clone.clone, body=%wide.region_0.2_spmd.clone.clone.sunk | while | flops 147317040 | bytes 22999700 | solution.py:85
  124.5 12.4 %fusion.47 = (bf16[1280,1,540]{0,2,1:T(8,128)(2,1)S(1)}, bf16[1280,1,540]{0,2,1:T(8,128)(2,1)S(1)}) fusion(s32[1280]{0:T(1024)S(1)} %get-tuple-element.302, f32[1280]{0:T(1024)S(1)} %get-tuple-element.273, f32[1280]{0:T(1024)S(1)} %get-tuple-element.274, f32[1280]{0:T(1024)S(1)} %reduce.4, f32[1280]{0:T(1024)S(1)} %reduce.5), kind=kLoop, calls=%fused_computation.12.clone.1 | loop fusion | flops 13132800 | bytes 2790400 | tf_op jit(solution)/shard_map/convert
  137.2 7.2 %copy.33 = bf16[1280,2,540]{2,1,0:T(2,128)(2,1)} copy(bf16[1280,2,540]{0,2,1:T(8,128)(2,1)S(1)} %pad_maximum_fusion.2) | data formatting | bytes 5529600 | tf_op jit(solution)/shard_map/while/body/eval_jaxpr/stack | solution.py:75
  144.4 6.6 %convert_element_type.80 = bf16[2560,540]{1,0:T(8,128)(2,1)S(1)} reshape(bf16[1280,2,540]{2,1,0:T(2,128)(2,1)} %copy.33) | data formatting | bytes 5529600 | tf_op jit(solution)/shard_map/while/body/eval_jaxpr/convert_element_type | solution.py:76
  151.0 1.5 convolution_bitcast_fusion.2
  154.6 12.4 %fusion.47 = (bf16[1280,1,540]{0,2,1:T(8,128)(2,1)S(1)}, bf16[1280,1,540]{0,2,1:T(8,128)(2,1)S(1)}) fusion(s32[1280]{0:T(1024)S(1)} %get-tuple-element.302, f32[1280]{0:T(1024)S(1)} %get-tuple-element.273, f32[1280]{0:T(1024)S(1)} %get-tuple-element.274, f32[1280]{0:T(1024)S(1)} %reduce.4, f32[1280]{0:T(1024)S(1)} %reduce.5), kind=kLoop, calls=%fused_computation.12.clone.1 | loop fusion | flops 13132800 | bytes 2790400 | tf_op jit(solution)/shard_map/convert
  167.3 7.2 %copy.33 = bf16[1280,2,540]{2,1,0:T(2,128)(2,1)} copy(bf16[1280,2,540]{0,2,1:T(8,128)(2,1)S(1)} %pad_maximum_fusion.2) | data formatting | bytes 5529600 | tf_op jit(solution)/shard_map/while/body/eval_jaxpr/stack | solution.py:75
  174.5 6.6 %convert_element_type.80 = bf16[2560,540]{1,0:T(8,128)(2,1)S(1)} reshape(bf16[1280,2,540]{2,1,0:T(2,128)(2,1)} %copy.33) | data formatting | bytes 5529600 | tf_op jit(solution)/shard_map/while/body/eval_jaxpr/convert_element_type | solution.py:76
  181.1 1.5 convolution_bitcast_fusion.2
  184.7 12.4 %fusion.47 = (bf16[1280,1,540]{0,2,1:T(8,128)(2,1)S(1)}, bf16[1280,1,540]{0,2,1:T(8,128)(2,1)S(1)}) fusion(s32[1280]{0:T(1024)S(1)} %get-tuple-element.302, f32[1280]{0:T(1024)S(1)} %get-tuple-element.273, f32[1280]{0:T(1024)S(1)} %get-tuple-element.274, f32[1280]{0:T(1024)S(1)} %reduce.4, f32[1280]{0:T(1024)S(1)} %reduce.5), kind=kLoop, calls=%fused_computation.12.clone.1 | loop fusion | flops 13132800 | bytes 2790400 | tf_op jit(solution)/shard_map/convert
  197.3 7.2 %copy.33 = bf16[1280,2,540]{2,1,0:T(2,128)(2,1)} copy(bf16[1280,2,540]{0,2,1:T(8,128)(2,1)S(1)} %pad_maximum_fusion.2) | data formatting | bytes 5529600 | tf_op jit(solution)/shard_map/while/body/eval_jaxpr/stack | solution.py:75
  204.5 6.6 %convert_element_type.80 = bf16[2560,540]{1,0:T(8,128)(2,1)S(1)} reshape(bf16[1280,2,540]{2,1,0:T(2,128)(2,1)} %copy.33) | data formatting | bytes 5529600 | tf_op jit(solution)/shard_map/while/body/eval_jaxpr/convert_element_type | solution.py:76
  211.2 1.5 convolution_bitcast_fusion.2
  214.7 12.4 %fusion.47 = (bf16[1280,1,540]{0,2,1:T(8,128)(2,1)S(1)}, bf16[1280,1,540]{0,2,1:T(8,128)(2,1)S(1)}) fusion(s32[1280]{0:T(1024)S(1)} %get-tuple-element.302, f32[1280]{0:T(1024)S(1)} %get-tuple-element.273, f32[1280]{0:T(1024)S(1)} %get-tuple-element.274, f32[1280]{0:T(1024)S(1)} %reduce.4, f32[1280]{0:T(1024)S(1)} %reduce.5), kind=kLoop, calls=%fused_computation.12.clone.1 | loop fusion | flops 13132800 | bytes 2790400 | tf_op jit(solution)/shard_map/convert
  227.4 7.2 %copy.33 = bf16[1280,2,540]{2,1,0:T(2,128)(2,1)} copy(bf16[1280,2,540]{0,2,1:T(8,128)(2,1)S(1)} %pad_maximum_fusion.2) | data formatting | bytes 5529600 | tf_op jit(solution)/shard_map/while/body/eval_jaxpr/stack | solution.py:75
  234.6 6.6 %convert_element_type.80 = bf16[2560,540]{1,0:T(8,128)(2,1)S(1)} reshape(bf16[1280,2,540]{2,1,0:T(2,128)(2,1)} %copy.33) | data formatting | bytes 5529600 | tf_op jit(solution)/shard_map/while/body/eval_jaxpr/convert_element_type | solution.py:76
  241.2 1.5 convolution_bitcast_fusion.2
  244.8 12.4 %fusion.47 = (bf16[1280,1,540]{0,2,1:T(8,128)(2,1)S(1)}, bf16[1280,1,540]{0,2,1:T(8,128)(2,1)S(1)}) fusion(s32[1280]{0:T(1024)S(1)} %get-tuple-element.302, f32[1280]{0:T(1024)S(1)} %get-tuple-element.273, f32[1280]{0:T(1024)S(1)} %get-tuple-element.274, f32[1280]{0:T(1024)S(1)} %reduce.4, f32[1280]{0:T(1024)S(1)} %reduce.5), kind=kLoop, calls=%fused_computation.12.clone.1 | loop fusion | flops 13132800 | bytes 2790400 | tf_op jit(solution)/shard_map/convert
  257.5 7.2 %copy.33 = bf16[1280,2,540]{2,1,0:T(2,128)(2,1)} copy(bf16[1280,2,540]{0,2,1:T(8,128)(2,1)S(1)} %pad_maximum_fusion.2) | data formatting | bytes 5529600 | tf_op jit(solution)/shard_map/while/body/eval_jaxpr/stack | solution.py:75
  264.7 6.6 %convert_element_type.80 = bf16[2560,540]{1,0:T(8,128)(2,1)S(1)} reshape(bf16[1280,2,540]{2,1,0:T(2,128)(2,1)} %copy.33) | data formatting | bytes 5529600 | tf_op jit(solution)/shard_map/while/body/eval_jaxpr/convert_element_type | solution.py:76
  271.3 1.5 convolution_bitcast_fusion.2
  274.9 12.4 %fusion.47 = (bf16[1280,1,540]{0,2,1:T(8,128)(2,1)S(1)}, bf16[1280,1,540]{0,2,1:T(8,128)(2,1)S(1)}) fusion(s32[1280]{0:T(1024)S(1)} %get-tuple-element.302, f32[1280]{0:T(1024)S(1)} %get-tuple-element.273, f32[1280]{0:T(1024)S(1)} %get-tuple-element.274, f32[1280]{0:T(1024)S(1)} %reduce.4, f32[1280]{0:T(1024)S(1)} %reduce.5), kind=kLoop, calls=%fused_computation.12.clone.1 | loop fusion | flops 13132800 | bytes 2790400 | tf_op jit(solution)/shard_map/convert
  287.5 7.2 %copy.33 = bf16[1280,2,540]{2,1,0:T(2,128)(2,1)} copy(bf16[1280,2,540]{0,2,1:T(8,128)(2,1)S(1)} %pad_maximum_fusion.2) | data formatting | bytes 5529600 | tf_op jit(solution)/shard_map/while/body/eval_jaxpr/stack | solution.py:75
  294.7 6.6 %convert_element_type.80 = bf16[2560,540]{1,0:T(8,128)(2,1)S(1)} reshape(bf16[1280,2,540]{2,1,0:T(2,128)(2,1)} %copy.33) | data formatting | bytes 5529600 | tf_op jit(solution)/shard_map/while/body/eval_jaxpr/convert_element_type | solution.py:76
  301.3 1.5 convolution_bitcast_fusion.2
  304.9 12.4 %fusion.47 = (bf16[1280,1,540]{0,2,1:T(8,128)(2,1)S(1)}, bf16[1280,1,540]{0,2,1:T(8,128)(2,1)S(1)}) fusion(s32[1280]{0:T(1024)S(1)} %get-tuple-element.302, f32[1280]{0:T(1024)S(1)} %get-tuple-element.273, f32[1280]{0:T(1024)S(1)} %get-tuple-element.274, f32[1280]{0:T(1024)S(1)} %reduce.4, f32[1280]{0:T(1024)S(1)} %reduce.5), kind=kLoop, calls=%fused_computation.12.clone.1 | loop fusion | flops 13132800 | bytes 2790400 | tf_op jit(solution)/shard_map/convert
  317.6 7.2 %copy.33 = bf16[1280,2,540]{2,1,0:T(2,128)(2,1)} copy(bf16[1280,2,540]{0,2,1:T(8,128)(2,1)S(1)} %pad_maximum_fusion.2) | data formatting | bytes 5529600 | tf_op jit(solution)/shard_map/while/body/eval_jaxpr/stack | solution.py:75
  324.8 6.6 %convert_element_type.80 = bf16[2560,540]{1,0:T(8,128)(2,1)S(1)} reshape(bf16[1280,2,540]{2,1,0:T(2,128)(2,1)} %copy.33) | data formatting | bytes 5529600 | tf_op jit(solution)/shard_map/while/body/eval_jaxpr/convert_element_type | solution.py:76
  331.4 1.5 convolution_bitcast_fusion.2
  335.0 12.4 %fusion.47 = (bf16[1280,1,540]{0,2,1:T(8,128)(2,1)S(1)}, bf16[1280,1,540]{0,2,1:T(8,128)(2,1)S(1)}) fusion(s32[1280]{0:T(1024)S(1)} %get-tuple-element.302, f32[1280]{0:T(1024)S(1)} %get-tuple-element.273, f32[1280]{0:T(1024)S(1)} %get-tuple-element.274, f32[1280]{0:T(1024)S(1)} %reduce.4, f32[1280]{0:T(1024)S(1)} %reduce.5), kind=kLoop, calls=%fused_computation.12.clone.1 | loop fusion | flops 13132800 | bytes 2790400 | tf_op jit(solution)/shard_map/convert
  347.7 7.2 %copy.33 = bf16[1280,2,540]{2,1,0:T(2,128)(2,1)} copy(bf16[1280,2,540]{0,2,1:T(8,128)(2,1)S(1)} %pad_maximum_fusion.2) | data formatting | bytes 5529600 | tf_op jit(solution)/shard_map/while/body/eval_jaxpr/stack | solution.py:75
  354.9 6.6 %convert_element_type.80 = bf16[2560,540]{1,0:T(8,128)(2,1)S(1)} reshape(bf16[1280,2,540]{2,1,0:T(2,128)(2,1)} %copy.33) | data formatting | bytes 5529600 | tf_op jit(solution)/shard_map/while/body/eval_jaxpr/convert_element_type | solution.py:76
  361.5 1.5 convolution_bitcast_fusion.2
  363.8 0.9 copy.22
  364.8 0.8 reshape.277
  365.6 35.4 %all-reduce.2.cloned.1.call-done = f32[2,4,4320]{2,1,0:T(4,128)} async-done(((f32[2,4,4320]{2,1,0:T(4,128)}), f32[2,4,4320]{2,1,0:T(4,128)}) %all-reduce.2.cloned.1.call-update) | async-done | bytes 138256 | tf_op jit(solution)/shard_map/psum | solution.py:91
  401.2 25.6 %all-gather.2.cloned.1.call-done = f32[16,4,4320]{2,1,0:T(4,128)} async-done(((f32[2,4,4320]{2,1,0:T(4,128)}), f32[16,4,4320]{2,1,0:T(4,128)}) %all-gather.2.cloned.1.call-update) | async-done | bytes 1105936 | tf_op jit(solution)/shard_map/all_gather | solution.py:92
  426.9 1.3 copy.23
  429.6 0.7 fusion.34
  (99 shorter events, 21.0 us)
Async XLA Ops:
  60.8 52.4 %copy-start = (s32[1280]{0:T(1024)S(1)}, s32[1280]{0:T(1024)}, u32[]{:S(2)}) copy-start(s32[1280]{0:T(1024)} %param.12) | copy-start | bytes 15364
  109.0 10.6 %all-to-all-start = ((bf16[320,8,48]{0,2,1:T(8,128)(2,1)}), bf16[320,8,48]{0,2,1:T(8,128)(2,1)S(1)}, u32[]{:S(2)}, u32[]{:S(2)}) async-start(bf16[320,8,48]{0,2,1:T(8,128)(2,1)} %copy.18), calls=%async_computation | async-start | bytes 589824 | tf_op jit(solution)/shard_map/all_to_all | solution.py:53
  113.2 287.8 %all-reduce.2.cloned.1.call-start = ((), (), s32[]{:S(2)}) async-start(), calls=%async_computation.1 | async-start | bytes 278528 | tf_op jit(solution)/shard_map/psum | solution.py:91
  113.2 10.0 %copy-start.1 = (f32[6]{0:T(128)S(1)}, f32[6]{0:T(128)}, u32[]{:S(2)}) copy-start(f32[6]{0:T(128)} %param.13) | copy-start | bytes 76
  123.3 277.8 %copy-start.2 = (f32[16]{0:T(128)S(1)}, f32[16]{0:T(128)}, u32[]{:S(2)}) copy-start(f32[16]{0:T(128)} %param.15) | copy-start | bytes 196
  123.3 277.9 %copy-start.3 = (s32[16]{0:T(128)S(1)}, s32[16]{0:T(128)}, u32[]{:S(2)}) copy-start(s32[16]{0:T(128)} %param.14) | copy-start | bytes 196
  365.6 61.3 %all-gather.2.cloned.1.call-start = ((), (), s32[]{:S(2)}) async-start(), calls=%async_computation.2 | async-start | bytes 1253376 | tf_op jit(solution)/shard_map/all_gather | solution.py:92
Sparse Core Ops, SparseCore 0:
  365.7 35.2 all-reduce.1
  403.0 23.7 all-gather.1
where the time goes:
time: 439 us; the launch traced here: 437 us
  local copies, waits for them, and re-layouts  156 us (36%)
  other arithmetic  136 us (31%)
  waiting for transfers between devices  67.4 us (15%)
  matrix products  59.3 us (14%)
  between operations  13.5 us (3%)
    another operation x24, other arithmetic  99.7 us
    another operation x8, local copies, waits for them, and re-layouts, one_block(): jnp.stack([factor * cos_vals, -factor * sin_vals], axis=1)  57.6 us
    convert_element_type x8, local copies, waits for them, and re-layouts, one_block(): fourier = jnp.stack([factor * cos_vals, -factor * sin_vals], axis=1).asty...  52.9 us
    dot_general x1, matrix products, local(): jnp.einsum('skj,slj->slk', coefficient, legendre, preferred_element_type=...  47 us
    psum x1, waiting for transfers between devices, local(): summed = lax.psum(partial_value, 'lev')  35.4 us
    unnamed x10, local copies, waits for them, and re-layouts  27.6 us
    select_n x1, other arithmetic, local(): jnp.where(in_triangle, coefficient, jnp.zeros_like(coefficient))  26.6 us
    all_gather x1, waiting for transfers between devices, local(): gathered = lax.all_gather(summed, ('wave', 'cpl'), axis=0, tiled=True)  25.6 us
  transfers between devices with their start and end apart: 3, of which 3 were waited for; matrix products, arithmetic and copies ran while one was open for 0% of the time, Pallas kernels for 0%

commit v1 on v0

v1 whole, which is shorter than its diff:
```python
import math

import jax
import jax.numpy as jnp
from jax import lax
from jax.sharding import PartitionSpec as P

NLON = 4320
LANE = 128


def phase_angle(phase, lon_total):
    return phase.astype(jnp.float32) * (2.0 * math.pi / lon_total)


def surface_flux(grid_vals, level_weight):
    wind_speed = jnp.sqrt(grid_vals[:, 0] ** 2 + grid_vals[:, 1] ** 2 + 0.25)
    return jnp.sum(level_weight[:, None] * wind_speed[:, None] * grid_vals, axis=2)


def latitude_order(gathered, wave_count, cpl_count, lat_dev):
    trailing = gathered.shape[1:]
    gathered = gathered.reshape((wave_count, cpl_count, lat_dev) + trailing)
    gathered = jnp.swapaxes(gathered, 0, 1)
    return gathered.reshape((wave_count * cpl_count * lat_dev,) + trailing)


def interpolate(gathered, source, weight_hi):
    lower = jnp.take(gathered, source, axis=0)
    upper = jnp.take(gathered, source + 1, axis=0)
    return (1.0 - weight_hi[:, None, None]) * lower + weight_hi[:, None, None] * upper


def quarter_tables(wavenumber, width):
    blocks = width // LANE
    factor = jnp.where(wavenumber == 0, 1.0, 2.0).astype(jnp.float32)[:, None]
    offsets = jnp.arange(LANE, dtype=jnp.int32)
    base_angle = phase_angle(wavenumber[:, None] * offsets[None, :] % NLON, NLON)
    base_cos = jnp.cos(base_angle)[:, None, :]
    base_sin = jnp.sin(base_angle)[:, None, :]
    starts = jnp.arange(blocks, dtype=jnp.int32) * LANE
    start_angle = phase_angle(wavenumber[:, None] * starts[None, :] % NLON, NLON)
    start_cos = (factor * jnp.cos(start_angle))[:, :, None]
    start_sin = (factor * jnp.sin(start_angle))[:, :, None]
    cos_tab = start_cos * base_cos - start_sin * base_sin
    sin_tab = start_sin * base_cos + start_cos * base_sin
    slots = wavenumber.shape[0]
    return (
        cos_tab.astype(jnp.bfloat16).reshape(slots, width),
        (-sin_tab).astype(jnp.bfloat16).reshape(slots, width),
    )


def local(spectral, legendre, wavenumber, level_weight, source_row, row_weight):
    slot_count = spectral.shape[0]
    fields = spectral.shape[2]
    levels = spectral.shape[3]
    degree = spectral.shape[4]
    channels = 2 * fields * levels
    wave_count = lax.axis_size("wave")
    cpl_count = lax.axis_size("cpl")
    lev_count = lax.axis_size("lev")
    wave_at = lax.axis_index("wave")
    cpl_at = lax.axis_index("cpl")
    owned_waves = lax.dynamic_slice_in_dim(wavenumber, wave_at * slot_count, slot_count)
    in_triangle = (
        lax.broadcasted_iota(jnp.int32, (slot_count, 1, degree), 2)
        < (degree - owned_waves)[:, None, None]
    )
    table_rows = jnp.where(in_triangle, legendre, jnp.zeros_like(legendre))
    coefficient = spectral.reshape(slot_count, channels, degree)
    spec_grid = jnp.einsum(
        "skj,slj->slk", coefficient, table_rows, preferred_element_type=jnp.float32
    ).astype(jnp.bfloat16)
    by_latitude = lax.all_to_all(spec_grid, "wave", split_axis=1, concat_axis=0, tiled=True)
    total_slots = by_latitude.shape[0]
    lat_dev = by_latitude.shape[1]
    rows = lat_dev * fields * levels
    parts = by_latitude.reshape(total_slots, lat_dev, 2, fields * levels)
    real = parts[:, :, 0].reshape(total_slots, rows).T
    imag = parts[:, :, 1].reshape(total_slots, rows).T
    parity = (1 - 2 * (wavenumber & 1)).astype(jnp.bfloat16)[None, :]
    lhs_cos = jnp.concatenate([real, real * parity], axis=0)
    lhs_sin = jnp.concatenate([imag, imag * parity], axis=0)

    quarter = NLON // 4
    width = -(-(quarter + 1) // LANE) * LANE
    cos_tab, sin_tab = quarter_tables(wavenumber, width)
    r_all = jnp.dot(lhs_cos, cos_tab, preferred_element_type=jnp.float32)
    q_all = jnp.dot(lhs_sin, sin_tab, preferred_element_type=jnp.float32)
    r1, r2 = r_all[:rows], r_all[rows:]
    q1, q2 = q_all[:rows], q_all[rows:]

    def flux_of(grid_rows):
        return surface_flux(grid_rows.reshape(lat_dev, fields, levels, quarter), level_weight)

    strip0 = flux_of((r1 + q1)[:, :quarter])
    strip1 = jnp.flip(flux_of((r2 - q2)[:, 1 : quarter + 1]), axis=-1)
    strip2 = flux_of((r2 + q2)[:, :quarter])
    strip3 = jnp.flip(flux_of((r1 - q1)[:, 1 : quarter + 1]), axis=-1)
    partial_value = jnp.concatenate([strip0, strip1, strip2, strip3], axis=-1)

    own_first = (wave_at * cpl_count + cpl_at) * lat_dev
    source = lax.dynamic_slice_in_dim(source_row, own_first, lat_dev)
    weight_hi = lax.dynamic_slice_in_dim(row_weight, own_first, lat_dev)
    summed = lax.psum_scatter(partial_value, "lev", scatter_dimension=2, tiled=True)
    gathered = lax.all_gather(summed, ("wave", "cpl"), axis=0, tiled=True)
    gathered = latitude_order(gathered, wave_count, cpl_count, lat_dev)
    del lev_count
    return interpolate(gathered, source, weight_hi)


def solution(mesh):
    placed = (P("wave", None, None, "lev", None), P("wave", "cpl", None), P(), P("lev"), P(), P())
    return jax.shard_map(
        local,
        mesh=mesh,
        in_specs=placed,
        out_specs=P(("wave", "cpl"), None, "lev"),
        check_vma=False,
    )
```

time: 439 us -> 169 us (0.38)
  other arithmetic: 136 us -> 12.4 us
  local copies, waits for them, and re-layouts: 156 us -> 33.7 us
  waiting for transfers between devices: 67.4 us -> 35.6 us
  blocking collectives: 0 us -> 16.7 us
  matrix products: 59.3 us -> 51.3 us
    another operation x32 -> x0, other arithmetic: 102 us -> none
    another operation x8 -> x0, local copies, waits for them, and re-layouts: 57.6 us -> none  [one_block(): jnp.stack([factor * cos_vals, -factor * sin_vals], axis=1)]
    convert_element_type x9 -> x1, local copies, waits for them, and re-layouts: 54 us -> 1.13 us  [local(): spec_grid = jnp.einsum('skj,slj->slk', coefficient, table_rows, preferred...]
    unnamed x2, waiting for transfers between devices: 0.03 us -> 35.6 us
    psum x1 -> x0, waiting for transfers between devices: 35.4 us -> none  [local(): summed = lax.psum(partial_value, 'lev')]
    select_n x1, other arithmetic: 26.6 us -> 0.01 us  [quarter_tables(): factor = jnp.where(wavenumber == 0, 1.0, 2.0).astype(jnp.float32)[:, None]]
    all_gather x1 -> x0, waiting for transfers between devices: 25.6 us -> none  [local(): gathered = lax.all_gather(summed, ('wave', 'cpl'), axis=0, tiled=True)]
    all_gather x0 -> x1, blocking collectives: none -> 16.7 us  [local(): gathered = lax.all_gather(summed, ('wave', 'cpl'), axis=0, tiled=True)]
  transfers between devices with their start and end apart: 3 -> 2, of which waited for: 3 -> 1; matrix products, arithmetic and copies ran while one was open for 0% -> 6% of each run, Pallas kernels for 0% -> 0%
where the time goes in v1:
time: 169 us; the launch traced here: 168 us
  matrix products  51.3 us (30%)
  waiting for transfers between devices  35.6 us (21%)
  local copies, waits for them, and re-layouts  33.7 us (20%)
  blocking collectives  16.7 us (10%)
  between operations  14.3 us (8%)
  other arithmetic  12.4 us (7%)
  starting transfers between devices  4.24 us (3%)
    dot_general x1, matrix products, local(): jnp.einsum('skj,slj->slk', coefficient, table_rows, preferred_element_typ...  47.4 us
    unnamed x2, waiting for transfers between devices  35.6 us
    unnamed x19, local copies, waits for them, and re-layouts  29.9 us
    all_gather x1, blocking collectives, local(): gathered = lax.all_gather(summed, ('wave', 'cpl'), axis=0, tiled=True)  16.7 us
    convert_element_type x1, other arithmetic, quarter_tables(): cos_tab.astype(jnp.bfloat16).reshape(slots, width)  4.6 us
    all_to_all x1, starting transfers between devices, local(): lax.all_to_all(spec_grid, 'wave', split_axis=1, concat_axis=0, tiled=True)  4.24 us
    cos x1, other arithmetic, quarter_tables(): base_cos = jnp.cos(base_angle)[:, None, :]  3.9 us
  transfers between devices with their start and end apart: 2, of which 1 were waited for; matrix products, arithmetic and copies ran while one was open for 6% of the time, Pallas kernels for 0%

profile of v1, /device:TPU:0, one launch (start us, length us, event | category | flops | bytes accessed | tf_op | source)
XLA Modules:
  0.0 168.1 jit_solution(15231933070154465908)
XLA Ops:
  6.5 0.8 dynamic-slice_subtract_fusion
  7.3 0.3 iota_compare_fusion
  7.6 26.6 %copy.14 = bf16[320,2,4,6,1280]{4,0,3,2,1:T(8,128)(2,1)} copy(bf16[320,2,4,6,1280]{4,2,3,1,0:T(4,128)(2,1)} %param.8) | data formatting | bytes 78643200 | tf_op args[0]
  34.3 0.0 copy-start
  34.3 0.0 copy-start.3
  34.3 47.4 %fusion.5 = bf16[320,8,48]{2,1,0:T(8,128)(2,1)S(1)} fusion(bf16[320,48,1280]{2,0,1:T(8,128)(2,1)} %bitcast.36, bf16[320,8,1280]{2,1,0:T(8,128)(2,1)} %param.9, pred[320,1280]{1,0:T(8,128)(4,1)S(1)} %iota_compare_fusion), kind=kOutput, calls=%fused_computation.10 | convolution fusion | flops 317972480 | bytes 46530560 | tf_op jit(solution)/shard_map/skj,slj->slk/dot_general | solution.py:72
  81.7 1.1 copy.16
  82.8 4.2 %all-to-all-start = ((bf16[320,8,48]{0,2,1:T(8,128)(2,1)}), bf16[320,8,48]{0,2,1:T(8,128)(2,1)S(1)}, u32[]{:S(2)}, u32[]{:S(2)}) async-start(bf16[320,8,48]{0,2,1:T(8,128)(2,1)} %copy.16), calls=%async_computation | async-start | bytes 589824 | tf_op jit(solution)/shard_map/all_to_all | solution.py:75
  87.1 0.0 all-reduce.3.cloned.1.call-start
  87.1 0.0 copy-done
  87.1 3.9 %fusion.15 = (f32[1280,128]{0,1:T(8,128)}, f32[1280,128]{0,1:T(8,128)}) fusion(s32[1280]{0:T(1024)S(1)} %copy-done), kind=kLoop, calls=%fused_computation.18 | loop fusion | flops 1474560 | bytes 1315840 | tf_op jit(solution)/shard_map/cos | solution.py:39
  91.0 0.4 cosine_multiply_fusion
  91.4 0.0 copy-done.3
  91.4 0.6 compare_and_fusion.1
  92.0 4.6 %subtract_convert_fusion = (bf16[1280,9,128]{0,2,1:T(8,128)(2,1)}, bf16[1280,9,128]{0,2,1:T(8,128)(2,1)S(1)}) fusion(f32[1280,128]{0,1:T(8,128)} %get-tuple-element.27, f32[1280,9]{0,1:T(8,128)S(1)} %get-tuple-element.25, f32[1280,128]{0,1:T(8,128)} %get-tuple-element.26, f32[1280,9]{0,1:T(8,128)S(1)} %get-tuple-element.24), kind=kLoop, calls=%fused_computation.7 | loop fusion | flops 13271040 | bytes 7301120 | tf_op jit(solution)/shard_map/convert_element_type | solution.py:49
  96.6 0.0 all-to-all-done
  96.6 0.2 copy.26
  96.8 0.3 reshape.214
  97.1 2.8 %fusion.17 = f32[96,1152]{1,0:T(8,128)S(1)} fusion(bf16[1280,1152]{0,1:T(8,128)(2,1)} %bitcast.38, bf16[48,1280]{1,0:T(8,128)(2,1)S(1)} %get-tuple-element.28, bf16[48,1280]{1,0:T(8,128)(2,1)S(1)} %bitcast.43), kind=kOutput, calls=%fused_computation.25 | convolution fusion | flops 283607040 | bytes 3637248 | tf_op jit(solution)/shard_map/dot_general | solution.py:89
  100.0 0.0 copy-start.2
  100.0 0.0 copy-start.4
  100.0 0.0 copy-start.5
  100.0 0.0 copy-start.1
  100.1 1.0 fusion.21
  101.1 0.3 slice_subtract_fusion
  101.6 0.0 copy-done.2
  101.6 0.2 fusion.34
  101.8 0.1 multiply_reduce_fusion
  101.9 0.8 reverse.1
  102.7 0.1 slice.163
  102.8 0.1 multiply_reduce_fusion.1
  102.9 0.1 multiply_reduce_fusion.2
  103.0 0.8 reverse
  103.8 0.1 slice.162
  103.9 0.1 multiply_reduce_fusion.3
  104.0 0.9 concatenate.11
  104.9 0.0 all-reduce.3.cloned.1.call-update
  104.9 0.0 copy-done.4
  104.9 0.1 broadcast_subtract_fusion
  105.0 0.0 copy-done.5
  105.0 0.6 dynamic-slice
  106.2 0.0 copy-done.1
  106.3 35.5 %all-reduce.3.cloned.1.call-done = f32[2,4,4320]{2,1,0:T(4,128)} async-done(((f32[2,4,4320]{2,1,0:T(4,128)}), f32[2,4,4320]{2,1,0:T(4,128)}) %all-reduce.3.cloned.1.call-update) | async-done | bytes 138256
  141.8 0.9 constant_dynamic-slice_fusion
  142.7 16.7 %all_gather.3 = f32[16,4,1080]{2,1,0:T(4,128)S(1)} all-gather(f32[2,4,1080]{2,1,0:T(4,128)S(1)} %constant_dynamic-slice_fusion), channel_id=1, replica_groups=mesh['wave'=4,'lev'=4,'cpl'=2] {'wave','cpl'}, dimensions={0}, use_global_device_ids=true | all-gather | bytes 311040 | tf_op jit(solution)/shard_map/all_gather | solution.py:107
  159.4 0.6 gather_fusion
  160.0 0.6 gather_fusion.1
  160.6 0.7 fusion.50
  (13 shorter events, 0.3 us)
Async XLA Ops:
  34.3 52.8 %copy-start = (s32[1280]{0:T(1024)S(1)}, s32[1280]{0:T(1024)}, u32[]{:S(2)}) copy-start(s32[1280]{0:T(1024)} %param.10) | copy-start | bytes 15364
  34.3 57.2 %copy-start.3 = (s32[16]{0:T(128)S(1)}, s32[16]{0:T(128)}, u32[]{:S(2)}) copy-start(s32[16]{0:T(128)} %param.12) | copy-start | bytes 196
  82.8 13.8 %all-to-all-start = ((bf16[320,8,48]{0,2,1:T(8,128)(2,1)}), bf16[320,8,48]{0,2,1:T(8,128)(2,1)S(1)}, u32[]{:S(2)}, u32[]{:S(2)}) async-start(bf16[320,8,48]{0,2,1:T(8,128)(2,1)} %copy.16), calls=%async_computation | async-start | bytes 589824 | tf_op jit(solution)/shard_map/all_to_all | solution.py:75
  87.1 54.7 %all-reduce.3.cloned.1.call-start = ((), (), s32[]{:S(2)}) async-start(), calls=%async_computation.1 | async-start | bytes 278528
  100.0 1.6 copy-start.2
  100.0 4.9 %copy-start.4 = (f32[16]{0:T(128)S(1)}, f32[16]{0:T(128)}, u32[]{:S(2)}) copy-start(f32[16]{0:T(128)} %param.13) | copy-start | bytes 196
  100.0 5.0 %copy-start.5 = (u32[32]{0:T(128)S(1)}, u32[32]{0:T(128)}, u32[]{:S(2)}) copy-start(u32[32]{0:T(128)} %constant.72) | copy-start | bytes 388
  100.0 6.2 %copy-start.1 = (s32[2]{0:T(128)S(1)}, s32[2]{0:T(128)}, u32[]{:S(2)}) copy-start(s32[2]{0:T(128)} %get-tuple-element.31) | copy-start | bytes 28
Sparse Core Ops, SparseCore 0:
  105.0 36.7 all-reduce.2

commit v2 on v1

--- a/solution.py
+++ b/solution.py
@@ -103,10 +103,15 @@
     own_first = (wave_at * cpl_count + cpl_at) * lat_dev
     source = lax.dynamic_slice_in_dim(source_row, own_first, lat_dev)
     weight_hi = lax.dynamic_slice_in_dim(row_weight, own_first, lat_dev)
-    summed = lax.psum_scatter(partial_value, "lev", scatter_dimension=2, tiled=True)
-    gathered = lax.all_gather(summed, ("wave", "cpl"), axis=0, tiled=True)
+    strip_width = NLON // lev_count
+    by_strip = partial_value.reshape(lat_dev, fields, lev_count, strip_width).transpose(2, 0, 1, 3)
+    summed = jnp.sum(
+        lax.all_to_all(by_strip, "lev", split_axis=0, concat_axis=0, tiled=True), axis=0
+    )
+    copies = jnp.broadcast_to(summed[None], (wave_count * cpl_count,) + summed.shape)
+    gathered = lax.all_to_all(copies, ("wave", "cpl"), split_axis=0, concat_axis=0, tiled=True)
+    gathered = gathered.reshape((wave_count * cpl_count * lat_dev,) + summed.shape[1:])
     gathered = latitude_order(gathered, wave_count, cpl_count, lat_dev)
-    del lev_count
     return interpolate(gathered, source, weight_hi)
 
 

time: 169 us -> 122 us (0.72)
  waiting for transfers between devices: 35.6 us -> 13.3 us
  blocking collectives: 16.7 us -> 0 us
  between operations: 14.3 us -> 0.22 us
  starting transfers between devices: 4.24 us -> 13.8 us
  other arithmetic: 12.4 us -> 9.35 us
    unnamed x2 -> x0, waiting for transfers between devices: 35.6 us -> none
    all_gather x1 -> x0, blocking collectives: 16.7 us -> none  [local(): gathered = lax.all_gather(summed, ('wave', 'cpl'), axis=0, tiled=True)]
    all_to_all x0 -> x2, waiting for transfers between devices: none -> 13.3 us  [the longest x1 6.64 us: local(): lax.all_to_all(by_strip, 'lev', split_axis=0, concat_axis=0, tiled=True)]
    all_to_all x0 -> x2, starting transfers between devices: none -> 9.53 us  [the longest x1 5.55 us: local(): lax.all_to_all(by_strip, 'lev', split_axis=0, concat_axis=0, tiled=True)]
    unnamed x19 -> x13, local copies, waits for them, and re-layouts: 29.9 us -> 28.4 us
  transfers between devices with their start and end apart: 2 -> 3, of which waited for: 1 -> 2; matrix products, arithmetic and copies ran while one was open for 6% -> 5% of each run, Pallas kernels for 0% -> 0%
where the time goes in v2:
time: 122 us; the launch traced here: 121 us
  matrix products  51.4 us (42%)
  local copies, waits for them, and re-layouts  33.2 us (27%)
  starting transfers between devices  13.8 us (11%)
  waiting for transfers between devices  13.3 us (11%)
  other arithmetic  9.35 us (8%)
    dot_general x1, matrix products, local(): jnp.einsum('skj,slj->slk', coefficient, table_rows, preferred_element_typ...  47.5 us
    unnamed x13, local copies, waits for them, and re-layouts  28.4 us
    all_to_all x1, waiting for transfers between devices, local(): lax.all_to_all(by_strip, 'lev', split_axis=0, concat_axis=0, tiled=True)  6.64 us
    all_to_all x1, waiting for transfers between devices, local(): lax.all_to_all(copies, ('wave', 'cpl'), split_axis=0, concat_axis=0, tile...  6.63 us
    all_to_all x1, starting transfers between devices, local(): lax.all_to_all(by_strip, 'lev', split_axis=0, concat_axis=0, tiled=True)  5.55 us
    all_to_all x1, starting transfers between devices, local(): lax.all_to_all(spec_grid, 'wave', split_axis=1, concat_axis=0, tiled=True)  4.24 us
    all_to_all x1, starting transfers between devices, local(): lax.all_to_all(copies, ('wave', 'cpl'), split_axis=0, concat_axis=0, tile...  3.98 us
    convert_element_type x1, other arithmetic, quarter_tables(): cos_tab.astype(jnp.bfloat16).reshape(slots, width)  3.34 us
  transfers between devices with their start and end apart: 3, of which 2 were waited for; matrix products, arithmetic and copies ran while one was open for 5% of the time, Pallas kernels for 0%

profile of v2, /device:TPU:0, one launch (start us, length us, event | category | flops | bytes accessed | tf_op | source)
XLA Modules:
  0.0 121.1 jit_solution(9876910115910982764)
XLA Ops:
  0.0 0.8 dynamic-slice_subtract_fusion
  0.8 0.3 iota_compare_fusion
  1.1 26.6 %copy.19 = bf16[320,2,4,6,1280]{4,0,3,2,1:T(8,128)(2,1)} copy(bf16[320,2,4,6,1280]{4,2,3,1,0:T(4,128)(2,1)} %param.8) | data formatting | bytes 78643200 | tf_op args[0]
  27.7 0.0 copy-start
  27.7 47.5 %fusion.5 = bf16[320,8,48]{2,1,0:T(8,128)(2,1)S(1)} fusion(bf16[320,48,1280]{2,0,1:T(8,128)(2,1)} %bitcast.34, bf16[320,8,1280]{2,1,0:T(8,128)(2,1)} %param.9, pred[320,1280]{1,0:T(8,128)(4,1)S(1)} %iota_compare_fusion), kind=kOutput, calls=%fused_computation.10 | convolution fusion | flops 317972480 | bytes 46530560 | tf_op jit(solution)/shard_map/skj,slj->slk/dot_general | solution.py:72
  75.2 1.1 copy.21
  76.4 4.2 %all-to-all-start = ((bf16[320,8,48]{0,2,1:T(8,128)(2,1)}), bf16[320,8,48]{0,2,1:T(8,128)(2,1)S(1)}, u32[]{:S(2)}, u32[]{:S(2)}) async-start(bf16[320,8,48]{0,2,1:T(8,128)(2,1)} %copy.21), calls=%async_computation | async-start | bytes 589824 | tf_op jit(solution)/shard_map/all_to_all | solution.py:75
  80.6 0.0 copy-done
  80.6 2.6 %fusion.15 = (f32[1280,128]{0,1:T(8,128)S(1)}, f32[1280,128]{0,1:T(8,128)S(1)}) fusion(s32[1280]{0:T(1024)S(1)} %copy-done), kind=kLoop, calls=%fused_computation.18 | loop fusion | flops 1474560 | bytes 1315840 | tf_op jit(solution)/shard_map/cos | solution.py:39
  83.3 0.4 cosine_multiply_fusion
  83.7 3.3 %subtract_convert_fusion = (bf16[1280,9,128]{0,2,1:T(8,128)(2,1)}, bf16[1280,9,128]{0,2,1:T(8,128)(2,1)S(1)}) fusion(f32[1280,128]{0,1:T(8,128)S(1)} %get-tuple-element.27, f32[1280,9]{0,1:T(8,128)S(1)} %get-tuple-element.25, f32[1280,128]{0,1:T(8,128)S(1)} %get-tuple-element.26, f32[1280,9]{0,1:T(8,128)S(1)} %get-tuple-element.24), kind=kLoop, calls=%fused_computation.7 | loop fusion | flops 13271040 | bytes 7301120 | tf_op jit(solution)/shard_map/convert_element_type | solution.py:49
  87.0 0.0 all-to-all-done
  87.0 0.2 copy.30
  87.2 0.3 reshape.215
  87.5 2.8 %fusion.17 = f32[96,1152]{1,0:T(8,128)S(1)} fusion(bf16[1280,1152]{0,1:T(8,128)(2,1)} %bitcast.36, bf16[48,1280]{1,0:T(8,128)(2,1)S(1)} %get-tuple-element.28, bf16[48,1280]{1,0:T(8,128)(2,1)S(1)} %bitcast.41), kind=kOutput, calls=%fused_computation.25 | convolution fusion | flops 283607040 | bytes 3637248 | tf_op jit(solution)/shard_map/dot_general | solution.py:89
  90.4 0.0 copy-start.1
  90.4 1.0 fusion.21
  91.4 0.0 copy-start.2
  91.5 0.0 copy-start.3
  91.5 0.3 slice_subtract_fusion
  92.0 0.0 copy-done.1
  92.0 0.2 fusion.34
  92.2 0.1 multiply_reduce_fusion
  92.3 0.8 reverse.1
  93.1 0.1 slice.163
  93.2 0.1 multiply_reduce_fusion.1
  93.3 0.1 multiply_reduce_fusion.2
  93.4 0.8 reverse
  94.2 0.1 slice.162
  94.3 0.1 multiply_reduce_fusion.3
  94.4 0.2 concatenate.11
  94.6 0.2 reshape.220
  94.8 0.7 copy.23
  95.5 5.5 %all-to-all-start.1 = ((f32[4,2,4,1080]{3,2,1,0:T(4,128)}), f32[4,2,4,1080]{3,2,1,0:T(4,128)S(1)}, u32[]{:S(2)}, u32[]{:S(2)}) async-start(f32[4,2,4,1080]{3,2,1,0:T(4,128)} %copy.23), calls=%async_computation.1 | async-start | bytes 294912 | tf_op jit(solution)/shard_map/all_to_all | solution.py:109
  101.0 6.6 %all-to-all-done.1 = f32[4,2,4,1080]{3,2,1,0:T(4,128)S(1)} async-done(((f32[4,2,4,1080]{3,2,1,0:T(4,128)}), f32[4,2,4,1080]{3,2,1,0:T(4,128)S(1)}, u32[]{:S(2)}, u32[]{:S(2)}) %all-to-all-start.1) | async-done | bytes 138272 | tf_op jit(solution)/shard_map/all_to_all | solution.py:109
  107.7 0.7 broadcast_in_dim.30
  108.5 4.0 %all-to-all-start.2 = ((f32[8,2,4,1080]{3,2,1,0:T(4,128)}), f32[8,2,4,1080]{3,2,1,0:T(4,128)S(1)}, u32[]{:S(2)}, u32[]{:S(2)}) async-start(f32[8,2,4,1080]{3,2,1,0:T(4,128)} %broadcast_in_dim.30), calls=%async_computation.2 | async-start | bytes 589824 | tf_op jit(solution)/shard_map/all_to_all | solution.py:112
  112.4 0.0 copy-done.2
  112.4 0.1 broadcast_subtract_fusion
  112.5 0.0 copy-done.3
  112.5 0.1 compare_and_fusion.1
  112.6 6.6 %all-to-all-done.2 = f32[8,2,4,1080]{3,2,1,0:T(4,128)S(1)} async-done(((f32[8,2,4,1080]{3,2,1,0:T(4,128)}), f32[8,2,4,1080]{3,2,1,0:T(4,128)S(1)}, u32[]{:S(2)}, u32[]{:S(2)}) %all-to-all-start.2) | async-done | bytes 276512 | tf_op jit(solution)/shard_map/all_to_all | solution.py:112
  119.3 0.6 gather_fusion
  119.9 0.6 gather_fusion.1
  120.4 0.7 fusion.50
  (14 shorter events, 0.3 us)
Async XLA Ops:
  27.7 52.9 %copy-start = (s32[1280]{0:T(1024)S(1)}, s32[1280]{0:T(1024)}, u32[]{:S(2)}) copy-start(s32[1280]{0:T(1024)} %param.10) | copy-start | bytes 15364
  76.4 10.7 %all-to-all-start = ((bf16[320,8,48]{0,2,1:T(8,128)(2,1)}), bf16[320,8,48]{0,2,1:T(8,128)(2,1)S(1)}, u32[]{:S(2)}, u32[]{:S(2)}) async-start(bf16[320,8,48]{0,2,1:T(8,128)(2,1)} %copy.21), calls=%async_computation | async-start | bytes 589824 | tf_op jit(solution)/shard_map/all_to_all | solution.py:75
  90.4 1.6 %copy-start.1 = (f32[6]{0:T(128)S(1)}, f32[6]{0:T(128)}, u32[]{:S(2)}) copy-start(f32[6]{0:T(128)} %param.11) | copy-start | bytes 76
  91.4 21.0 %copy-start.2 = (f32[16]{0:T(128)S(1)}, f32[16]{0:T(128)}, u32[]{:S(2)}) copy-start(f32[16]{0:T(128)} %param.13) | copy-start | bytes 196
  91.5 21.1 %copy-start.3 = (s32[16]{0:T(128)S(1)}, s32[16]{0:T(128)}, u32[]{:S(2)}) copy-start(s32[16]{0:T(128)} %param.12) | copy-start | bytes 196
  95.5 12.2 %all-to-all-start.1 = ((f32[4,2,4,1080]{3,2,1,0:T(4,128)}), f32[4,2,4,1080]{3,2,1,0:T(4,128)S(1)}, u32[]{:S(2)}, u32[]{:S(2)}) async-start(f32[4,2,4,1080]{3,2,1,0:T(4,128)} %copy.23), calls=%async_computation.1 | async-start | bytes 294912 | tf_op jit(solution)/shard_map/all_to_all | solution.py:109
  108.5 10.8 %all-to-all-start.2 = ((f32[8,2,4,1080]{3,2,1,0:T(4,128)}), f32[8,2,4,1080]{3,2,1,0:T(4,128)S(1)}, u32[]{:S(2)}, u32[]{:S(2)}) async-start(f32[8,2,4,1080]{3,2,1,0:T(4,128)} %broadcast_in_dim.30), calls=%async_computation.2 | async-start | bytes 589824 | tf_op jit(solution)/shard_map/all_to_all | solution.py:112

commit v3 on v2

--- a/solution.py
+++ b/solution.py
@@ -68,10 +68,10 @@
         < (degree - owned_waves)[:, None, None]
     )
     table_rows = jnp.where(in_triangle, legendre, jnp.zeros_like(legendre))
-    coefficient = spectral.reshape(slot_count, channels, degree)
+    stored = jnp.transpose(spectral, (0, 1, 3, 2, 4))
     spec_grid = jnp.einsum(
-        "skj,slj->slk", coefficient, table_rows, preferred_element_type=jnp.float32
-    ).astype(jnp.bfloat16)
+        "spafj,srj->srpfa", stored, table_rows, preferred_element_type=jnp.float32
+    ).astype(jnp.bfloat16).reshape(slot_count, table_rows.shape[1], channels)
     by_latitude = lax.all_to_all(spec_grid, "wave", split_axis=1, concat_axis=0, tiled=True)
     total_slots = by_latitude.shape[0]
     lat_dev = by_latitude.shape[1]

time: 122 us -> 175 us (1.43)
  matrix products: 51.4 us -> 124 us
  local copies, waits for them, and re-layouts: 33.2 us -> 13 us
    dot_general x1, matrix products: 47.5 us -> 121 us  [local(): jnp.einsum('spafj,srj->srpfa', stored, table_rows, preferred_element_type...]
    unnamed x13 -> x12, local copies, waits for them, and re-layouts: 28.4 us -> 1.82 us
    convert_element_type x1, local copies, waits for them, and re-layouts: 1.15 us -> 6.84 us  [local(): spec_grid = jnp.einsum('spafj,srj->srpfa', stored, table_rows, preferred_...]
  transfers between devices with their start and end apart: 3 -> 3, of which waited for: 2 -> 2; matrix products, arithmetic and copies ran while one was open for 5% -> 4% of each run, Pallas kernels for 0% -> 0%
where the time goes in v3:
time: 175 us; the launch traced here: 174 us
  matrix products  124 us (71%)
  starting transfers between devices  13.8 us (8%)
  waiting for transfers between devices  13.3 us (8%)
  local copies, waits for them, and re-layouts  13 us (7%)
  other arithmetic  9.35 us (5%)
    dot_general x1, matrix products, local(): jnp.einsum('spafj,srj->srpfa', stored, table_rows, preferred_element_type...  121 us
    convert_element_type x1, local copies, waits for them, and re-layouts, local(): spec_grid = jnp.einsum('spafj,srj->srpfa', stored, table_rows, preferred_...  6.84 us
    all_to_all x1, waiting for transfers between devices, local(): lax.all_to_all(by_strip, 'lev', split_axis=0, concat_axis=0, tiled=True)  6.64 us
    all_to_all x1, waiting for transfers between devices, local(): lax.all_to_all(copies, ('wave', 'cpl'), split_axis=0, concat_axis=0, tile...  6.63 us
    all_to_all x1, starting transfers between devices, local(): lax.all_to_all(by_strip, 'lev', split_axis=0, concat_axis=0, tiled=True)  5.55 us
    all_to_all x1, starting transfers between devices, local(): lax.all_to_all(spec_grid, 'wave', split_axis=1, concat_axis=0, tiled=True)  4.24 us
    all_to_all x1, starting transfers between devices, local(): lax.all_to_all(copies, ('wave', 'cpl'), split_axis=0, concat_axis=0, tile...  3.98 us
  transfers between devices with their start and end apart: 3, of which 2 were waited for; matrix products, arithmetic and copies ran while one was open for 4% of the time, Pallas kernels for 0%

profile of v3, /device:TPU:0, one launch (start us, length us, event | category | flops | bytes accessed | tf_op | source)
XLA Modules:
  0.0 174.0 jit_solution(3528552680953584130)
XLA Ops:
  0.0 0.8 dynamic-slice_subtract_fusion
  0.8 0.3 iota_compare_fusion
  1.1 120.5 %convert_bitcast_fusion = bf16[320,8,2,4,6]{4,1,3,2,0:T(8,128)(2,1)} fusion(bf16[320,2,6,4,1280]{4,3,2,1,0:T(4,128)(2,1)} %bitcast.57, bf16[320,8,1280]{2,1,0:T(8,128)(2,1)} %param.9, pred[320,1280]{1,0:T(8,128)(4,1)S(1)} %iota_compare_fusion), kind=kOutput, calls=%fused_computation.9 | convolution fusion | flops 317972480 | bytes 46530560 | tf_op jit(solution)/shard_map/spafj,srj->srpfa/dot_general | solution.py:72
  121.6 0.0 copy-start
  121.6 6.8 %copy.21 = bf16[320,8,2,4,6]{0,1,4,3,2:T(8,128)(2,1)S(1)} copy(bf16[320,8,2,4,6]{4,1,3,2,0:T(8,128)(2,1)} %convert_bitcast_fusion) | data formatting | bytes 491520 | tf_op jit(solution)/shard_map/convert_element_type | solution.py:74
  128.5 0.8 copy.22
  129.2 4.2 %all-to-all-start = ((bf16[320,8,48]{0,2,1:T(8,128)(2,1)}), bf16[320,8,48]{0,2,1:T(8,128)(2,1)S(1)}, u32[]{:S(2)}, u32[]{:S(2)}) async-start(bf16[320,8,48]{0,2,1:T(8,128)(2,1)} %copy.22), calls=%async_computation | async-start | bytes 589824 | tf_op jit(solution)/shard_map/all_to_all | solution.py:75
  133.5 0.0 copy-done
  133.5 2.6 %fusion.15 = (f32[1280,128]{0,1:T(8,128)S(1)}, f32[1280,128]{0,1:T(8,128)S(1)}) fusion(s32[1280]{0:T(1024)S(1)} %copy-done), kind=kLoop, calls=%fused_computation.19 | loop fusion | flops 1474560 | bytes 1315840 | tf_op jit(solution)/shard_map/cos | solution.py:39
  136.1 0.4 cosine_multiply_fusion
  136.5 3.3 %subtract_convert_fusion = (bf16[1280,9,128]{0,2,1:T(8,128)(2,1)}, bf16[1280,9,128]{0,2,1:T(8,128)(2,1)S(1)}) fusion(f32[1280,128]{0,1:T(8,128)S(1)} %get-tuple-element.27, f32[1280,9]{0,1:T(8,128)S(1)} %get-tuple-element.25, f32[1280,128]{0,1:T(8,128)S(1)} %get-tuple-element.26, f32[1280,9]{0,1:T(8,128)S(1)} %get-tuple-element.24), kind=kLoop, calls=%fused_computation.8 | loop fusion | flops 13271040 | bytes 7301120 | tf_op jit(solution)/shard_map/convert_element_type | solution.py:49
  139.9 0.0 all-to-all-done
  139.9 0.2 copy.32
  140.1 0.3 reshape.215
  140.4 2.8 %fusion.17 = f32[96,1152]{1,0:T(8,128)S(1)} fusion(bf16[1280,1152]{0,1:T(8,128)(2,1)} %bitcast.45, bf16[48,1280]{1,0:T(8,128)(2,1)S(1)} %get-tuple-element.28, bf16[48,1280]{1,0:T(8,128)(2,1)S(1)} %bitcast.51), kind=kOutput, calls=%fused_computation.26 | convolution fusion | flops 283607040 | bytes 3637248 | tf_op jit(solution)/shard_map/dot_general | solution.py:89
  143.2 0.0 copy-start.1
  143.3 1.0 fusion.21
  144.3 0.0 copy-start.2
  144.3 0.0 copy-start.3
  144.4 0.3 slice_subtract_fusion
  144.8 0.0 copy-done.1
  144.8 0.2 fusion.34
  145.0 0.1 multiply_reduce_fusion
  145.1 0.8 reverse.1
  145.9 0.1 slice.163
  146.0 0.1 multiply_reduce_fusion.1
  146.1 0.1 multiply_reduce_fusion.2
  146.3 0.8 reverse
  147.1 0.1 slice.162
  147.2 0.1 multiply_reduce_fusion.3
  147.3 0.2 concatenate.11
  147.5 0.2 reshape.220
  147.6 0.7 copy.24
  148.3 5.5 %all-to-all-start.1 = ((f32[4,2,4,1080]{3,2,1,0:T(4,128)}), f32[4,2,4,1080]{3,2,1,0:T(4,128)S(1)}, u32[]{:S(2)}, u32[]{:S(2)}) async-start(f32[4,2,4,1080]{3,2,1,0:T(4,128)} %copy.24), calls=%async_computation.1 | async-start | bytes 294912 | tf_op jit(solution)/shard_map/all_to_all | solution.py:109
  153.9 6.6 %all-to-all-done.1 = f32[4,2,4,1080]{3,2,1,0:T(4,128)S(1)} async-done(((f32[4,2,4,1080]{3,2,1,0:T(4,128)}), f32[4,2,4,1080]{3,2,1,0:T(4,128)S(1)}, u32[]{:S(2)}, u32[]{:S(2)}) %all-to-all-start.1) | async-done | bytes 138272 | tf_op jit(solution)/shard_map/all_to_all | solution.py:109
  160.6 0.7 broadcast_in_dim.30
  161.3 4.0 %all-to-all-start.2 = ((f32[8,2,4,1080]{3,2,1,0:T(4,128)}), f32[8,2,4,1080]{3,2,1,0:T(4,128)S(1)}, u32[]{:S(2)}, u32[]{:S(2)}) async-start(f32[8,2,4,1080]{3,2,1,0:T(4,128)} %broadcast_in_dim.30), calls=%async_computation.2 | async-start | bytes 589824 | tf_op jit(solution)/shard_map/all_to_all | solution.py:112
  165.3 0.0 copy-done.2
  165.3 0.1 broadcast_subtract_fusion
  165.4 0.0 copy-done.3
  165.4 0.1 compare_and_fusion.1
  165.5 6.6 %all-to-all-done.2 = f32[8,2,4,1080]{3,2,1,0:T(4,128)S(1)} async-done(((f32[8,2,4,1080]{3,2,1,0:T(4,128)}), f32[8,2,4,1080]{3,2,1,0:T(4,128)S(1)}, u32[]{:S(2)}, u32[]{:S(2)}) %all-to-all-start.2) | async-done | bytes 276512 | tf_op jit(solution)/shard_map/all_to_all | solution.py:112
  172.1 0.6 gather_fusion
  172.7 0.6 gather_fusion.1
  173.3 0.7 fusion.50
  (14 shorter events, 0.3 us)
Async XLA Ops:
  121.6 11.9 %copy-start = (s32[1280]{0:T(1024)S(1)}, s32[1280]{0:T(1024)}, u32[]{:S(2)}) copy-start(s32[1280]{0:T(1024)} %param.10) | copy-start | bytes 15364
  129.2 10.7 %all-to-all-start = ((bf16[320,8,48]{0,2,1:T(8,128)(2,1)}), bf16[320,8,48]{0,2,1:T(8,128)(2,1)S(1)}, u32[]{:S(2)}, u32[]{:S(2)}) async-start(bf16[320,8,48]{0,2,1:T(8,128)(2,1)} %copy.22), calls=%async_computation | async-start | bytes 589824 | tf_op jit(solution)/shard_map/all_to_all | solution.py:75
  143.2 1.6 copy-start.1
  144.3 21.0 %copy-start.2 = (f32[16]{0:T(128)S(1)}, f32[16]{0:T(128)}, u32[]{:S(2)}) copy-start(f32[16]{0:T(128)} %param.13) | copy-start | bytes 196
  144.3 21.1 %copy-start.3 = (s32[16]{0:T(128)S(1)}, s32[16]{0:T(128)}, u32[]{:S(2)}) copy-start(s32[16]{0:T(128)} %param.12) | copy-start | bytes 196
  148.3 12.2 %all-to-all-start.1 = ((f32[4,2,4,1080]{3,2,1,0:T(4,128)}), f32[4,2,4,1080]{3,2,1,0:T(4,128)S(1)}, u32[]{:S(2)}, u32[]{:S(2)}) async-start(f32[4,2,4,1080]{3,2,1,0:T(4,128)} %copy.24), calls=%async_computation.1 | async-start | bytes 294912 | tf_op jit(solution)/shard_map/all_to_all | solution.py:109
  161.3 10.8 %all-to-all-start.2 = ((f32[8,2,4,1080]{3,2,1,0:T(4,128)}), f32[8,2,4,1080]{3,2,1,0:T(4,128)S(1)}, u32[]{:S(2)}, u32[]{:S(2)}) async-start(f32[8,2,4,1080]{3,2,1,0:T(4,128)} %broadcast_in_dim.30), calls=%async_computation.2 | async-start | bytes 589824 | tf_op jit(solution)/shard_map/all_to_all | solution.py:112

commit v4 on v3

--- a/solution.py
+++ b/solution.py
@@ -4,9 +4,12 @@
 import jax.numpy as jnp
 from jax import lax
 from jax.sharding import PartitionSpec as P
+from jax.experimental import pallas as pl
+from jax.experimental.pallas import tpu as pltpu
 
 NLON = 4320
 LANE = 128
+SLOT_BLOCK = 8
 
 
 def phase_angle(phase, lon_total):
@@ -51,6 +54,50 @@
     )
 
 
+def legendre_kernel(waves_ref, spec_ref, table_ref, out_ref):
+    block = spec_ref.shape[0]
+    degree = spec_ref.shape[-1]
+    first = pl.program_id(0) * block
+
+    def one_slot(s, carry):
+        limit = degree - waves_ref[first + s]
+        rows = table_ref[s]
+        column = lax.broadcasted_iota(jnp.int32, rows.shape, 1)
+        rows = jnp.where(column < limit, rows, jnp.zeros_like(rows))
+        coefficient = spec_ref[s].reshape(-1, degree)
+        out_ref[s] = lax.dot_general(
+            rows, coefficient, (((1,), (1,)), ((), ())), preferred_element_type=jnp.float32
+        ).astype(out_ref.dtype)
+        return carry
+
+    lax.fori_loop(0, block, one_slot, 0)
+
+
+def legendre_transform(stored, legendre, owned_waves):
+    slots, _, levels, fields, degree = stored.shape
+    lats = legendre.shape[1]
+    channels = 2 * levels * fields
+    block = SLOT_BLOCK
+    return pl.pallas_call(
+        legendre_kernel,
+        out_shape=jax.ShapeDtypeStruct((slots, lats, channels), jnp.bfloat16),
+        grid_spec=pltpu.PrefetchScalarGridSpec(
+            num_scalar_prefetch=1,
+            grid=(slots // block,),
+            in_specs=[
+                pl.BlockSpec((block, 2, levels, fields, degree), lambda i, w: (i, 0, 0, 0, 0)),
+                pl.BlockSpec((block, lats, degree), lambda i, w: (i, 0, 0)),
+            ],
+            out_specs=pl.BlockSpec((block, lats, channels), lambda i, w: (i, 0, 0)),
+        ),
+        cost_estimate=pl.CostEstimate(
+            flops=2 * slots * lats * channels * degree,
+            bytes_accessed=2 * slots * degree * (channels + lats),
+            transcendentals=0,
+        ),
+    )(owned_waves, stored, legendre)
+
+
 def local(spectral, legendre, wavenumber, level_weight, source_row, row_weight):
     slot_count = spectral.shape[0]
     fields = spectral.shape[2]
@@ -63,15 +110,13 @@
     wave_at = lax.axis_index("wave")
     cpl_at = lax.axis_index("cpl")
     owned_waves = lax.dynamic_slice_in_dim(wavenumber, wave_at * slot_count, slot_count)
-    in_triangle = (
-        lax.broadcasted_iota(jnp.int32, (slot_count, 1, degree), 2)
-        < (degree - owned_waves)[:, None, None]
+    stored = jnp.transpose(spectral, (0, 1, 3, 2, 4))
+    spec_grid = (
+        legendre_transform(stored, legendre, owned_waves)
+        .reshape(slot_count, legendre.shape[1], 2, levels, fields)
+        .transpose(0, 1, 2, 4, 3)
+        .reshape(slot_count, legendre.shape[1], channels)
     )
-    table_rows = jnp.where(in_triangle, legendre, jnp.zeros_like(legendre))
-    stored = jnp.transpose(spectral, (0, 1, 3, 2, 4))
-    spec_grid = jnp.einsum(
-        "spafj,srj->srpfa", stored, table_rows, preferred_element_type=jnp.float32
-    ).astype(jnp.bfloat16).reshape(slot_count, table_rows.shape[1], channels)
     by_latitude = lax.all_to_all(spec_grid, "wave", split_axis=1, concat_axis=0, tiled=True)
     total_slots = by_latitude.shape[0]
     lat_dev = by_latitude.shape[1]

time: 175 us -> 104 us (0.59)
  matrix products: 124 us -> 3.85 us
  Pallas kernels: 0 us -> 55 us
  local copies, waits for them, and re-layouts: 13 us -> 9.23 us
    dot_general x1 -> x0, matrix products: 121 us -> none  [local(): jnp.einsum('spafj,srj->srpfa', stored, table_rows, preferred_element_type...]
    pallas_call x0 -> x1, Pallas kernels: none -> 55 us  [legendre_transform(): pl.pallas_call(legendre_kernel, out_shape=jax.ShapeDtypeStruct((slots, la...]
    convert_element_type x1 -> x0, local copies, waits for them, and re-layouts: 6.84 us -> none  [local(): spec_grid = jnp.einsum('spafj,srj->srpfa', stored, table_rows, preferred_...]
    dot_general x1, matrix products: 2.84 us -> 1.01 us  [local(): r_all = jnp.dot(lhs_cos, cos_tab, preferred_element_type=jnp.float32)]
    dot_general x1, matrix products: 1.01 us -> 2.84 us  [local(): q_all = jnp.dot(lhs_sin, sin_tab, preferred_element_type=jnp.float32)]
  transfers between devices with their start and end apart: 3 -> 3, of which waited for: 2 -> 2; matrix products, arithmetic and copies ran while one was open for 4% -> 6% of each run, Pallas kernels for 0% -> 0%
where the time goes in v4:
time: 104 us
  Pallas kernels  55 us (53%)
  starting transfers between devices  13.8 us (13%)
  waiting for transfers between devices  13.3 us (13%)
  local copies, waits for them, and re-layouts  9.23 us (9%)
  other arithmetic  8.29 us (8%)
  matrix products  3.85 us (4%)
    pallas_call x1, Pallas kernels, legendre_transform(): pl.pallas_call(legendre_kernel, out_shape=jax.ShapeDtypeStruct((slots, la...  55 us
    all_to_all x1, waiting for transfers between devices, local(): lax.all_to_all(by_strip, 'lev', split_axis=0, concat_axis=0, tiled=True)  6.64 us
    all_to_all x1, waiting for transfers between devices, local(): lax.all_to_all(copies, ('wave', 'cpl'), split_axis=0, concat_axis=0, tile...  6.63 us
    all_to_all x1, starting transfers between devices, local(): lax.all_to_all(by_strip, 'lev', split_axis=0, concat_axis=0, tiled=True)  5.55 us
    all_to_all x1, starting transfers between devices, local(): lax.all_to_all(spec_grid, 'wave', split_axis=1, concat_axis=0, tiled=True)  4.24 us
    all_to_all x1, starting transfers between devices, local(): lax.all_to_all(copies, ('wave', 'cpl'), split_axis=0, concat_axis=0, tile...  3.98 us
    convert_element_type x1, other arithmetic, quarter_tables(): cos_tab.astype(jnp.bfloat16).reshape(slots, width)  3.36 us
    dot_general x1, matrix products, local(): q_all = jnp.dot(lhs_sin, sin_tab, preferred_element_type=jnp.float32)  2.84 us
  transfers between devices with their start and end apart: 3, of which 2 were waited for; matrix products, arithmetic and copies ran while one was open for 6% of the time, Pallas kernels for 0%

profile of v4, /device:TPU:0, one launch (start us, length us, event | category | flops | bytes accessed | tf_op | source)
XLA Modules:
  0.0 103.6 jit_solution(7027823705953700585)
XLA Ops:
  0.0 1.3 %dynamic_slice.10.waves_ref = s32[320]{0:T(512)} dynamic-slice(s32[1280]{0:T(1024)} %param.10, s32[]{:T(128)S(6)} %select_n.46), dynamic_slice_sizes={320} | dynamic-slice | bytes 2564 | tf_op jit(solution)/shard_map/dynamic_slice | solution.py:112
  1.3 0.0 copy-start
  1.3 55.0 %shard_map.64 = bf16[320,8,48]{2,1,0:T(8,128)(2,1)} custom-call(s32[320]{0:T(512)} %dynamic_slice.10.waves_ref, bf16[320,2,6,4,1280]{4,3,2,1,0:T(4,128)(2,1)} %bitcast.38, bf16[320,8,1280]{2,1,0:T(8,128)(2,1)} %table_ref.1), custom_call_target="tpu_custom_call" | custom-call | flops 314572800 | bytes 45875200 | tf_op jit(solution)/shard_map/pallas_call | solution.py:81
  56.4 1.7 %copy.19 = bf16[320,8,48]{0,1,2:T(8,128)(2,1)S(1)} copy(bf16[320,8,48]{2,1,0:T(8,128)(2,1)} %shard_map.64) | data formatting | bytes 491520 | tf_op jit(solution)/shard_map/pallas_call | solution.py:81
  58.1 0.8 copy.21
  58.8 4.2 %all-to-all-start = ((bf16[320,8,48]{0,2,1:T(8,128)(2,1)}), bf16[320,8,48]{0,2,1:T(8,128)(2,1)S(1)}, u32[]{:S(2)}, u32[]{:S(2)}) async-start(bf16[320,8,48]{0,2,1:T(8,128)(2,1)} %copy.21), calls=%async_computation | async-start | bytes 589824 | tf_op jit(solution)/shard_map/all_to_all | solution.py:120
  63.1 0.0 copy-done
  63.1 2.6 %fusion.5 = (f32[1280,128]{0,1:T(8,128)S(1)}, f32[1280,128]{0,1:T(8,128)S(1)}) fusion(s32[1280]{0:T(1024)S(1)} %copy-done), kind=kLoop, calls=%fused_computation.11 | loop fusion | flops 1474560 | bytes 1315840 | tf_op jit(solution)/shard_map/cos | solution.py:42
  65.7 0.4 cosine_multiply_fusion
  66.2 3.4 %subtract_convert_fusion = (bf16[1280,9,128]{0,2,1:T(8,128)(2,1)S(1)}, bf16[1280,9,128]{0,2,1:T(8,128)(2,1)}) fusion(f32[1280,128]{0,1:T(8,128)S(1)} %get-tuple-element.27, f32[1280,9]{0,1:T(8,128)S(1)} %get-tuple-element.25, f32[1280,128]{0,1:T(8,128)S(1)} %get-tuple-element.26, f32[1280,9]{0,1:T(8,128)S(1)} %get-tuple-element.24), kind=kLoop, calls=%fused_computation.3 | loop fusion | flops 13271040 | bytes 7301120 | tf_op jit(solution)/shard_map/convert_element_type | solution.py:52
  69.5 0.0 all-to-all-done
  69.5 0.2 copy.26
  69.7 0.3 reshape.201
  70.0 2.8 %fusion.11 = f32[96,1152]{1,0:T(8,128)S(1)} fusion(bf16[1280,1152]{0,1:T(8,128)(2,1)} %bitcast.40, bf16[48,1280]{1,0:T(8,128)(2,1)S(1)} %get-tuple-element.29, bf16[48,1280]{1,0:T(8,128)(2,1)S(1)} %bitcast.47), kind=kOutput, calls=%fused_computation.22 | convolution fusion | flops 283607040 | bytes 3637248 | tf_op jit(solution)/shard_map/dot_general | solution.py:135
  72.9 0.0 copy-start.1
  72.9 1.0 fusion.7
  73.9 0.0 copy-start.2
  73.9 0.0 copy-start.3
  74.0 0.3 slice_subtract_fusion
  74.5 0.0 copy-done.1
  74.5 0.2 fusion.24
  74.6 0.1 multiply_reduce_fusion.3
  74.8 0.1 multiply_reduce_fusion.2
  74.9 0.8 reverse
  75.7 0.1 slice.162
  75.8 0.1 multiply_reduce_fusion.1
  75.9 0.1 multiply_reduce_fusion
  76.0 0.8 reverse.1
  76.8 0.1 slice.163
  76.9 0.2 concatenate.11
  77.1 0.2 reshape.206
  77.3 0.7 copy.23
  78.0 5.6 %all-to-all-start.1 = ((f32[4,2,4,1080]{3,2,1,0:T(4,128)}), f32[4,2,4,1080]{3,2,1,0:T(4,128)S(1)}, u32[]{:S(2)}, u32[]{:S(2)}) async-start(f32[4,2,4,1080]{3,2,1,0:T(4,128)} %copy.23), calls=%async_computation.1 | async-start | bytes 294912 | tf_op jit(solution)/shard_map/all_to_all | solution.py:154
  83.5 6.6 %all-to-all-done.1 = f32[4,2,4,1080]{3,2,1,0:T(4,128)S(1)} async-done(((f32[4,2,4,1080]{3,2,1,0:T(4,128)}), f32[4,2,4,1080]{3,2,1,0:T(4,128)S(1)}, u32[]{:S(2)}, u32[]{:S(2)}) %all-to-all-start.1) | async-done | bytes 138272 | tf_op jit(solution)/shard_map/all_to_all | solution.py:154
  90.2 0.7 broadcast_in_dim.18
  91.0 4.0 %all-to-all-start.2 = ((f32[8,2,4,1080]{3,2,1,0:T(4,128)}), f32[8,2,4,1080]{3,2,1,0:T(4,128)S(1)}, u32[]{:S(2)}, u32[]{:S(2)}) async-start(f32[8,2,4,1080]{3,2,1,0:T(4,128)} %broadcast_in_dim.18), calls=%async_computation.2 | async-start | bytes 589824 | tf_op jit(solution)/shard_map/all_to_all | solution.py:157
  94.9 0.0 copy-done.2
  94.9 0.1 broadcast_subtract_fusion
  95.0 0.0 copy-done.3
  95.0 0.1 compare_and_fusion.1
  95.1 6.6 %all-to-all-done.2 = f32[8,2,4,1080]{3,2,1,0:T(4,128)S(1)} async-done(((f32[8,2,4,1080]{3,2,1,0:T(4,128)}), f32[8,2,4,1080]{3,2,1,0:T(4,128)S(1)}, u32[]{:S(2)}, u32[]{:S(2)}) %all-to-all-start.2) | async-done | bytes 276512 | tf_op jit(solution)/shard_map/all_to_all | solution.py:157
  101.8 0.6 gather_fusion.1
  102.3 0.6 gather_fusion
  102.9 0.7 fusion.40
  (15 shorter events, 0.3 us)
Async XLA Ops:
  1.3 61.7 %copy-start = (s32[1280]{0:T(1024)S(1)}, s32[1280]{0:T(1024)}, u32[]{:S(2)}) copy-start(s32[1280]{0:T(1024)} %param.10) | copy-start | bytes 15364
  58.8 10.7 %all-to-all-start = ((bf16[320,8,48]{0,2,1:T(8,128)(2,1)}), bf16[320,8,48]{0,2,1:T(8,128)(2,1)S(1)}, u32[]{:S(2)}, u32[]{:S(2)}) async-start(bf16[320,8,48]{0,2,1:T(8,128)(2,1)} %copy.21), calls=%async_computation | async-start | bytes 589824 | tf_op jit(solution)/shard_map/all_to_all | solution.py:120
  72.9 1.6 %copy-start.1 = (f32[6]{0:T(128)S(1)}, f32[6]{0:T(128)}, u32[]{:S(2)}) copy-start(f32[6]{0:T(128)} %param.11) | copy-start | bytes 76
  73.9 21.0 %copy-start.2 = (f32[16]{0:T(128)S(1)}, f32[16]{0:T(128)}, u32[]{:S(2)}) copy-start(f32[16]{0:T(128)} %param.13) | copy-start | bytes 196
  73.9 21.1 %copy-start.3 = (s32[16]{0:T(128)S(1)}, s32[16]{0:T(128)}, u32[]{:S(2)}) copy-start(s32[16]{0:T(128)} %param.12) | copy-start | bytes 196
  78.0 12.2 %all-to-all-start.1 = ((f32[4,2,4,1080]{3,2,1,0:T(4,128)}), f32[4,2,4,1080]{3,2,1,0:T(4,128)S(1)}, u32[]{:S(2)}, u32[]{:S(2)}) async-start(f32[4,2,4,1080]{3,2,1,0:T(4,128)} %copy.23), calls=%async_computation.1 | async-start | bytes 294912 | tf_op jit(solution)/shard_map/all_to_all | solution.py:154
  91.0 10.8 %all-to-all-start.2 = ((f32[8,2,4,1080]{3,2,1,0:T(4,128)}), f32[8,2,4,1080]{3,2,1,0:T(4,128)S(1)}, u32[]{:S(2)}, u32[]{:S(2)}) async-start(f32[8,2,4,1080]{3,2,1,0:T(4,128)} %broadcast_in_dim.18), calls=%async_computation.2 | async-start | bytes 589824 | tf_op jit(solution)/shard_map/all_to_all | solution.py:157

commit v5 on v4

--- a/solution.py
+++ b/solution.py
@@ -57,17 +57,25 @@
 def legendre_kernel(waves_ref, spec_ref, table_ref, out_ref):
     block = spec_ref.shape[0]
     degree = spec_ref.shape[-1]
+    chunk = 256 if degree % 256 == 0 else LANE
     first = pl.program_id(0) * block
 
     def one_slot(s, carry):
         limit = degree - waves_ref[first + s]
-        rows = table_ref[s]
-        column = lax.broadcasted_iota(jnp.int32, rows.shape, 1)
-        rows = jnp.where(column < limit, rows, jnp.zeros_like(rows))
-        coefficient = spec_ref[s].reshape(-1, degree)
-        out_ref[s] = lax.dot_general(
-            rows, coefficient, (((1,), (1,)), ((), ())), preferred_element_type=jnp.float32
-        ).astype(out_ref.dtype)
+        needed = (limit + chunk - 1) // chunk
+
+        def one_chunk(c, total):
+            start = pl.multiple_of(c * chunk, chunk)
+            rows = table_ref[s, :, pl.ds(start, chunk)]
+            column = start + lax.broadcasted_iota(jnp.int32, rows.shape, 1)
+            rows = jnp.where(column < limit, rows, jnp.zeros_like(rows))
+            coefficient = spec_ref[s, :, :, :, pl.ds(start, chunk)].reshape(-1, chunk)
+            return total + lax.dot_general(
+                rows, coefficient, (((1,), (1,)), ((), ())), preferred_element_type=jnp.float32
+            )
+
+        total = jnp.zeros(out_ref.shape[1:], jnp.float32)
+        out_ref[s] = lax.fori_loop(0, needed, one_chunk, total).astype(out_ref.dtype)
         return carry
 
     lax.fori_loop(0, block, one_slot, 0)

time: 104 us -> 184 us (1.77)
  Pallas kernels: 55 us -> 136 us
    pallas_call x1, Pallas kernels: 55 us -> 136 us  [legendre_transform(): pl.pallas_call(legendre_kernel, out_shape=jax.ShapeDtypeStruct((slots, la...]
  transfers between devices with their start and end apart: 3 -> 3, of which waited for: 2 -> 2; matrix products, arithmetic and copies ran while one was open for 6% -> 4% of each run, Pallas kernels for 0% -> 0%
where the time goes in v5:
time: 184 us; the launch traced here: 185 us
  Pallas kernels  136 us (74%)
  starting transfers between devices  13.7 us (7%)
  waiting for transfers between devices  13.3 us (7%)
  local copies, waits for them, and re-layouts  9.23 us (5%)
  other arithmetic  8.29 us (5%)
  matrix products  3.85 us (2%)
    pallas_call x1, Pallas kernels, legendre_transform(): pl.pallas_call(legendre_kernel, out_shape=jax.ShapeDtypeStruct((slots, la...  136 us
    all_to_all x1, waiting for transfers between devices, local(): lax.all_to_all(by_strip, 'lev', split_axis=0, concat_axis=0, tiled=True)  6.64 us
    all_to_all x1, waiting for transfers between devices, local(): lax.all_to_all(copies, ('wave', 'cpl'), split_axis=0, concat_axis=0, tile...  6.63 us
    all_to_all x1, starting transfers between devices, local(): lax.all_to_all(by_strip, 'lev', split_axis=0, concat_axis=0, tiled=True)  6.32 us
    all_to_all x1, starting transfers between devices, local(): lax.all_to_all(copies, ('wave', 'cpl'), split_axis=0, concat_axis=0, tile...  3.98 us
  transfers between devices with their start and end apart: 3, of which 2 were waited for; matrix products, arithmetic and copies ran while one was open for 4% of the time, Pallas kernels for 0%

profile of v5, /device:TPU:0, one launch (start us, length us, event | category | flops | bytes accessed | tf_op | source)
XLA Modules:
  0.0 185.0 jit_solution(4510283539047893300)
XLA Ops:
  0.0 1.3 dynamic_slice.10.waves_ref
  1.3 0.0 copy-start
  1.3 136.3 %shard_map.64 = bf16[320,8,48]{2,1,0:T(8,128)(2,1)} custom-call(s32[320]{0:T(512)} %dynamic_slice.10.waves_ref, bf16[320,2,6,4,1280]{4,3,2,1,0:T(4,128)(2,1)} %bitcast.38, bf16[320,8,1280]{2,1,0:T(8,128)(2,1)} %table_ref.1), custom_call_target="tpu_custom_call" | custom-call | flops 314572800 | bytes 45875200 | tf_op jit(solution)/shard_map/pallas_call | solution.py:89
  137.7 1.7 copy.19
  139.4 0.8 copy.21
  140.2 3.5 %all-to-all-start = ((bf16[320,8,48]{0,2,1:T(8,128)(2,1)}), bf16[320,8,48]{0,2,1:T(8,128)(2,1)S(1)}, u32[]{:S(2)}, u32[]{:S(2)}) async-start(bf16[320,8,48]{0,2,1:T(8,128)(2,1)} %copy.21), calls=%async_computation | async-start | bytes 589824 | tf_op jit(solution)/shard_map/all_to_all | solution.py:128
  143.6 0.0 copy-done
  143.7 2.6 %fusion.5 = (f32[1280,128]{0,1:T(8,128)S(1)}, f32[1280,128]{0,1:T(8,128)S(1)}) fusion(s32[1280]{0:T(1024)S(1)} %copy-done), kind=kLoop, calls=%fused_computation.11 | loop fusion | flops 1474560 | bytes 1315840 | tf_op jit(solution)/shard_map/cos | solution.py:42
  146.3 0.4 cosine_multiply_fusion
  146.7 3.4 %subtract_convert_fusion = (bf16[1280,9,128]{0,2,1:T(8,128)(2,1)S(1)}, bf16[1280,9,128]{0,2,1:T(8,128)(2,1)}) fusion(f32[1280,128]{0,1:T(8,128)S(1)} %get-tuple-element.27, f32[1280,9]{0,1:T(8,128)S(1)} %get-tuple-element.25, f32[1280,128]{0,1:T(8,128)S(1)} %get-tuple-element.26, f32[1280,9]{0,1:T(8,128)S(1)} %get-tuple-element.24), kind=kLoop, calls=%fused_computation.3 | loop fusion | flops 13271040 | bytes 7301120 | tf_op jit(solution)/shard_map/convert_element_type | solution.py:52
  150.1 0.0 all-to-all-done
  150.1 0.2 copy.26
  150.3 0.3 reshape.201
  150.6 2.8 %fusion.11 = f32[96,1152]{1,0:T(8,128)S(1)} fusion(bf16[1280,1152]{0,1:T(8,128)(2,1)} %bitcast.40, bf16[48,1280]{1,0:T(8,128)(2,1)S(1)} %get-tuple-element.29, bf16[48,1280]{1,0:T(8,128)(2,1)S(1)} %bitcast.47), kind=kOutput, calls=%fused_computation.22 | convolution fusion | flops 283607040 | bytes 3637248 | tf_op jit(solution)/shard_map/dot_general | solution.py:143
  153.4 0.0 copy-start.1
  153.5 1.0 fusion.7
  154.5 0.0 copy-start.2
  154.5 0.0 copy-start.3
  154.6 0.3 slice_subtract_fusion
  155.0 0.0 copy-done.1
  155.1 0.2 fusion.24
  155.2 0.1 multiply_reduce_fusion.3
  155.3 0.1 multiply_reduce_fusion.2
  155.4 0.8 reverse
  156.3 0.1 slice.162
  156.3 0.1 multiply_reduce_fusion.1
  156.5 0.1 multiply_reduce_fusion
  156.6 0.8 reverse.1
  157.4 0.1 slice.163
  157.5 0.2 concatenate.11
  157.7 0.2 reshape.206
  157.9 0.7 copy.23
  158.5 6.3 %all-to-all-start.1 = ((f32[4,2,4,1080]{3,2,1,0:T(4,128)}), f32[4,2,4,1080]{3,2,1,0:T(4,128)S(1)}, u32[]{:S(2)}, u32[]{:S(2)}) async-start(f32[4,2,4,1080]{3,2,1,0:T(4,128)} %copy.23), calls=%async_computation.1 | async-start | bytes 294912 | tf_op jit(solution)/shard_map/all_to_all | solution.py:162
  164.9 6.6 %all-to-all-done.1 = f32[4,2,4,1080]{3,2,1,0:T(4,128)S(1)} async-done(((f32[4,2,4,1080]{3,2,1,0:T(4,128)}), f32[4,2,4,1080]{3,2,1,0:T(4,128)S(1)}, u32[]{:S(2)}, u32[]{:S(2)}) %all-to-all-start.1) | async-done | bytes 138272 | tf_op jit(solution)/shard_map/all_to_all | solution.py:162
  171.5 0.7 broadcast_in_dim.18
  172.3 4.0 %all-to-all-start.2 = ((f32[8,2,4,1080]{3,2,1,0:T(4,128)}), f32[8,2,4,1080]{3,2,1,0:T(4,128)S(1)}, u32[]{:S(2)}, u32[]{:S(2)}) async-start(f32[8,2,4,1080]{3,2,1,0:T(4,128)} %broadcast_in_dim.18), calls=%async_computation.2 | async-start | bytes 589824 | tf_op jit(solution)/shard_map/all_to_all | solution.py:165
  176.3 0.0 copy-done.2
  176.3 0.1 broadcast_subtract_fusion
  176.4 0.0 copy-done.3
  176.4 0.1 compare_and_fusion.1
  176.4 6.6 %all-to-all-done.2 = f32[8,2,4,1080]{3,2,1,0:T(4,128)S(1)} async-done(((f32[8,2,4,1080]{3,2,1,0:T(4,128)}), f32[8,2,4,1080]{3,2,1,0:T(4,128)S(1)}, u32[]{:S(2)}, u32[]{:S(2)}) %all-to-all-start.2) | async-done | bytes 276512 | tf_op jit(solution)/shard_map/all_to_all | solution.py:165
  183.1 0.6 gather_fusion.1
  183.7 0.6 gather_fusion
  184.3 0.7 fusion.40
  (15 shorter events, 0.3 us)
Async XLA Ops:
  1.3 142.3 %copy-start = (s32[1280]{0:T(1024)S(1)}, s32[1280]{0:T(1024)}, u32[]{:S(2)}) copy-start(s32[1280]{0:T(1024)} %param.10) | copy-start | bytes 15364
  140.2 9.9 %all-to-all-start = ((bf16[320,8,48]{0,2,1:T(8,128)(2,1)}), bf16[320,8,48]{0,2,1:T(8,128)(2,1)S(1)}, u32[]{:S(2)}, u32[]{:S(2)}) async-start(bf16[320,8,48]{0,2,1:T(8,128)(2,1)} %copy.21), calls=%async_computation | async-start | bytes 589824 | tf_op jit(solution)/shard_map/all_to_all | solution.py:128
  153.4 1.6 copy-start.1
  154.5 21.8 %copy-start.2 = (f32[16]{0:T(128)S(1)}, f32[16]{0:T(128)}, u32[]{:S(2)}) copy-start(f32[16]{0:T(128)} %param.13) | copy-start | bytes 196
  154.5 21.8 %copy-start.3 = (s32[16]{0:T(128)S(1)}, s32[16]{0:T(128)}, u32[]{:S(2)}) copy-start(s32[16]{0:T(128)} %param.12) | copy-start | bytes 196
  158.5 13.0 %all-to-all-start.1 = ((f32[4,2,4,1080]{3,2,1,0:T(4,128)}), f32[4,2,4,1080]{3,2,1,0:T(4,128)S(1)}, u32[]{:S(2)}, u32[]{:S(2)}) async-start(f32[4,2,4,1080]{3,2,1,0:T(4,128)} %copy.23), calls=%async_computation.1 | async-start | bytes 294912 | tf_op jit(solution)/shard_map/all_to_all | solution.py:162
  172.3 10.8 %all-to-all-start.2 = ((f32[8,2,4,1080]{3,2,1,0:T(4,128)}), f32[8,2,4,1080]{3,2,1,0:T(4,128)S(1)}, u32[]{:S(2)}, u32[]{:S(2)}) async-start(f32[8,2,4,1080]{3,2,1,0:T(4,128)} %broadcast_in_dim.18), calls=%async_computation.2 | async-start | bytes 589824 | tf_op jit(solution)/shard_map/all_to_all | solution.py:165

commit v6 on v4

--- a/solution.py
+++ b/solution.py
@@ -9,7 +9,7 @@
 
 NLON = 4320
 LANE = 128
-SLOT_BLOCK = 8
+SLOT_BLOCK = 64
 
 
 def phase_angle(phase, lon_total):
@@ -70,14 +70,14 @@
         ).astype(out_ref.dtype)
         return carry
 
-    lax.fori_loop(0, block, one_slot, 0)
+    lax.fori_loop(0, block, one_slot, 0, unroll=True)
 
 
 def legendre_transform(stored, legendre, owned_waves):
     slots, _, levels, fields, degree = stored.shape
     lats = legendre.shape[1]
     channels = 2 * levels * fields
-    block = SLOT_BLOCK
+    block = max(b for b in range(1, SLOT_BLOCK + 1) if slots % b == 0)
     return pl.pallas_call(
         legendre_kernel,
         out_shape=jax.ShapeDtypeStruct((slots, lats, channels), jnp.bfloat16),

time: 104 us -> 68.2 us (0.66)
  Pallas kernels: 55 us -> 19 us
    pallas_call x1, Pallas kernels: 55 us -> 19 us  [legendre_transform(): pl.pallas_call(legendre_kernel, out_shape=jax.ShapeDtypeStruct((slots, la...]
  transfers between devices with their start and end apart: 3 -> 3, of which waited for: 2 -> 2; matrix products, arithmetic and copies ran while one was open for 6% -> 10% of each run, Pallas kernels for 0% -> 0%
where the time goes in v6:
time: 68.2 us; the launch traced here: 67.7 us
  Pallas kernels  19 us (28%)
  starting transfers between devices  13.8 us (20%)
  waiting for transfers between devices  13.3 us (20%)
  local copies, waits for them, and re-layouts  9.23 us (14%)
  other arithmetic  8.29 us (12%)
  matrix products  3.85 us (6%)
    pallas_call x1, Pallas kernels, legendre_transform(): pl.pallas_call(legendre_kernel, out_shape=jax.ShapeDtypeStruct((slots, la...  19 us
    all_to_all x1, waiting for transfers between devices, local(): lax.all_to_all(by_strip, 'lev', split_axis=0, concat_axis=0, tiled=True)  6.64 us
    all_to_all x1, waiting for transfers between devices, local(): lax.all_to_all(copies, ('wave', 'cpl'), split_axis=0, concat_axis=0, tile...  6.63 us
    all_to_all x1, starting transfers between devices, local(): lax.all_to_all(by_strip, 'lev', split_axis=0, concat_axis=0, tiled=True)  5.55 us
    all_to_all x1, starting transfers between devices, local(): lax.all_to_all(spec_grid, 'wave', split_axis=1, concat_axis=0, tiled=True)  4.24 us
    all_to_all x1, starting transfers between devices, local(): lax.all_to_all(copies, ('wave', 'cpl'), split_axis=0, concat_axis=0, tile...  3.98 us
    convert_element_type x1, other arithmetic, quarter_tables(): cos_tab.astype(jnp.bfloat16).reshape(slots, width)  3.36 us
    dot_general x1, matrix products, local(): q_all = jnp.dot(lhs_sin, sin_tab, preferred_element_type=jnp.float32)  2.84 us
  transfers between devices with their start and end apart: 3, of which 2 were waited for; matrix products, arithmetic and copies ran while one was open for 10% of the time, Pallas kernels for 0%

profile of v6, /device:TPU:0, one launch (start us, length us, event | category | flops | bytes accessed | tf_op | source)
XLA Modules:
  0.0 67.7 jit_solution(15287186190842461130)
XLA Ops:
  0.0 1.3 %dynamic_slice.10.waves_ref = s32[320]{0:T(512)} dynamic-slice(s32[1280]{0:T(1024)} %param.10, s32[]{:T(128)S(6)} %select_n.46), dynamic_slice_sizes={320} | dynamic-slice | bytes 2564 | tf_op jit(solution)/shard_map/dynamic_slice | solution.py:112
  1.3 0.0 copy-start
  1.3 19.0 %shard_map.64 = bf16[320,8,48]{2,1,0:T(8,128)(2,1)} custom-call(s32[320]{0:T(512)} %dynamic_slice.10.waves_ref, bf16[320,2,6,4,1280]{4,3,2,1,0:T(4,128)(2,1)} %bitcast.38, bf16[320,8,1280]{2,1,0:T(8,128)(2,1)} %table_ref.1), custom_call_target="tpu_custom_call" | custom-call | flops 314572800 | bytes 45875200 | tf_op jit(solution)/shard_map/pallas_call | solution.py:81
  20.4 1.7 %copy.19 = bf16[320,8,48]{0,1,2:T(8,128)(2,1)S(1)} copy(bf16[320,8,48]{2,1,0:T(8,128)(2,1)} %shard_map.64) | data formatting | bytes 491520 | tf_op jit(solution)/shard_map/pallas_call | solution.py:81
  22.1 0.8 %copy.21 = bf16[320,8,48]{0,2,1:T(8,128)(2,1)} copy(bf16[320,8,48]{0,1,2:T(8,128)(2,1)S(1)} %bitcast.43) | data formatting | bytes 491520 | tf_op jit(solution)/shard_map/reshape | solution.py:118
  22.9 4.2 %all-to-all-start = ((bf16[320,8,48]{0,2,1:T(8,128)(2,1)}), bf16[320,8,48]{0,2,1:T(8,128)(2,1)S(1)}, u32[]{:S(2)}, u32[]{:S(2)}) async-start(bf16[320,8,48]{0,2,1:T(8,128)(2,1)} %copy.21), calls=%async_computation | async-start | bytes 589824 | tf_op jit(solution)/shard_map/all_to_all | solution.py:120
  27.1 0.0 copy-done
  27.1 2.6 %fusion.5 = (f32[1280,128]{0,1:T(8,128)S(1)}, f32[1280,128]{0,1:T(8,128)S(1)}) fusion(s32[1280]{0:T(1024)S(1)} %copy-done), kind=kLoop, calls=%fused_computation.11 | loop fusion | flops 1474560 | bytes 1315840 | tf_op jit(solution)/shard_map/cos | solution.py:42
  29.8 0.4 cosine_multiply_fusion
  30.2 3.4 %subtract_convert_fusion = (bf16[1280,9,128]{0,2,1:T(8,128)(2,1)S(1)}, bf16[1280,9,128]{0,2,1:T(8,128)(2,1)}) fusion(f32[1280,128]{0,1:T(8,128)S(1)} %get-tuple-element.27, f32[1280,9]{0,1:T(8,128)S(1)} %get-tuple-element.25, f32[1280,128]{0,1:T(8,128)S(1)} %get-tuple-element.26, f32[1280,9]{0,1:T(8,128)S(1)} %get-tuple-element.24), kind=kLoop, calls=%fused_computation.3 | loop fusion | flops 13271040 | bytes 7301120 | tf_op jit(solution)/shard_map/convert_element_type | solution.py:52
  33.6 0.0 all-to-all-done
  33.6 0.2 copy.26
  33.7 0.3 reshape.201
  34.1 2.8 %fusion.11 = f32[96,1152]{1,0:T(8,128)S(1)} fusion(bf16[1280,1152]{0,1:T(8,128)(2,1)} %bitcast.40, bf16[48,1280]{1,0:T(8,128)(2,1)S(1)} %get-tuple-element.29, bf16[48,1280]{1,0:T(8,128)(2,1)S(1)} %bitcast.47), kind=kOutput, calls=%fused_computation.22 | convolution fusion | flops 283607040 | bytes 3637248 | tf_op jit(solution)/shard_map/dot_general | solution.py:135
  36.9 0.0 copy-start.1
  37.0 1.0 %fusion.7 = f32[96,1152]{1,0:T(8,128)S(1)} fusion(bf16[1280,1152]{0,1:T(8,128)(2,1)S(1)} %bitcast.39, bf16[48,1280]{1,0:T(8,128)(2,1)S(1)} %get-tuple-element.28, bf16[48,1280]{1,0:T(8,128)(2,1)S(1)} %bitcast.46), kind=kOutput, calls=%fused_computation.18 | convolution fusion | flops 283607040 | bytes 3637248 | tf_op jit(solution)/shard_map/dot_general | solution.py:134
  38.0 0.0 copy-start.2
  38.0 0.0 copy-start.3
  38.0 0.3 slice_subtract_fusion
  38.5 0.0 copy-done.1
  38.5 0.2 fusion.24
  38.7 0.1 multiply_reduce_fusion.3
  38.8 0.1 multiply_reduce_fusion.2
  38.9 0.8 %reverse = f32[2,4,1152]{2,1,0:T(4,128)S(1)} reverse(f32[2,4,1152]{2,1,0:T(4,128)S(1)} %bitcast.51), dimensions={2} | reverse | bytes 73728
  39.7 0.1 slice.162
  39.8 0.1 multiply_reduce_fusion.1
  39.9 0.1 multiply_reduce_fusion
  40.0 0.8 %reverse.1 = f32[2,4,1152]{2,1,0:T(4,128)S(1)} reverse(f32[2,4,1152]{2,1,0:T(4,128)S(1)} %bitcast.52), dimensions={2} | reverse | bytes 73728
  40.9 0.1 slice.163
  40.9 0.2 concatenate.11
  41.2 0.2 reshape.206
  41.3 0.7 %copy.23 = f32[4,2,4,1080]{3,2,1,0:T(4,128)} copy(f32[4,2,4,1080]{3,0,2,1:T(4,128)S(1)} %bitcast.48) | data formatting | bytes 276480 | tf_op jit(solution)/shard_map/transpose | solution.py:152
  42.0 5.5 %all-to-all-start.1 = ((f32[4,2,4,1080]{3,2,1,0:T(4,128)}), f32[4,2,4,1080]{3,2,1,0:T(4,128)S(1)}, u32[]{:S(2)}, u32[]{:S(2)}) async-start(f32[4,2,4,1080]{3,2,1,0:T(4,128)} %copy.23), calls=%async_computation.1 | async-start | bytes 294912 | tf_op jit(solution)/shard_map/all_to_all | solution.py:154
  47.6 6.6 %all-to-all-done.1 = f32[4,2,4,1080]{3,2,1,0:T(4,128)S(1)} async-done(((f32[4,2,4,1080]{3,2,1,0:T(4,128)}), f32[4,2,4,1080]{3,2,1,0:T(4,128)S(1)}, u32[]{:S(2)}, u32[]{:S(2)}) %all-to-all-start.1) | async-done | bytes 138272 | tf_op jit(solution)/shard_map/all_to_all | solution.py:154
  54.2 0.7 %broadcast_in_dim.18 = f32[8,2,4,1080]{3,2,1,0:T(4,128)} broadcast(f32[2,4,1080]{2,1,0:T(4,128)S(1)} %reduce_sum.49), dimensions={1,2,3} | broadcast | bytes 311040 | tf_op jit(solution)/shard_map/broadcast_in_dim | solution.py:156
  55.0 4.0 %all-to-all-start.2 = ((f32[8,2,4,1080]{3,2,1,0:T(4,128)}), f32[8,2,4,1080]{3,2,1,0:T(4,128)S(1)}, u32[]{:S(2)}, u32[]{:S(2)}) async-start(f32[8,2,4,1080]{3,2,1,0:T(4,128)} %broadcast_in_dim.18), calls=%async_computation.2 | async-start | bytes 589824 | tf_op jit(solution)/shard_map/all_to_all | solution.py:157
  59.0 0.0 copy-done.2
  59.0 0.1 broadcast_subtract_fusion
  59.1 0.0 copy-done.3
  59.1 0.1 compare_and_fusion.1
  59.1 6.6 %all-to-all-done.2 = f32[8,2,4,1080]{3,2,1,0:T(4,128)S(1)} async-done(((f32[8,2,4,1080]{3,2,1,0:T(4,128)}), f32[8,2,4,1080]{3,2,1,0:T(4,128)S(1)}, u32[]{:S(2)}, u32[]{:S(2)}) %all-to-all-start.2) | async-done | bytes 276512 | tf_op jit(solution)/shard_map/all_to_all | solution.py:157
  65.8 0.6 gather_fusion.1
  66.4 0.6 gather_fusion
  67.0 0.7 %fusion.40 = f32[2,4,1080]{2,1,0:T(4,128)} fusion(f32[2,4,1080]{2,1,0:T(4,128)S(1)} %gather_fusion.1, f32[2,4,1080]{2,1,0:T(4,128)S(1)} %gather_fusion, f32[2]{0:T(128)S(1)} %get-tuple-element.11, f32[2]{0:T(128)S(1)} %get-tuple-element.10, pred[2]{0:T(512)(128)(4,1)S(1)} %get-tuple-element.30, pred[2]{0:T(512)(128)(4,1)S(1)} %get-tuple-element.6), kind=kLoop, calls=%fused_computation.70 | loop fusion | flops 43200 | bytes 103700 | tf_op jit(solution)/shard_map/add | solution.py:34
  (15 shorter events, 0.3 us)
Async XLA Ops:
  1.3 25.8 %copy-start = (s32[1280]{0:T(1024)S(1)}, s32[1280]{0:T(1024)}, u32[]{:S(2)}) copy-start(s32[1280]{0:T(1024)} %param.10) | copy-start | bytes 15364
  22.9 10.7 %all-to-all-start = ((bf16[320,8,48]{0,2,1:T(8,128)(2,1)}), bf16[320,8,48]{0,2,1:T(8,128)(2,1)S(1)}, u32[]{:S(2)}, u32[]{:S(2)}) async-start(bf16[320,8,48]{0,2,1:T(8,128)(2,1)} %copy.21), calls=%async_computation | async-start | bytes 589824 | tf_op jit(solution)/shard_map/all_to_all | solution.py:120
  36.9 1.6 %copy-start.1 = (f32[6]{0:T(128)S(1)}, f32[6]{0:T(128)}, u32[]{:S(2)}) copy-start(f32[6]{0:T(128)} %param.11) | copy-start | bytes 76
  38.0 21.0 %copy-start.2 = (f32[16]{0:T(128)S(1)}, f32[16]{0:T(128)}, u32[]{:S(2)}) copy-start(f32[16]{0:T(128)} %param.13) | copy-start | bytes 196
  38.0 21.1 %copy-start.3 = (s32[16]{0:T(128)S(1)}, s32[16]{0:T(128)}, u32[]{:S(2)}) copy-start(s32[16]{0:T(128)} %param.12) | copy-start | bytes 196
  42.0 12.2 %all-to-all-start.1 = ((f32[4,2,4,1080]{3,2,1,0:T(4,128)}), f32[4,2,4,1080]{3,2,1,0:T(4,128)S(1)}, u32[]{:S(2)}, u32[]{:S(2)}) async-start(f32[4,2,4,1080]{3,2,1,0:T(4,128)} %copy.23), calls=%async_computation.1 | async-start | bytes 294912 | tf_op jit(solution)/shard_map/all_to_all | solution.py:154
  55.0 10.8 %all-to-all-start.2 = ((f32[8,2,4,1080]{3,2,1,0:T(4,128)}), f32[8,2,4,1080]{3,2,1,0:T(4,128)S(1)}, u32[]{:S(2)}, u32[]{:S(2)}) async-start(f32[8,2,4,1080]{3,2,1,0:T(4,128)} %broadcast_in_dim.18), calls=%async_computation.2 | async-start | bytes 589824 | tf_op jit(solution)/shard_map/all_to_all | solution.py:157

commit v7 on v6

--- a/solution.py
+++ b/solution.py
@@ -145,19 +145,21 @@
     strip3 = jnp.flip(flux_of((r1 - q1)[:, 1 : quarter + 1]), axis=-1)
     partial_value = jnp.concatenate([strip0, strip1, strip2, strip3], axis=-1)
 
-    own_first = (wave_at * cpl_count + cpl_at) * lat_dev
-    source = lax.dynamic_slice_in_dim(source_row, own_first, lat_dev)
-    weight_hi = lax.dynamic_slice_in_dim(row_weight, own_first, lat_dev)
+    lat_total = wave_count * cpl_count * lat_dev
+    row_at = lax.broadcasted_iota(jnp.int32, (source_row.shape[0], lat_total), 1)
+    weights = jnp.where(row_at == source_row[:, None], (1.0 - row_weight)[:, None], 0.0) + jnp.where(
+        row_at == source_row[:, None] + 1, row_weight[:, None], 0.0
+    )
+    own_rows = (cpl_at * wave_count + wave_at) * lat_dev
+    own_weights = lax.dynamic_slice_in_dim(weights, own_rows, lat_dev, 1)
+    own_weights = own_weights.reshape(wave_count, 1, cpl_count, lat_dev, lat_dev, 1, 1)
     strip_width = NLON // lev_count
-    by_strip = partial_value.reshape(lat_dev, fields, lev_count, strip_width).transpose(2, 0, 1, 3)
-    summed = jnp.sum(
-        lax.all_to_all(by_strip, "lev", split_axis=0, concat_axis=0, tiled=True), axis=0
-    )
-    copies = jnp.broadcast_to(summed[None], (wave_count * cpl_count,) + summed.shape)
-    gathered = lax.all_to_all(copies, ("wave", "cpl"), split_axis=0, concat_axis=0, tiled=True)
-    gathered = gathered.reshape((wave_count * cpl_count * lat_dev,) + summed.shape[1:])
-    gathered = latitude_order(gathered, wave_count, cpl_count, lat_dev)
-    return interpolate(gathered, source, weight_hi)
+    strips = partial_value.reshape(lat_dev, fields, lev_count, strip_width).transpose(2, 0, 1, 3)
+    strips = strips.reshape(1, lev_count, 1, 1, lat_dev, fields, strip_width)
+    shares = jnp.sum(own_weights * strips, axis=4)
+    shares = shares.reshape((wave_count * lev_count * cpl_count, lat_dev, fields, strip_width))
+    received = lax.all_to_all(shares, ("wave", "lev", "cpl"), split_axis=0, concat_axis=0, tiled=True)
+    return jnp.sum(received, axis=0)
 
 
 def solution(mesh):

time: 68.2 us -> 83.3 us (1.22)
  blocking collectives: 0 us -> 37.2 us
  waiting for transfers between devices: 13.3 us -> 0.01 us
  starting transfers between devices: 13.8 us -> 4.24 us
  other arithmetic: 8.29 us -> 11.5 us
  local copies, waits for them, and re-layouts: 9.23 us -> 6.86 us
    all_to_all x0 -> x1, blocking collectives: none -> 37.2 us  [local(): lax.all_to_all(shares, ('wave', 'lev', 'cpl'), split_axis=0, concat_axis=...]
    all_to_all x2 -> x0, waiting for transfers between devices: 13.3 us -> none  [the longest x1 6.64 us: local(): lax.all_to_all(by_strip, 'lev', split_axis=0, concat_axis=0, tiled=True)]
    all_to_all x2 -> x0, starting transfers between devices: 9.53 us -> none  [the longest x1 5.55 us: local(): lax.all_to_all(by_strip, 'lev', split_axis=0, concat_axis=0, tiled=True)]
    reduce_sum x1 -> x2, other arithmetic: 0.03 us -> 1.6 us  [the longest x1 0.81 us: local(): return jnp.sum(received, axis=0)]
    convert_element_type x1, other arithmetic: 3.36 us -> 4.63 us  [quarter_tables(): cos_tab.astype(jnp.bfloat16).reshape(slots, width)]
    cos x1, other arithmetic: 2.63 us -> 3.85 us  [quarter_tables(): base_cos = jnp.cos(base_angle)[:, None, :]]
    gather x2 -> x0, local copies, waits for them, and re-layouts: 1.16 us -> none  [the longest x1 0.58 us: interpolate(): upper = jnp.take(gathered, source + 1, axis=0)]
  transfers between devices with their start and end apart: 3 -> 1, of which waited for: 2 -> 0; matrix products, arithmetic and copies ran while one was open for 10% -> 11% of each run, Pallas kernels for 0% -> 0%
where the time goes in v7:
time: 83.3 us; the launch traced here: 82.9 us
  blocking collectives  37.2 us (45%)
  Pallas kernels  19.1 us (23%)
  other arithmetic  11.5 us (14%)
  local copies, waits for them, and re-layouts  6.86 us (8%)
  starting transfers between devices  4.24 us (5%)
  matrix products  3.85 us (5%)
    all_to_all x1, blocking collectives, local(): lax.all_to_all(shares, ('wave', 'lev', 'cpl'), split_axis=0, concat_axis=...  37.2 us
    pallas_call x1, Pallas kernels, legendre_transform(): pl.pallas_call(legendre_kernel, out_shape=jax.ShapeDtypeStruct((slots, la...  19.1 us
    convert_element_type x1, other arithmetic, quarter_tables(): cos_tab.astype(jnp.bfloat16).reshape(slots, width)  4.63 us
    all_to_all x1, starting transfers between devices, local(): lax.all_to_all(spec_grid, 'wave', split_axis=1, concat_axis=0, tiled=True)  4.24 us
    cos x1, other arithmetic, quarter_tables(): base_cos = jnp.cos(base_angle)[:, None, :]  3.85 us
    dot_general x1, matrix products, local(): q_all = jnp.dot(lhs_sin, sin_tab, preferred_element_type=jnp.float32)  2.84 us
    unnamed x12, local copies, waits for them, and re-layouts  1.95 us
    pallas_call x1, local copies, waits for them, and re-layouts, legendre_transform(): pl.pallas_call(legendre_kernel, out_shape=jax.ShapeDtypeStruct((slots, la...  1.69 us
  transfers between devices with their start and end apart: 1, of which 0 were waited for; matrix products, arithmetic and copies ran while one was open for 11% of the time, Pallas kernels for 0%

profile of v7, /device:TPU:0, one launch (start us, length us, event | category | flops | bytes accessed | tf_op | source)
XLA Modules:
  0.0 82.9 jit_solution(6980420965344420870)
XLA Ops:
  0.0 1.3 %dynamic_slice.7.waves_ref = s32[320]{0:T(512)} dynamic-slice(s32[1280]{0:T(1024)} %param.8, s32[]{:T(128)S(6)} %select_n.47), dynamic_slice_sizes={320} | dynamic-slice | bytes 2564 | tf_op jit(solution)/shard_map/dynamic_slice | solution.py:112
  1.3 0.0 copy-start
  1.3 19.1 %shard_map.64 = bf16[320,8,48]{2,1,0:T(8,128)(2,1)} custom-call(s32[320]{0:T(512)} %dynamic_slice.7.waves_ref, bf16[320,2,6,4,1280]{4,3,2,1,0:T(4,128)(2,1)} %bitcast.36, bf16[320,8,1280]{2,1,0:T(8,128)(2,1)} %table_ref.1), custom_call_target="tpu_custom_call" | custom-call | flops 314572800 | bytes 45875200 | tf_op jit(solution)/shard_map/pallas_call | solution.py:81
  20.4 0.0 copy-start.2
  20.4 0.0 copy-start.3
  20.4 1.7 %copy.27 = bf16[320,8,48]{0,1,2:T(8,128)(2,1)S(1)} copy(bf16[320,8,48]{2,1,0:T(8,128)(2,1)} %shard_map.64) | data formatting | bytes 491520 | tf_op jit(solution)/shard_map/pallas_call | solution.py:81
  22.2 0.7 copy.29
  22.9 4.2 %all-to-all-start = ((bf16[320,8,48]{0,2,1:T(8,128)(2,1)}), bf16[320,8,48]{0,2,1:T(8,128)(2,1)S(1)}, u32[]{:S(2)}, u32[]{:S(2)}) async-start(bf16[320,8,48]{0,2,1:T(8,128)(2,1)} %copy.29), calls=%async_computation | async-start | bytes 589824 | tf_op jit(solution)/shard_map/all_to_all | solution.py:120
  27.1 0.0 copy-done
  27.1 3.8 %fusion.5 = (f32[1280,128]{0,1:T(8,128)}, f32[1280,128]{0,1:T(8,128)}) fusion(s32[1280]{0:T(1024)S(1)} %copy-done), kind=kLoop, calls=%fused_computation.10 | loop fusion | flops 1474560 | bytes 1315840 | tf_op jit(solution)/shard_map/cos | solution.py:42
  31.0 0.0 copy-done.2
  31.0 0.0 copy-done.3
  31.1 0.1 copy.33
  31.1 0.4 cosine_multiply_fusion
  31.6 4.6 %subtract_convert_fusion = (bf16[1280,9,128]{0,2,1:T(8,128)(2,1)S(1)}, bf16[1280,9,128]{0,2,1:T(8,128)(2,1)}) fusion(f32[1280,128]{0,1:T(8,128)} %get-tuple-element.20, f32[1280,9]{0,1:T(8,128)S(1)} %get-tuple-element.18, f32[1280,128]{0,1:T(8,128)} %get-tuple-element.19, f32[1280,9]{0,1:T(8,128)S(1)} %get-tuple-element.17), kind=kLoop, calls=%fused_computation.1 | loop fusion | flops 13271040 | bytes 7301120 | tf_op jit(solution)/shard_map/convert_element_type | solution.py:52
  36.2 0.0 all-to-all-done
  36.2 0.2 copy.36
  36.4 0.3 reshape.201
  36.7 2.8 %fusion.11 = f32[96,1152]{1,0:T(8,128)S(1)} fusion(bf16[1280,1152]{0,1:T(8,128)(2,1)} %bitcast.38, bf16[48,1280]{1,0:T(8,128)(2,1)S(1)} %get-tuple-element.22, bf16[48,1280]{1,0:T(8,128)(2,1)S(1)} %bitcast.45), kind=kOutput, calls=%fused_computation.21 | convolution fusion | flops 283607040 | bytes 3637248 | tf_op jit(solution)/shard_map/dot_general | solution.py:135
  39.6 1.0 %fusion.7 = f32[96,1152]{1,0:T(8,128)S(1)} fusion(bf16[1280,1152]{0,1:T(8,128)(2,1)S(1)} %bitcast.37, bf16[48,1280]{1,0:T(8,128)(2,1)S(1)} %get-tuple-element.21, bf16[48,1280]{1,0:T(8,128)(2,1)S(1)} %bitcast.44), kind=kOutput, calls=%fused_computation.17 | convolution fusion | flops 283607040 | bytes 3637248 | tf_op jit(solution)/shard_map/dot_general | solution.py:134
  40.6 0.0 copy-start.1
  40.6 0.3 slice_subtract_fusion
  41.1 0.1 copy-done.1
  41.3 0.2 fusion.24
  41.4 0.1 multiply_reduce_fusion.4
  41.5 0.1 multiply_reduce_fusion.3
  41.6 0.8 reverse
  42.5 0.1 slice.158
  42.5 0.1 multiply_reduce_fusion.2
  42.7 0.1 multiply_reduce_fusion.1
  42.8 0.8 reverse.1
  43.6 0.1 slice.159
  43.7 0.2 concatenate.11
  43.9 0.2 reshape.206
  44.1 0.8 multiply_reduce_fusion
  44.9 37.2 %all_to_all.20 = f32[32,2,4,1080]{3,2,1,0:T(4,128)S(1)} all-to-all(f32[32,2,4,1080]{3,2,1,0:T(4,128)S(1)} %bitcast.39), channel_id=1, replica_groups=mesh['wave'=4,'lev'=4,'cpl'=2] {'wave','lev','cpl'}, dimensions={0} | all-to-all | bytes 2211840 | tf_op jit(solution)/shard_map/all_to_all | solution.py:161
  82.1 0.8 reduce_sum.59
  (16 shorter events, 0.3 us)
Async XLA Ops:
  1.3 25.8 %copy-start = (s32[1280]{0:T(1024)S(1)}, s32[1280]{0:T(1024)}, u32[]{:S(2)}) copy-start(s32[1280]{0:T(1024)} %param.8) | copy-start | bytes 15364
  20.4 10.6 %copy-start.2 = (f32[16]{0:T(128)S(1)}, f32[16]{0:T(128)}, u32[]{:S(2)}) copy-start(f32[16]{0:T(128)} %param.11) | copy-start | bytes 196
  20.4 10.6 %copy-start.3 = (s32[16]{0:T(128)S(1)}, s32[16]{0:T(128)}, u32[]{:S(2)}) copy-start(s32[16]{0:T(128)} %param.10) | copy-start | bytes 196
  22.9 13.3 %all-to-all-start = ((bf16[320,8,48]{0,2,1:T(8,128)(2,1)}), bf16[320,8,48]{0,2,1:T(8,128)(2,1)S(1)}, u32[]{:S(2)}, u32[]{:S(2)}) async-start(bf16[320,8,48]{0,2,1:T(8,128)(2,1)} %copy.29), calls=%async_computation | async-start | bytes 589824 | tf_op jit(solution)/shard_map/all_to_all | solution.py:120
  40.6 0.7 copy-start.1

commit v8 on v6

--- a/solution.py
+++ b/solution.py
@@ -149,13 +149,23 @@
     source = lax.dynamic_slice_in_dim(source_row, own_first, lat_dev)
     weight_hi = lax.dynamic_slice_in_dim(row_weight, own_first, lat_dev)
     strip_width = NLON // lev_count
+    lev_at = lax.axis_index("lev")
     by_strip = partial_value.reshape(lat_dev, fields, lev_count, strip_width).transpose(2, 0, 1, 3)
-    summed = jnp.sum(
-        lax.all_to_all(by_strip, "lev", split_axis=0, concat_axis=0, tiled=True), axis=0
-    )
-    copies = jnp.broadcast_to(summed[None], (wave_count * cpl_count,) + summed.shape)
-    gathered = lax.all_to_all(copies, ("wave", "cpl"), split_axis=0, concat_axis=0, tiled=True)
-    gathered = gathered.reshape((wave_count * cpl_count * lat_dev,) + summed.shape[1:])
+    summed = lax.dynamic_index_in_dim(by_strip, lev_at, 0, keepdims=False)
+    for k in range(1, lev_count):
+        outgoing = lax.dynamic_index_in_dim(by_strip, (lev_at + k) % lev_count, 0, keepdims=False)
+        pairs = [(j, (j + k) % lev_count) for j in range(lev_count)]
+        summed = summed + lax.ppermute(outgoing, "lev", pairs)
+    group = wave_count * cpl_count
+    own = wave_at * cpl_count + cpl_at
+    arrived = [summed]
+    for k in range(1, group):
+        pairs = [(j, (j + k) % group) for j in range(group)]
+        arrived.append(lax.ppermute(summed, ("wave", "cpl"), pairs))
+    stacked = jnp.stack(arrived)
+    member = (own - jnp.arange(group, dtype=jnp.int32)) % group
+    gathered = jnp.take(stacked, member, axis=0)
+    gathered = gathered.reshape((group * lat_dev,) + summed.shape[1:])
     gathered = latitude_order(gathered, wave_count, cpl_count, lat_dev)
     return interpolate(gathered, source, weight_hi)
 

time: 68.2 us -> 69.6 us (1.021)
  waiting for transfers between devices: 13.3 us -> 8.39 us
  starting transfers between devices: 13.8 us -> 17.3 us
  other arithmetic: 8.29 us -> 11.4 us
    all_to_all x2 -> x0, waiting for transfers between devices: 13.3 us -> none  [the longest x1 6.64 us: local(): lax.all_to_all(by_strip, 'lev', split_axis=0, concat_axis=0, tiled=True)]
    ppermute x0 -> x10, starting transfers between devices: none -> 13.1 us  [the longest x7 7.64 us: local(): arrived.append(lax.ppermute(summed, ('wave', 'cpl'), pairs))]
    all_to_all x2 -> x0, starting transfers between devices: 9.53 us -> none  [the longest x1 5.55 us: local(): lax.all_to_all(by_strip, 'lev', split_axis=0, concat_axis=0, tiled=True)]
    ppermute x0 -> x10, waiting for transfers between devices: none -> 8.39 us  [the longest x3 4.68 us: local(): summed = summed + lax.ppermute(outgoing, 'lev', pairs)]
    convert_element_type x1, other arithmetic: 3.36 us -> 4.58 us  [quarter_tables(): cos_tab.astype(jnp.bfloat16).reshape(slots, width)]
    cos x1, other arithmetic: 2.63 us -> 3.82 us  [quarter_tables(): base_cos = jnp.cos(base_angle)[:, None, :]]
    broadcast_in_dim x1 -> x0, local copies, waits for them, and re-layouts: 0.75 us -> none  [local(): jnp.broadcast_to(summed[None], (wave_count * cpl_count,) + summed.shape)]
    gather x0 -> x1, local copies, waits for them, and re-layouts: none -> 0.73 us  [local(): gathered = jnp.take(stacked, member, axis=0)]
  transfers between devices with their start and end apart: 3 -> 11, of which waited for: 2 -> 6; matrix products, arithmetic and copies ran while one was open for 10% -> 14% of each run, Pallas kernels for 0% -> 0%
where the time goes in v8:
time: 69.6 us; the launch traced here: 69.2 us
  Pallas kernels  19.1 us (27%)
  starting transfers between devices  17.3 us (25%)
  other arithmetic  11.4 us (16%)
  local copies, waits for them, and re-layouts  8.76 us (13%)
  waiting for transfers between devices  8.39 us (12%)
  matrix products  3.85 us (6%)
    pallas_call x1, Pallas kernels, legendre_transform(): pl.pallas_call(legendre_kernel, out_shape=jax.ShapeDtypeStruct((slots, la...  19.1 us
    ppermute x7, starting transfers between devices, local(): arrived.append(lax.ppermute(summed, ('wave', 'cpl'), pairs))  7.64 us
    ppermute x3, starting transfers between devices, local(): summed = summed + lax.ppermute(outgoing, 'lev', pairs)  5.47 us
    ppermute x3, waiting for transfers between devices, local(): summed = summed + lax.ppermute(outgoing, 'lev', pairs)  4.68 us
    convert_element_type x1, other arithmetic, quarter_tables(): cos_tab.astype(jnp.bfloat16).reshape(slots, width)  4.58 us
    all_to_all x1, starting transfers between devices, local(): lax.all_to_all(spec_grid, 'wave', split_axis=1, concat_axis=0, tiled=True)  4.24 us
    cos x1, other arithmetic, quarter_tables(): base_cos = jnp.cos(base_angle)[:, None, :]  3.82 us
    ppermute x7, waiting for transfers between devices, local(): arrived.append(lax.ppermute(summed, ('wave', 'cpl'), pairs))  3.71 us
  transfers between devices with their start and end apart: 11, of which 6 were waited for; matrix products, arithmetic and copies ran while one was open for 14% of the time, Pallas kernels for 0%

profile of v8, /device:TPU:0, one launch (start us, length us, event | category | flops | bytes accessed | tf_op | source)
XLA Modules:
  0.0 69.2 jit_solution(16224736760560202031)
XLA Ops:
  0.0 1.3 %dynamic_slice.15.waves_ref = s32[320]{0:T(512)} dynamic-slice(s32[1280]{0:T(1024)} %param.10, s32[]{:T(128)S(6)} %select_n.115), dynamic_slice_sizes={320} | dynamic-slice | bytes 2564 | tf_op jit(solution)/shard_map/dynamic_slice | solution.py:112
  1.4 19.1 %shard_map.64 = bf16[320,8,48]{2,1,0:T(8,128)(2,1)} custom-call(s32[320]{0:T(512)} %dynamic_slice.15.waves_ref, bf16[320,2,6,4,1280]{4,3,2,1,0:T(4,128)(2,1)} %bitcast.71, bf16[320,8,1280]{2,1,0:T(8,128)(2,1)} %table_ref.1), custom_call_target="tpu_custom_call" | custom-call | flops 314572800 | bytes 45875200 | tf_op jit(solution)/shard_map/pallas_call | solution.py:81
  20.4 1.7 %copy.14 = bf16[320,8,48]{0,1,2:T(8,128)(2,1)S(1)} copy(bf16[320,8,48]{2,1,0:T(8,128)(2,1)} %shard_map.64) | data formatting | bytes 491520 | tf_op jit(solution)/shard_map/pallas_call | solution.py:81
  22.1 0.8 %copy.16 = bf16[320,8,48]{0,2,1:T(8,128)(2,1)} copy(bf16[320,8,48]{0,1,2:T(8,128)(2,1)S(1)} %bitcast.75) | data formatting | bytes 491520 | tf_op jit(solution)/shard_map/reshape | solution.py:118
  22.9 4.2 %all-to-all-start = ((bf16[320,8,48]{0,2,1:T(8,128)(2,1)}), bf16[320,8,48]{0,2,1:T(8,128)(2,1)S(1)}, u32[]{:S(2)}, u32[]{:S(2)}) async-start(bf16[320,8,48]{0,2,1:T(8,128)(2,1)} %copy.16), calls=%async_computation | async-start | bytes 589824 | tf_op jit(solution)/shard_map/all_to_all | solution.py:120
  27.1 3.8 %fusion.5 = (f32[1280,128]{0,1:T(8,128)}, f32[1280,128]{0,1:T(8,128)}) fusion(s32[1280]{0:T(1024)S(1)} %copy-done), kind=kLoop, calls=%fused_computation.12 | loop fusion | flops 1474560 | bytes 1315840 | tf_op jit(solution)/shard_map/cos | solution.py:42
  31.0 0.4 cosine_multiply_fusion
  31.5 0.7 compare_and_fusion.1
  32.1 4.6 %subtract_convert_fusion = (bf16[1280,9,128]{0,2,1:T(8,128)(2,1)S(1)}, bf16[1280,9,128]{0,2,1:T(8,128)(2,1)}) fusion(f32[1280,128]{0,1:T(8,128)} %get-tuple-element.33, f32[1280,9]{0,1:T(8,128)S(1)} %get-tuple-element.31, f32[1280,128]{0,1:T(8,128)} %get-tuple-element.32, f32[1280,9]{0,1:T(8,128)S(1)} %get-tuple-element.30), kind=kLoop, calls=%fused_computation.4 | loop fusion | flops 13271040 | bytes 7301120 | tf_op jit(solution)/shard_map/convert_element_type | solution.py:52
  36.7 0.2 copy.29
  36.9 0.3 reshape.265
  37.2 2.8 %fusion.11 = f32[96,1152]{1,0:T(8,128)S(1)} fusion(bf16[1280,1152]{0,1:T(8,128)(2,1)} %bitcast.73, bf16[48,1280]{1,0:T(8,128)(2,1)S(1)} %get-tuple-element.35, bf16[48,1280]{1,0:T(8,128)(2,1)S(1)} %bitcast.80), kind=kOutput, calls=%fused_computation.24 | convolution fusion | flops 283607040 | bytes 3637248 | tf_op jit(solution)/shard_map/dot_general | solution.py:135
  40.1 1.0 %fusion.7 = f32[96,1152]{1,0:T(8,128)S(1)} fusion(bf16[1280,1152]{0,1:T(8,128)(2,1)S(1)} %bitcast.72, bf16[48,1280]{1,0:T(8,128)(2,1)S(1)} %get-tuple-element.34, bf16[48,1280]{1,0:T(8,128)(2,1)S(1)} %bitcast.79), kind=kOutput, calls=%fused_computation.20 | convolution fusion | flops 283607040 | bytes 3637248 | tf_op jit(solution)/shard_map/dot_general | solution.py:134
  41.2 0.3 slice_subtract_fusion
  41.7 0.2 fusion.24
  41.8 0.1 multiply_reduce_fusion.3
  42.0 0.1 multiply_reduce_fusion.2
  42.1 0.8 %reverse = f32[2,4,1152]{2,1,0:T(4,128)S(1)} reverse(f32[2,4,1152]{2,1,0:T(4,128)S(1)} %bitcast.83), dimensions={2} | reverse | bytes 73728
  42.9 0.1 slice.164
  43.0 0.1 multiply_reduce_fusion.1
  43.1 0.1 multiply_reduce_fusion
  43.2 0.8 %reverse.1 = f32[2,4,1152]{2,1,0:T(4,128)S(1)} reverse(f32[2,4,1152]{2,1,0:T(4,128)S(1)} %bitcast.84), dimensions={2} | reverse | bytes 73728
  44.0 0.1 slice.165
  44.1 0.2 concatenate.11
  44.3 0.2 reshape.270
  44.5 0.1 constant_dynamic-slice_fusion.3
  44.6 4.4 %collective-permute-start.2 = (f32[2,4,1080]{2,1,0:T(4,128)S(1)}, f32[2,4,1080]{2,1,0:T(4,128)S(1)}, u32[]{:S(2)}, u32[]{:S(2)}) collective-permute-start(f32[2,4,1080]{2,1,0:T(4,128)S(1)} %bitcast.85), channel_id=1, source_target_pairs={{0,6},{2,0},{4,2},{6,4},{1,7},{3,1},{5,3},{7,5},{8,14},{10,8},{12,... | collective-permute-start | bytes 103688 | tf_op jit(solution)/shard_map/ppermute | solution.py:158
  49.0 0.1 collective-permute-start.1
  49.1 1.0 %collective-permute-start = (f32[2,4,1080]{2,1,0:T(4,128)S(1)}, f32[2,4,1080]{2,1,0:T(4,128)S(1)}, u32[]{:S(2)}, u32[]{:S(2)}) collective-permute-start(f32[2,4,1080]{2,1,0:T(4,128)S(1)} %bitcast.87), channel_id=1, source_target_pairs={{0,2},{2,4},{4,6},{6,0},{1,3},{3,5},{5,7},{7,1},{8,10},{10,12},{12... | collective-permute-start | bytes 103688 | tf_op jit(solution)/shard_map/ppermute | solution.py:158
  50.2 0.1 broadcast_subtract_fusion
  50.2 0.6 collective-permute-done.2
  50.8 3.5 %collective-permute-done.1 = f32[2,4,1080]{2,1,0:T(4,128)S(1)} collective-permute-done((f32[2,4,1080]{2,1,0:T(4,128)S(1)}, f32[2,4,1080]{2,1,0:T(4,128)S(1)}, u32[]{:S(2)}, u32[]{:S(2)}) %collective-permute-start.1) | collective-permute-done | bytes 34592 | tf_op jit(solution)/shard_map/ppermute | solution.py:158
  54.3 0.6 collective-permute-done
  54.9 1.6 %collective-permute-start.3 = (f32[2,4,1080]{2,1,0:T(4,128)S(1)}, f32[2,4,1080]{2,1,0:T(4,128)S(1)}, u32[]{:S(2)}, u32[]{:S(2)}) collective-permute-start(f32[2,4,1080]{2,1,0:T(4,128)S(1)} %get-tuple-element.13), channel_id=1, source_target_pairs={{0,1},{1,8},{8,9},{9,16},{16,17},{17,24},{24,25},{25,0},{2,3},{3,1... | collective-permute-start | bytes 103688 | tf_op jit(solution)/shard_map/ppermute | solution.py:164
  56.5 0.1 collective-permute-start.4
  56.6 1.7 %collective-permute-start.5 = (f32[2,4,1080]{2,1,0:T(4,128)S(1)}, f32[2,4,1080]{2,1,0:T(4,128)S(1)}, u32[]{:S(2)}, u32[]{:S(2)}) collective-permute-start(f32[2,4,1080]{2,1,0:T(4,128)S(1)} %get-tuple-element.13), channel_id=1, source_target_pairs={{0,9},{1,16},{8,17},{9,24},{16,25},{17,0},{24,1},{25,8},{2,11},{3,... | collective-permute-start | bytes 103688 | tf_op jit(solution)/shard_map/ppermute | solution.py:164
  58.3 0.4 collective-permute-start.6
  58.7 2.8 %collective-permute-start.7 = (f32[2,4,1080]{2,1,0:T(4,128)S(1)}, f32[2,4,1080]{2,1,0:T(4,128)S(1)}, u32[]{:S(2)}, u32[]{:S(2)}) collective-permute-start(f32[2,4,1080]{2,1,0:T(4,128)S(1)} %get-tuple-element.13), channel_id=1, source_target_pairs={{0,17},{1,24},{8,25},{9,0},{16,1},{17,8},{24,9},{25,16},{2,19},{3,... | collective-permute-start | bytes 103688 | tf_op jit(solution)/shard_map/ppermute | solution.py:164
  61.5 0.8 %collective-permute-start.8 = (f32[2,4,1080]{2,1,0:T(4,128)S(1)}, f32[2,4,1080]{2,1,0:T(4,128)S(1)}, u32[]{:S(2)}, u32[]{:S(2)}) collective-permute-start(f32[2,4,1080]{2,1,0:T(4,128)S(1)} %get-tuple-element.13), channel_id=1, source_target_pairs={{0,24},{1,25},{8,0},{9,1},{16,8},{17,9},{24,16},{25,17},{2,26},{3,... | collective-permute-start | bytes 103688 | tf_op jit(solution)/shard_map/ppermute | solution.py:164
  62.4 0.3 collective-permute-start.9
  62.7 0.7 collective-permute-done.7
  63.4 0.6 collective-permute-done.8
  64.0 2.4 %collective-permute-done.9 = f32[2,4,1080]{2,1,0:T(4,128)S(1)} collective-permute-done((f32[2,4,1080]{2,1,0:T(4,128)S(1)}, f32[2,4,1080]{2,1,0:T(4,128)S(1)}, u32[]{:S(2)}, u32[]{:S(2)}) %collective-permute-start.9) | collective-permute-done | bytes 34592 | tf_op jit(solution)/shard_map/ppermute | solution.py:164
  66.4 0.7 %gather_fusion = f32[8,2,4,1080]{3,2,1,0:T(4,128)S(1)} fusion(f32[8,2,4,1080]{3,2,1,0:T(4,128)S(1)} %bitcast_dynamic-update-slice_fusion, s32[1024]{0:T(1024)S(1)} %pad_clamp_fusion.2), kind=kCustom, calls=%fused_computation.2 | custom fusion | bytes 552992 | tf_op jit(solution)/shard_map/jit(_take)/gather | solution.py:167
  67.1 0.1 select_bitcast_fusion
  67.3 0.6 gather_fusion.2
  67.9 0.6 gather_fusion.1
  68.5 0.7 %fusion.42 = f32[2,4,1080]{2,1,0:T(4,128)} fusion(f32[2,4,1080]{2,1,0:T(4,128)S(1)} %gather_fusion.2, f32[2,4,1080]{2,1,0:T(4,128)S(1)} %gather_fusion.1, f32[2]{0:T(128)S(1)} %get-tuple-element.11, f32[2]{0:T(128)S(1)} %get-tuple-element.10, pred[2]{0:T(512)(128)(4,1)S(1)} %copy-done.2, pred[2]{0:T(512)(128)(4,1)S(1)} %copy-done.1), kind=kLoop, calls=%fused_computation.86 | loop fusion | flops 43200 | bytes 103700 | tf_op jit(solution)/shard_map/add | solution.py:34
  (45 shorter events, 0.5 us)
Async XLA Ops:
  1.3 25.8 %copy-start = (s32[1280]{0:T(1024)S(1)}, s32[1280]{0:T(1024)}, u32[]{:S(2)}) copy-start(s32[1280]{0:T(1024)} %param.10) | copy-start | bytes 15364
  1.3 30.1 %copy-start.4 = (s32[16]{0:T(128)S(1)}, s32[16]{0:T(128)}, u32[]{:S(2)}) copy-start(s32[16]{0:T(128)} %param.12) | copy-start | bytes 196
  22.9 13.8 %all-to-all-start = ((bf16[320,8,48]{0,2,1:T(8,128)(2,1)}), bf16[320,8,48]{0,2,1:T(8,128)(2,1)S(1)}, u32[]{:S(2)}, u32[]{:S(2)}) async-start(bf16[320,8,48]{0,2,1:T(8,128)(2,1)} %copy.16), calls=%async_computation | async-start | bytes 589824 | tf_op jit(solution)/shard_map/all_to_all | solution.py:120
  40.1 1.6 %copy-start.3 = (f32[6]{0:T(128)S(1)}, f32[6]{0:T(128)}, u32[]{:S(2)}) copy-start(f32[6]{0:T(128)} %param.11) | copy-start | bytes 76
  40.1 10.0 %copy-start.5 = (f32[16]{0:T(128)S(1)}, f32[16]{0:T(128)}, u32[]{:S(2)}) copy-start(f32[16]{0:T(128)} %param.13) | copy-start | bytes 196
  41.1 27.3 %copy-start.1 = (pred[2]{0:T(512)(128)(4,1)S(1)}, pred[2]{0:T(512)(128)(4,1)}, u32[]{:S(2)}) copy-start(pred[2]{0:T(512)(128)(4,1)} %get-tuple-element.6) | copy-start | bytes 10
  41.1 27.3 %copy-start.2 = (pred[2]{0:T(512)(128)(4,1)S(1)}, pred[2]{0:T(512)(128)(4,1)}, u32[]{:S(2)}) copy-start(pred[2]{0:T(512)(128)(4,1)} %get-tuple-element.36) | copy-start | bytes 10
  44.6 6.2 %collective-permute-start.2 = (f32[2,4,1080]{2,1,0:T(4,128)S(1)}, f32[2,4,1080]{2,1,0:T(4,128)S(1)}, u32[]{:S(2)}, u32[]{:S(2)}) collective-permute-start(f32[2,4,1080]{2,1,0:T(4,128)S(1)} %bitcast.85), channel_id=1, source_target_pairs={{0,6},{2,0},{4,2},{6,4},{1,7},{3,1},{5,3},{7,5},{8,14},{10,8},{12,... | collective-permute-start | bytes 103688 | tf_op jit(solution)/shard_map/ppermute | solution.py:158
  49.0 5.3 %collective-permute-start.1 = (f32[2,4,1080]{2,1,0:T(4,128)S(1)}, f32[2,4,1080]{2,1,0:T(4,128)S(1)}, u32[]{:S(2)}, u32[]{:S(2)}) collective-permute-start(f32[2,4,1080]{2,1,0:T(4,128)S(1)} %bitcast.86), channel_id=1, source_target_pairs={{0,4},{2,6},{4,0},{6,2},{1,5},{3,7},{5,1},{7,3},{8,12},{10,14},{12... | collective-permute-start | bytes 103688 | tf_op jit(solution)/shard_map/ppermute | solution.py:158
  49.1 5.8 %collective-permute-start = (f32[2,4,1080]{2,1,0:T(4,128)S(1)}, f32[2,4,1080]{2,1,0:T(4,128)S(1)}, u32[]{:S(2)}, u32[]{:S(2)}) collective-permute-start(f32[2,4,1080]{2,1,0:T(4,128)S(1)} %bitcast.87), channel_id=1, source_target_pairs={{0,2},{2,4},{4,6},{6,0},{1,3},{3,5},{5,7},{7,1},{8,10},{10,12},{12... | collective-permute-start | bytes 103688 | tf_op jit(solution)/shard_map/ppermute | solution.py:158
  54.9 6.6 %collective-permute-start.3 = (f32[2,4,1080]{2,1,0:T(4,128)S(1)}, f32[2,4,1080]{2,1,0:T(4,128)S(1)}, u32[]{:S(2)}, u32[]{:S(2)}) collective-permute-start(f32[2,4,1080]{2,1,0:T(4,128)S(1)} %get-tuple-element.13), channel_id=1, source_target_pairs={{0,1},{1,8},{8,9},{9,16},{16,17},{17,24},{24,25},{25,0},{2,3},{3,1... | collective-permute-start | bytes 103688 | tf_op jit(solution)/shard_map/ppermute | solution.py:164
  56.5 5.9 %collective-permute-start.4 = (f32[2,4,1080]{2,1,0:T(4,128)S(1)}, f32[2,4,1080]{2,1,0:T(4,128)S(1)}, u32[]{:S(2)}, u32[]{:S(2)}) collective-permute-start(f32[2,4,1080]{2,1,0:T(4,128)S(1)} %get-tuple-element.13), channel_id=1, source_target_pairs={{0,8},{1,9},{8,16},{9,17},{16,24},{17,25},{24,0},{25,1},{2,10},{3,... | collective-permute-start | bytes 103688 | tf_op jit(solution)/shard_map/ppermute | solution.py:164
  56.6 6.1 %collective-permute-start.5 = (f32[2,4,1080]{2,1,0:T(4,128)S(1)}, f32[2,4,1080]{2,1,0:T(4,128)S(1)}, u32[]{:S(2)}, u32[]{:S(2)}) collective-permute-start(f32[2,4,1080]{2,1,0:T(4,128)S(1)} %get-tuple-element.13), channel_id=1, source_target_pairs={{0,9},{1,16},{8,17},{9,24},{16,25},{17,0},{24,1},{25,8},{2,11},{3,... | collective-permute-start | bytes 103688 | tf_op jit(solution)/shard_map/ppermute | solution.py:164
  58.3 4.4 %collective-permute-start.6 = (f32[2,4,1080]{2,1,0:T(4,128)S(1)}, f32[2,4,1080]{2,1,0:T(4,128)S(1)}, u32[]{:S(2)}, u32[]{:S(2)}) collective-permute-start(f32[2,4,1080]{2,1,0:T(4,128)S(1)} %get-tuple-element.13), channel_id=1, source_target_pairs={{0,16},{1,17},{8,24},{9,25},{16,0},{17,1},{24,8},{25,9},{2,18},{3,... | collective-permute-start | bytes 103688 | tf_op jit(solution)/shard_map/ppermute | solution.py:164
  58.7 4.7 %collective-permute-start.7 = (f32[2,4,1080]{2,1,0:T(4,128)S(1)}, f32[2,4,1080]{2,1,0:T(4,128)S(1)}, u32[]{:S(2)}, u32[]{:S(2)}) collective-permute-start(f32[2,4,1080]{2,1,0:T(4,128)S(1)} %get-tuple-element.13), channel_id=1, source_target_pairs={{0,17},{1,24},{8,25},{9,0},{16,1},{17,8},{24,9},{25,16},{2,19},{3,... | collective-permute-start | bytes 103688 | tf_op jit(solution)/shard_map/ppermute | solution.py:164
  61.5 2.5 %collective-permute-start.8 = (f32[2,4,1080]{2,1,0:T(4,128)S(1)}, f32[2,4,1080]{2,1,0:T(4,128)S(1)}, u32[]{:S(2)}, u32[]{:S(2)}) collective-permute-start(f32[2,4,1080]{2,1,0:T(4,128)S(1)} %get-tuple-element.13), channel_id=1, source_target_pairs={{0,24},{1,25},{8,0},{9,1},{16,8},{17,9},{24,16},{25,17},{2,26},{3,... | collective-permute-start | bytes 103688 | tf_op jit(solution)/shard_map/ppermute | solution.py:164
  62.4 4.0 %collective-permute-start.9 = (f32[2,4,1080]{2,1,0:T(4,128)S(1)}, f32[2,4,1080]{2,1,0:T(4,128)S(1)}, u32[]{:S(2)}, u32[]{:S(2)}) collective-permute-start(f32[2,4,1080]{2,1,0:T(4,128)S(1)} %get-tuple-element.13), channel_id=1, source_target_pairs={{0,25},{1,0},{8,1},{9,8},{16,9},{17,16},{24,17},{25,24},{2,27},{3,... | collective-permute-start | bytes 103688 | tf_op jit(solution)/shard_map/ppermute | solution.py:164

commit v9 on v6

--- a/solution.py
+++ b/solution.py
@@ -54,19 +54,52 @@
     )
 
 
-def legendre_kernel(waves_ref, spec_ref, table_ref, out_ref):
-    block = spec_ref.shape[0]
-    degree = spec_ref.shape[-1]
-    first = pl.program_id(0) * block
+def legendre_kernel(waves_ref, spec_hbm, table_ref, out_ref, buf, sem):
+    block = out_ref.shape[0]
+    degree = table_ref.shape[-1]
+    chunk = 256 if degree % 256 == 0 else LANE
+    chunks = degree // chunk
+    step = pl.program_id(0)
+    steps = pl.num_programs(0)
+
+    def each_copy(at, held, act):
+        def one(s, carry):
+            needed = (degree - waves_ref[at * block + s] + chunk - 1) // chunk
+            for n in range(1, chunks + 1):
+
+                @pl.when(needed == n)
+                def _():
+                    act(
+                        pltpu.make_async_copy(
+                            spec_hbm.at[at * block + s, :, :, :, pl.ds(0, n * chunk)],
+                            buf.at[held, s, :, :, :, pl.ds(0, n * chunk)],
+                            sem.at[held],
+                        )
+                    )
+
+            return carry
+
+        lax.fori_loop(0, block, one, 0)
+
+    @pl.when(step == 0)
+    def _():
+        each_copy(0, 0, lambda c: c.start())
+
+    @pl.when(step + 1 < steps)
+    def _():
+        each_copy(step + 1, (step + 1) % 2, lambda c: c.start())
+
+    current = step % 2
+    each_copy(step, current, lambda c: c.wait())
+    first = step * block
 
     def one_slot(s, carry):
         limit = degree - waves_ref[first + s]
-        rows = table_ref[s]
-        column = lax.broadcasted_iota(jnp.int32, rows.shape, 1)
-        rows = jnp.where(column < limit, rows, jnp.zeros_like(rows))
-        coefficient = spec_ref[s].reshape(-1, degree)
+        coefficient = buf[current, s].reshape(-1, degree).astype(jnp.float32)
+        column = lax.broadcasted_iota(jnp.int32, coefficient.shape, 1)
+        coefficient = jnp.where(column < limit, coefficient, 0.0).astype(jnp.bfloat16)
         out_ref[s] = lax.dot_general(
-            rows, coefficient, (((1,), (1,)), ((), ())), preferred_element_type=jnp.float32
+            table_ref[s], coefficient, (((1,), (1,)), ((), ())), preferred_element_type=jnp.float32
         ).astype(out_ref.dtype)
         return carry
 
@@ -85,14 +118,18 @@
             num_scalar_prefetch=1,
             grid=(slots // block,),
             in_specs=[
-                pl.BlockSpec((block, 2, levels, fields, degree), lambda i, w: (i, 0, 0, 0, 0)),
+                pl.BlockSpec(memory_space=pl.ANY),
                 pl.BlockSpec((block, lats, degree), lambda i, w: (i, 0, 0)),
             ],
             out_specs=pl.BlockSpec((block, lats, channels), lambda i, w: (i, 0, 0)),
+            scratch_shapes=[
+                pltpu.VMEM((2, block, 2, levels, fields, degree), stored.dtype),
+                pltpu.SemaphoreType.DMA((2,)),
+            ],
         ),
         cost_estimate=pl.CostEstimate(
             flops=2 * slots * lats * channels * degree,
-            bytes_accessed=2 * slots * degree * (channels + lats),
+            bytes_accessed=slots * degree * (channels + lats),
             transcendentals=0,
         ),
     )(owned_waves, stored, legendre)

time: 68.2 us -> 75 us (1.100)
  Pallas kernels: 19 us -> 25.8 us
    pallas_call x1, Pallas kernels: 19 us -> 25.8 us  [legendre_transform(): pl.pallas_call(legendre_kernel, out_shape=jax.ShapeDtypeStruct((slots, la...]
  transfers between devices with their start and end apart: 3 -> 3, of which waited for: 2 -> 2; matrix products, arithmetic and copies ran while one was open for 10% -> 9% of each run, Pallas kernels for 0% -> 0%
where the time goes in v9:
time: 75 us; the launch traced here: 74.5 us
  Pallas kernels  25.8 us (34%)
  starting transfers between devices  13.8 us (18%)
  waiting for transfers between devices  13.3 us (18%)
  local copies, waits for them, and re-layouts  9.23 us (12%)
  other arithmetic  8.29 us (11%)
  matrix products  3.85 us (5%)
    pallas_call x1, Pallas kernels, legendre_transform(): pl.pallas_call(legendre_kernel, out_shape=jax.ShapeDtypeStruct((slots, la...  25.8 us
    all_to_all x1, waiting for transfers between devices, local(): lax.all_to_all(by_strip, 'lev', split_axis=0, concat_axis=0, tiled=True)  6.64 us
    all_to_all x1, waiting for transfers between devices, local(): lax.all_to_all(copies, ('wave', 'cpl'), split_axis=0, concat_axis=0, tile...  6.63 us
    all_to_all x1, starting transfers between devices, local(): lax.all_to_all(by_strip, 'lev', split_axis=0, concat_axis=0, tiled=True)  5.55 us
    all_to_all x1, starting transfers between devices, local(): lax.all_to_all(spec_grid, 'wave', split_axis=1, concat_axis=0, tiled=True)  4.24 us
    all_to_all x1, starting transfers between devices, local(): lax.all_to_all(copies, ('wave', 'cpl'), split_axis=0, concat_axis=0, tile...  3.98 us
    convert_element_type x1, other arithmetic, quarter_tables(): cos_tab.astype(jnp.bfloat16).reshape(slots, width)  3.36 us
    dot_general x1, matrix products, local(): q_all = jnp.dot(lhs_sin, sin_tab, preferred_element_type=jnp.float32)  2.84 us
  transfers between devices with their start and end apart: 3, of which 2 were waited for; matrix products, arithmetic and copies ran while one was open for 9% of the time, Pallas kernels for 0%

profile of v9, /device:TPU:0, one launch (start us, length us, event | category | flops | bytes accessed | tf_op | source)
XLA Modules:
  0.0 74.5 jit_solution(12838134204295241032)
XLA Ops:
  0.0 1.3 %dynamic_slice.10.waves_ref = s32[320]{0:T(512)} dynamic-slice(s32[1280]{0:T(1024)} %param.10, s32[]{:T(128)S(6)} %select_n.46), dynamic_slice_sizes={320} | dynamic-slice | bytes 2564 | tf_op jit(solution)/shard_map/dynamic_slice | solution.py:149
  1.3 0.0 copy-start
  1.3 25.8 %shard_map.64 = bf16[320,8,48]{2,1,0:T(8,128)(2,1)} custom-call(s32[320]{0:T(512)} %dynamic_slice.10.waves_ref, bf16[320,2,6,4,1280]{4,3,2,1,0:T(4,128)(2,1)} %bitcast.38, bf16[320,8,1280]{2,1,0:T(8,128)(2,1)} %table_ref.1), custom_call_target="tpu_custom_call" | custom-call | flops 314572800 | bytes 22937600 | tf_op jit(solution)/shard_map/pallas_call | solution.py:114
  27.2 1.7 %copy.19 = bf16[320,8,48]{0,1,2:T(8,128)(2,1)S(1)} copy(bf16[320,8,48]{2,1,0:T(8,128)(2,1)} %shard_map.64) | data formatting | bytes 491520 | tf_op jit(solution)/shard_map/pallas_call | solution.py:114
  28.9 0.8 %copy.21 = bf16[320,8,48]{0,2,1:T(8,128)(2,1)} copy(bf16[320,8,48]{0,1,2:T(8,128)(2,1)S(1)} %bitcast.43) | data formatting | bytes 491520 | tf_op jit(solution)/shard_map/reshape | solution.py:155
  29.7 4.2 %all-to-all-start = ((bf16[320,8,48]{0,2,1:T(8,128)(2,1)}), bf16[320,8,48]{0,2,1:T(8,128)(2,1)S(1)}, u32[]{:S(2)}, u32[]{:S(2)}) async-start(bf16[320,8,48]{0,2,1:T(8,128)(2,1)} %copy.21), calls=%async_computation | async-start | bytes 589824 | tf_op jit(solution)/shard_map/all_to_all | solution.py:157
  33.9 0.0 copy-done
  33.9 2.6 %fusion.5 = (f32[1280,128]{0,1:T(8,128)S(1)}, f32[1280,128]{0,1:T(8,128)S(1)}) fusion(s32[1280]{0:T(1024)S(1)} %copy-done), kind=kLoop, calls=%fused_computation.11 | loop fusion | flops 1474560 | bytes 1315840 | tf_op jit(solution)/shard_map/cos | solution.py:42
  36.6 0.4 cosine_multiply_fusion
  37.0 3.4 %subtract_convert_fusion = (bf16[1280,9,128]{0,2,1:T(8,128)(2,1)S(1)}, bf16[1280,9,128]{0,2,1:T(8,128)(2,1)}) fusion(f32[1280,128]{0,1:T(8,128)S(1)} %get-tuple-element.27, f32[1280,9]{0,1:T(8,128)S(1)} %get-tuple-element.25, f32[1280,128]{0,1:T(8,128)S(1)} %get-tuple-element.26, f32[1280,9]{0,1:T(8,128)S(1)} %get-tuple-element.24), kind=kLoop, calls=%fused_computation.3 | loop fusion | flops 13271040 | bytes 7301120 | tf_op jit(solution)/shard_map/convert_element_type | solution.py:52
  40.3 0.0 all-to-all-done
  40.4 0.2 copy.26
  40.5 0.3 reshape.201
  40.8 2.8 %fusion.11 = f32[96,1152]{1,0:T(8,128)S(1)} fusion(bf16[1280,1152]{0,1:T(8,128)(2,1)} %bitcast.40, bf16[48,1280]{1,0:T(8,128)(2,1)S(1)} %get-tuple-element.29, bf16[48,1280]{1,0:T(8,128)(2,1)S(1)} %bitcast.47), kind=kOutput, calls=%fused_computation.22 | convolution fusion | flops 283607040 | bytes 3637248 | tf_op jit(solution)/shard_map/dot_general | solution.py:172
  43.7 0.0 copy-start.1
  43.7 1.0 %fusion.7 = f32[96,1152]{1,0:T(8,128)S(1)} fusion(bf16[1280,1152]{0,1:T(8,128)(2,1)S(1)} %bitcast.39, bf16[48,1280]{1,0:T(8,128)(2,1)S(1)} %get-tuple-element.28, bf16[48,1280]{1,0:T(8,128)(2,1)S(1)} %bitcast.46), kind=kOutput, calls=%fused_computation.18 | convolution fusion | flops 283607040 | bytes 3637248 | tf_op jit(solution)/shard_map/dot_general | solution.py:171
  44.8 0.0 copy-start.2
  44.8 0.0 copy-start.3
  44.8 0.3 slice_subtract_fusion
  45.3 0.0 copy-done.1
  45.3 0.2 fusion.24
  45.5 0.1 multiply_reduce_fusion.3
  45.6 0.1 multiply_reduce_fusion.2
  45.7 0.8 %reverse = f32[2,4,1152]{2,1,0:T(4,128)S(1)} reverse(f32[2,4,1152]{2,1,0:T(4,128)S(1)} %bitcast.51), dimensions={2} | reverse | bytes 73728
  46.5 0.1 slice.162
  46.6 0.1 multiply_reduce_fusion.1
  46.7 0.1 multiply_reduce_fusion
  46.8 0.8 %reverse.1 = f32[2,4,1152]{2,1,0:T(4,128)S(1)} reverse(f32[2,4,1152]{2,1,0:T(4,128)S(1)} %bitcast.52), dimensions={2} | reverse | bytes 73728
  47.6 0.1 slice.163
  47.7 0.2 concatenate.11
  47.9 0.2 reshape.206
  48.1 0.7 copy.23
  48.8 5.5 %all-to-all-start.1 = ((f32[4,2,4,1080]{3,2,1,0:T(4,128)}), f32[4,2,4,1080]{3,2,1,0:T(4,128)S(1)}, u32[]{:S(2)}, u32[]{:S(2)}) async-start(f32[4,2,4,1080]{3,2,1,0:T(4,128)} %copy.23), calls=%async_computation.1 | async-start | bytes 294912 | tf_op jit(solution)/shard_map/all_to_all | solution.py:191
  54.3 6.6 %all-to-all-done.1 = f32[4,2,4,1080]{3,2,1,0:T(4,128)S(1)} async-done(((f32[4,2,4,1080]{3,2,1,0:T(4,128)}), f32[4,2,4,1080]{3,2,1,0:T(4,128)S(1)}, u32[]{:S(2)}, u32[]{:S(2)}) %all-to-all-start.1) | async-done | bytes 138272 | tf_op jit(solution)/shard_map/all_to_all | solution.py:191
  61.0 0.7 %broadcast_in_dim.18 = f32[8,2,4,1080]{3,2,1,0:T(4,128)} broadcast(f32[2,4,1080]{2,1,0:T(4,128)S(1)} %reduce_sum.49), dimensions={1,2,3} | broadcast | bytes 311040 | tf_op jit(solution)/shard_map/broadcast_in_dim | solution.py:193
  61.8 4.0 %all-to-all-start.2 = ((f32[8,2,4,1080]{3,2,1,0:T(4,128)}), f32[8,2,4,1080]{3,2,1,0:T(4,128)S(1)}, u32[]{:S(2)}, u32[]{:S(2)}) async-start(f32[8,2,4,1080]{3,2,1,0:T(4,128)} %broadcast_in_dim.18), calls=%async_computation.2 | async-start | bytes 589824 | tf_op jit(solution)/shard_map/all_to_all | solution.py:194
  65.7 0.0 copy-done.2
  65.8 0.1 broadcast_subtract_fusion
  65.8 0.0 copy-done.3
  65.8 0.1 compare_and_fusion.1
  65.9 6.6 %all-to-all-done.2 = f32[8,2,4,1080]{3,2,1,0:T(4,128)S(1)} async-done(((f32[8,2,4,1080]{3,2,1,0:T(4,128)}), f32[8,2,4,1080]{3,2,1,0:T(4,128)S(1)}, u32[]{:S(2)}, u32[]{:S(2)}) %all-to-all-start.2) | async-done | bytes 276512 | tf_op jit(solution)/shard_map/all_to_all | solution.py:194
  72.6 0.6 gather_fusion.1
  73.2 0.6 gather_fusion
  73.7 0.7 fusion.40
  (15 shorter events, 0.3 us)
Async XLA Ops:
  1.3 32.6 %copy-start = (s32[1280]{0:T(1024)S(1)}, s32[1280]{0:T(1024)}, u32[]{:S(2)}) copy-start(s32[1280]{0:T(1024)} %param.10) | copy-start | bytes 15364
  29.7 10.7 %all-to-all-start = ((bf16[320,8,48]{0,2,1:T(8,128)(2,1)}), bf16[320,8,48]{0,2,1:T(8,128)(2,1)S(1)}, u32[]{:S(2)}, u32[]{:S(2)}) async-start(bf16[320,8,48]{0,2,1:T(8,128)(2,1)} %copy.21), calls=%async_computation | async-start | bytes 589824 | tf_op jit(solution)/shard_map/all_to_all | solution.py:157
  43.7 1.6 %copy-start.1 = (f32[6]{0:T(128)S(1)}, f32[6]{0:T(128)}, u32[]{:S(2)}) copy-start(f32[6]{0:T(128)} %param.11) | copy-start | bytes 76
  44.8 21.0 %copy-start.2 = (f32[16]{0:T(128)S(1)}, f32[16]{0:T(128)}, u32[]{:S(2)}) copy-start(f32[16]{0:T(128)} %param.13) | copy-start | bytes 196
  44.8 21.1 %copy-start.3 = (s32[16]{0:T(128)S(1)}, s32[16]{0:T(128)}, u32[]{:S(2)}) copy-start(s32[16]{0:T(128)} %param.12) | copy-start | bytes 196
  48.8 12.2 %all-to-all-start.1 = ((f32[4,2,4,1080]{3,2,1,0:T(4,128)}), f32[4,2,4,1080]{3,2,1,0:T(4,128)S(1)}, u32[]{:S(2)}, u32[]{:S(2)}) async-start(f32[4,2,4,1080]{3,2,1,0:T(4,128)} %copy.23), calls=%async_computation.1 | async-start | bytes 294912 | tf_op jit(solution)/shard_map/all_to_all | solution.py:191
  61.8 10.8 %all-to-all-start.2 = ((f32[8,2,4,1080]{3,2,1,0:T(4,128)}), f32[8,2,4,1080]{3,2,1,0:T(4,128)S(1)}, u32[]{:S(2)}, u32[]{:S(2)}) async-start(f32[8,2,4,1080]{3,2,1,0:T(4,128)} %broadcast_in_dim.18), calls=%async_computation.2 | async-start | bytes 589824 | tf_op jit(solution)/shard_map/all_to_all | solution.py:194

commit v10 on v9

--- a/solution.py
+++ b/solution.py
@@ -83,6 +83,7 @@
 
     @pl.when(step == 0)
     def _():
+        buf[...] = jnp.zeros(buf.shape, buf.dtype)
         each_copy(0, 0, lambda c: c.start())
 
     @pl.when(step + 1 < steps)
@@ -95,11 +96,12 @@
 
     def one_slot(s, carry):
         limit = degree - waves_ref[first + s]
-        coefficient = buf[current, s].reshape(-1, degree).astype(jnp.float32)
-        column = lax.broadcasted_iota(jnp.int32, coefficient.shape, 1)
-        coefficient = jnp.where(column < limit, coefficient, 0.0).astype(jnp.bfloat16)
+        coefficient = buf[current, s].reshape(-1, degree)
+        rows = table_ref[s]
+        column = lax.broadcasted_iota(jnp.int32, rows.shape, 1)
+        rows = jnp.where(column < limit, rows, jnp.zeros_like(rows))
         out_ref[s] = lax.dot_general(
-            table_ref[s], coefficient, (((1,), (1,)), ((), ())), preferred_element_type=jnp.float32
+            rows, coefficient, (((1,), (1,)), ((), ())), preferred_element_type=jnp.float32
         ).astype(out_ref.dtype)
         return carry
 

time: 75 us -> 76.4 us (1.019)
  Pallas kernels: 25.8 us -> 27.2 us
    pallas_call x1, Pallas kernels: 25.8 us -> 27.2 us  [legendre_transform(): pl.pallas_call(legendre_kernel, out_shape=jax.ShapeDtypeStruct((slots, la...]
where the time goes in v10:
time: 76.4 us; the launch traced here: 75.8 us
  Pallas kernels  27.2 us (36%)
  starting transfers between devices  13.8 us (18%)
  waiting for transfers between devices  13.3 us (17%)
  local copies, waits for them, and re-layouts  9.23 us (12%)
  other arithmetic  8.29 us (11%)
  matrix products  3.85 us (5%)
    pallas_call x1, Pallas kernels, legendre_transform(): pl.pallas_call(legendre_kernel, out_shape=jax.ShapeDtypeStruct((slots, la...  27.2 us
    all_to_all x1, waiting for transfers between devices, local(): lax.all_to_all(by_strip, 'lev', split_axis=0, concat_axis=0, tiled=True)  6.64 us
    all_to_all x1, waiting for transfers between devices, local(): lax.all_to_all(copies, ('wave', 'cpl'), split_axis=0, concat_axis=0, tile...  6.63 us
    all_to_all x1, starting transfers between devices, local(): lax.all_to_all(by_strip, 'lev', split_axis=0, concat_axis=0, tiled=True)  5.55 us
    all_to_all x1, starting transfers between devices, local(): lax.all_to_all(spec_grid, 'wave', split_axis=1, concat_axis=0, tiled=True)  4.24 us
    all_to_all x1, starting transfers between devices, local(): lax.all_to_all(copies, ('wave', 'cpl'), split_axis=0, concat_axis=0, tile...  3.98 us
    convert_element_type x1, other arithmetic, quarter_tables(): cos_tab.astype(jnp.bfloat16).reshape(slots, width)  3.36 us
    dot_general x1, matrix products, local(): q_all = jnp.dot(lhs_sin, sin_tab, preferred_element_type=jnp.float32)  2.84 us
  transfers between devices with their start and end apart: 3, of which 2 were waited for; matrix products, arithmetic and copies ran while one was open for 9% of the time, Pallas kernels for 0%

profile of v10, /device:TPU:0, one launch (start us, length us, event | category | flops | bytes accessed | tf_op | source)
XLA Modules:
  0.0 75.8 jit_solution(13150009443950764828)
XLA Ops:
  0.0 1.3 %dynamic_slice.10.waves_ref = s32[320]{0:T(512)} dynamic-slice(s32[1280]{0:T(1024)} %param.10, s32[]{:T(128)S(6)} %select_n.46), dynamic_slice_sizes={320} | dynamic-slice | bytes 2564 | tf_op jit(solution)/shard_map/dynamic_slice | solution.py:151
  1.3 0.0 copy-start
  1.3 27.2 %shard_map.64 = bf16[320,8,48]{2,1,0:T(8,128)(2,1)} custom-call(s32[320]{0:T(512)} %dynamic_slice.10.waves_ref, bf16[320,2,6,4,1280]{4,3,2,1,0:T(4,128)(2,1)} %bitcast.38, bf16[320,8,1280]{2,1,0:T(8,128)(2,1)} %table_ref.1), custom_call_target="tpu_custom_call" | custom-call | flops 314572800 | bytes 22937600 | tf_op jit(solution)/shard_map/pallas_call | solution.py:116
  28.5 1.7 %copy.19 = bf16[320,8,48]{0,1,2:T(8,128)(2,1)S(1)} copy(bf16[320,8,48]{2,1,0:T(8,128)(2,1)} %shard_map.64) | data formatting | bytes 491520 | tf_op jit(solution)/shard_map/pallas_call | solution.py:116
  30.3 0.8 %copy.21 = bf16[320,8,48]{0,2,1:T(8,128)(2,1)} copy(bf16[320,8,48]{0,1,2:T(8,128)(2,1)S(1)} %bitcast.43) | data formatting | bytes 491520 | tf_op jit(solution)/shard_map/reshape | solution.py:157
  31.0 4.2 %all-to-all-start = ((bf16[320,8,48]{0,2,1:T(8,128)(2,1)}), bf16[320,8,48]{0,2,1:T(8,128)(2,1)S(1)}, u32[]{:S(2)}, u32[]{:S(2)}) async-start(bf16[320,8,48]{0,2,1:T(8,128)(2,1)} %copy.21), calls=%async_computation | async-start | bytes 589824 | tf_op jit(solution)/shard_map/all_to_all | solution.py:159
  35.3 0.0 copy-done
  35.3 2.6 %fusion.5 = (f32[1280,128]{0,1:T(8,128)S(1)}, f32[1280,128]{0,1:T(8,128)S(1)}) fusion(s32[1280]{0:T(1024)S(1)} %copy-done), kind=kLoop, calls=%fused_computation.11 | loop fusion | flops 1474560 | bytes 1315840 | tf_op jit(solution)/shard_map/cos | solution.py:42
  37.9 0.4 cosine_multiply_fusion
  38.3 3.4 %subtract_convert_fusion = (bf16[1280,9,128]{0,2,1:T(8,128)(2,1)S(1)}, bf16[1280,9,128]{0,2,1:T(8,128)(2,1)}) fusion(f32[1280,128]{0,1:T(8,128)S(1)} %get-tuple-element.27, f32[1280,9]{0,1:T(8,128)S(1)} %get-tuple-element.25, f32[1280,128]{0,1:T(8,128)S(1)} %get-tuple-element.26, f32[1280,9]{0,1:T(8,128)S(1)} %get-tuple-element.24), kind=kLoop, calls=%fused_computation.3 | loop fusion | flops 13271040 | bytes 7301120 | tf_op jit(solution)/shard_map/convert_element_type | solution.py:52
  41.7 0.0 all-to-all-done
  41.7 0.2 copy.26
  41.9 0.3 reshape.201
  42.2 2.8 %fusion.11 = f32[96,1152]{1,0:T(8,128)S(1)} fusion(bf16[1280,1152]{0,1:T(8,128)(2,1)} %bitcast.40, bf16[48,1280]{1,0:T(8,128)(2,1)S(1)} %get-tuple-element.29, bf16[48,1280]{1,0:T(8,128)(2,1)S(1)} %bitcast.47), kind=kOutput, calls=%fused_computation.22 | convolution fusion | flops 283607040 | bytes 3637248 | tf_op jit(solution)/shard_map/dot_general | solution.py:174
  45.1 0.0 copy-start.1
  45.1 1.0 %fusion.7 = f32[96,1152]{1,0:T(8,128)S(1)} fusion(bf16[1280,1152]{0,1:T(8,128)(2,1)S(1)} %bitcast.39, bf16[48,1280]{1,0:T(8,128)(2,1)S(1)} %get-tuple-element.28, bf16[48,1280]{1,0:T(8,128)(2,1)S(1)} %bitcast.46), kind=kOutput, calls=%fused_computation.18 | convolution fusion | flops 283607040 | bytes 3637248 | tf_op jit(solution)/shard_map/dot_general | solution.py:173
  46.1 0.0 copy-start.2
  46.1 0.0 copy-start.3
  46.2 0.3 slice_subtract_fusion
  46.7 0.0 copy-done.1
  46.7 0.2 fusion.24
  46.8 0.1 multiply_reduce_fusion.3
  46.9 0.1 multiply_reduce_fusion.2
  47.1 0.8 %reverse = f32[2,4,1152]{2,1,0:T(4,128)S(1)} reverse(f32[2,4,1152]{2,1,0:T(4,128)S(1)} %bitcast.51), dimensions={2} | reverse | bytes 73728
  47.9 0.1 slice.162
  48.0 0.1 multiply_reduce_fusion.1
  48.1 0.1 multiply_reduce_fusion
  48.2 0.8 %reverse.1 = f32[2,4,1152]{2,1,0:T(4,128)S(1)} reverse(f32[2,4,1152]{2,1,0:T(4,128)S(1)} %bitcast.52), dimensions={2} | reverse | bytes 73728
  49.0 0.1 slice.163
  49.1 0.2 concatenate.11
  49.3 0.2 reshape.206
  49.5 0.7 copy.23
  50.2 5.5 %all-to-all-start.1 = ((f32[4,2,4,1080]{3,2,1,0:T(4,128)}), f32[4,2,4,1080]{3,2,1,0:T(4,128)S(1)}, u32[]{:S(2)}, u32[]{:S(2)}) async-start(f32[4,2,4,1080]{3,2,1,0:T(4,128)} %copy.23), calls=%async_computation.1 | async-start | bytes 294912 | tf_op jit(solution)/shard_map/all_to_all | solution.py:193
  55.7 6.6 %all-to-all-done.1 = f32[4,2,4,1080]{3,2,1,0:T(4,128)S(1)} async-done(((f32[4,2,4,1080]{3,2,1,0:T(4,128)}), f32[4,2,4,1080]{3,2,1,0:T(4,128)S(1)}, u32[]{:S(2)}, u32[]{:S(2)}) %all-to-all-start.1) | async-done | bytes 138272 | tf_op jit(solution)/shard_map/all_to_all | solution.py:193
  62.4 0.7 broadcast_in_dim.18
  63.1 4.0 %all-to-all-start.2 = ((f32[8,2,4,1080]{3,2,1,0:T(4,128)}), f32[8,2,4,1080]{3,2,1,0:T(4,128)S(1)}, u32[]{:S(2)}, u32[]{:S(2)}) async-start(f32[8,2,4,1080]{3,2,1,0:T(4,128)} %broadcast_in_dim.18), calls=%async_computation.2 | async-start | bytes 589824 | tf_op jit(solution)/shard_map/all_to_all | solution.py:196
  67.1 0.0 copy-done.2
  67.1 0.1 broadcast_subtract_fusion
  67.2 0.0 copy-done.3
  67.2 0.1 compare_and_fusion.1
  67.3 6.6 %all-to-all-done.2 = f32[8,2,4,1080]{3,2,1,0:T(4,128)S(1)} async-done(((f32[8,2,4,1080]{3,2,1,0:T(4,128)}), f32[8,2,4,1080]{3,2,1,0:T(4,128)S(1)}, u32[]{:S(2)}, u32[]{:S(2)}) %all-to-all-start.2) | async-done | bytes 276512 | tf_op jit(solution)/shard_map/all_to_all | solution.py:196
  74.0 0.6 gather_fusion.1
  74.5 0.6 gather_fusion
  75.1 0.7 fusion.40
  (15 shorter events, 0.3 us)
Async XLA Ops:
  1.3 33.9 %copy-start = (s32[1280]{0:T(1024)S(1)}, s32[1280]{0:T(1024)}, u32[]{:S(2)}) copy-start(s32[1280]{0:T(1024)} %param.10) | copy-start | bytes 15364
  31.0 10.7 %all-to-all-start = ((bf16[320,8,48]{0,2,1:T(8,128)(2,1)}), bf16[320,8,48]{0,2,1:T(8,128)(2,1)S(1)}, u32[]{:S(2)}, u32[]{:S(2)}) async-start(bf16[320,8,48]{0,2,1:T(8,128)(2,1)} %copy.21), calls=%async_computation | async-start | bytes 589824 | tf_op jit(solution)/shard_map/all_to_all | solution.py:159
  45.1 1.6 %copy-start.1 = (f32[6]{0:T(128)S(1)}, f32[6]{0:T(128)}, u32[]{:S(2)}) copy-start(f32[6]{0:T(128)} %param.11) | copy-start | bytes 76
  46.1 21.0 %copy-start.2 = (f32[16]{0:T(128)S(1)}, f32[16]{0:T(128)}, u32[]{:S(2)}) copy-start(f32[16]{0:T(128)} %param.13) | copy-start | bytes 196
  46.1 21.1 %copy-start.3 = (s32[16]{0:T(128)S(1)}, s32[16]{0:T(128)}, u32[]{:S(2)}) copy-start(s32[16]{0:T(128)} %param.12) | copy-start | bytes 196
  50.2 12.2 %all-to-all-start.1 = ((f32[4,2,4,1080]{3,2,1,0:T(4,128)}), f32[4,2,4,1080]{3,2,1,0:T(4,128)S(1)}, u32[]{:S(2)}, u32[]{:S(2)}) async-start(f32[4,2,4,1080]{3,2,1,0:T(4,128)} %copy.23), calls=%async_computation.1 | async-start | bytes 294912 | tf_op jit(solution)/shard_map/all_to_all | solution.py:193
  63.1 10.8 %all-to-all-start.2 = ((f32[8,2,4,1080]{3,2,1,0:T(4,128)}), f32[8,2,4,1080]{3,2,1,0:T(4,128)S(1)}, u32[]{:S(2)}, u32[]{:S(2)}) async-start(f32[8,2,4,1080]{3,2,1,0:T(4,128)} %broadcast_in_dim.18), calls=%async_computation.2 | async-start | bytes 589824 | tf_op jit(solution)/shard_map/all_to_all | solution.py:196

commit v11 on v6

--- a/solution.py
+++ b/solution.py
@@ -37,10 +37,15 @@
 def quarter_tables(wavenumber, width):
     blocks = width // LANE
     factor = jnp.where(wavenumber == 0, 1.0, 2.0).astype(jnp.float32)[:, None]
-    offsets = jnp.arange(LANE, dtype=jnp.int32)
-    base_angle = phase_angle(wavenumber[:, None] * offsets[None, :] % NLON, NLON)
-    base_cos = jnp.cos(base_angle)[:, None, :]
-    base_sin = jnp.sin(base_angle)[:, None, :]
+    fine_count = 16
+    fine = jnp.arange(fine_count, dtype=jnp.int32)
+    coarse = jnp.arange(LANE // fine_count, dtype=jnp.int32) * fine_count
+    fine_angle = phase_angle(wavenumber[:, None] * fine[None, :] % NLON, NLON)[:, None, :]
+    coarse_angle = phase_angle(wavenumber[:, None] * coarse[None, :] % NLON, NLON)[:, :, None]
+    fine_cos, fine_sin = jnp.cos(fine_angle), jnp.sin(fine_angle)
+    coarse_cos, coarse_sin = jnp.cos(coarse_angle), jnp.sin(coarse_angle)
+    base_cos = (coarse_cos * fine_cos - coarse_sin * fine_sin).reshape(-1, 1, LANE)
+    base_sin = (coarse_sin * fine_cos + coarse_cos * fine_sin).reshape(-1, 1, LANE)
     starts = jnp.arange(blocks, dtype=jnp.int32) * LANE
     start_angle = phase_angle(wavenumber[:, None] * starts[None, :] % NLON, NLON)
     start_cos = (factor * jnp.cos(start_angle))[:, :, None]
@@ -54,10 +59,10 @@
     )
 
 
-def legendre_kernel(waves_ref, spec_ref, table_ref, out_ref):
+def legendre_kernel(offset_ref, waves_ref, spec_ref, table_ref, out_ref):
     block = spec_ref.shape[0]
     degree = spec_ref.shape[-1]
-    first = pl.program_id(0) * block
+    first = offset_ref[0] + pl.program_id(0) * block
 
     def one_slot(s, carry):
         limit = degree - waves_ref[first + s]
@@ -73,7 +78,7 @@
     lax.fori_loop(0, block, one_slot, 0, unroll=True)
 
 
-def legendre_transform(stored, legendre, owned_waves):
+def legendre_transform(stored, legendre, wavenumber, offset):
     slots, _, levels, fields, degree = stored.shape
     lats = legendre.shape[1]
     channels = 2 * levels * fields
@@ -82,20 +87,20 @@
         legendre_kernel,
         out_shape=jax.ShapeDtypeStruct((slots, lats, channels), jnp.bfloat16),
         grid_spec=pltpu.PrefetchScalarGridSpec(
-            num_scalar_prefetch=1,
+            num_scalar_prefetch=2,
             grid=(slots // block,),
             in_specs=[
-                pl.BlockSpec((block, 2, levels, fields, degree), lambda i, w: (i, 0, 0, 0, 0)),
-                pl.BlockSpec((block, lats, degree), lambda i, w: (i, 0, 0)),
+                pl.BlockSpec((block, 2, levels, fields, degree), lambda i, o, w: (i, 0, 0, 0, 0)),
+                pl.BlockSpec((block, lats, degree), lambda i, o, w: (i, 0, 0)),
             ],
-            out_specs=pl.BlockSpec((block, lats, channels), lambda i, w: (i, 0, 0)),
+            out_specs=pl.BlockSpec((block, lats, channels), lambda i, o, w: (i, 0, 0)),
         ),
         cost_estimate=pl.CostEstimate(
             flops=2 * slots * lats * channels * degree,
             bytes_accessed=2 * slots * degree * (channels + lats),
             transcendentals=0,
         ),
-    )(owned_waves, stored, legendre)
+    )(offset, wavenumber, stored, legendre)
 
 
 def local(spectral, legendre, wavenumber, level_weight, source_row, row_weight):
@@ -109,10 +114,11 @@
     lev_count = lax.axis_size("lev")
     wave_at = lax.axis_index("wave")
     cpl_at = lax.axis_index("cpl")
-    owned_waves = lax.dynamic_slice_in_dim(wavenumber, wave_at * slot_count, slot_count)
     stored = jnp.transpose(spectral, (0, 1, 3, 2, 4))
     spec_grid = (
-        legendre_transform(stored, legendre, owned_waves)
+        legendre_transform(
+            stored, legendre, wavenumber, (wave_at * slot_count).astype(jnp.int32).reshape(1)
+        )
         .reshape(slot_count, legendre.shape[1], 2, levels, fields)
         .transpose(0, 1, 2, 4, 3)
         .reshape(slot_count, legendre.shape[1], channels)

time: 68.2 us -> 65.8 us (0.965)
  other arithmetic: 8.29 us -> 6.43 us
  local copies, waits for them, and re-layouts: 9.23 us -> 7.88 us
  waiting for transfers between devices: 13.3 us -> 14.6 us
    cos x1 -> x2, other arithmetic: 2.63 us -> 0.6 us  [the longest x1 0.35 us: quarter_tables(): fine_cos, fine_sin = (jnp.cos(fine_angle), jnp.sin(fine_angle))]
    dot_general x1, matrix products: 1.01 us -> 2.84 us  [local(): r_all = jnp.dot(lhs_cos, cos_tab, preferred_element_type=jnp.float32)]
    dot_general x1, matrix products: 2.84 us -> 1.01 us  [local(): q_all = jnp.dot(lhs_sin, sin_tab, preferred_element_type=jnp.float32)]
    all_to_all x1, waiting for transfers between devices: 0.01 us -> 1.79 us  [local(): lax.all_to_all(spec_grid, 'wave', split_axis=1, concat_axis=0, tiled=True)]
    dynamic_slice x1 -> x0, local copies, waits for them, and re-layouts: 1.35 us -> none  [local(): lax.dynamic_slice_in_dim(wavenumber, wave_at * slot_count, slot_count)]
  transfers between devices with their start and end apart: 3 -> 3, of which waited for: 2 -> 3; matrix products, arithmetic and copies ran while one was open for 10% -> 7% of each run, Pallas kernels for 0% -> 0%
where the time goes in v11:
time: 65.8 us; the launch traced here: 65.3 us
  Pallas kernels  19.1 us (29%)
  waiting for transfers between devices  14.6 us (22%)
  starting transfers between devices  13.2 us (20%)
  local copies, waits for them, and re-layouts  7.88 us (12%)
  other arithmetic  6.43 us (10%)
  matrix products  3.85 us (6%)
    pallas_call x1, Pallas kernels, legendre_transform(): pl.pallas_call(legendre_kernel, out_shape=jax.ShapeDtypeStruct((slots, la...  19.1 us
    all_to_all x1, waiting for transfers between devices, local(): lax.all_to_all(copies, ('wave', 'cpl'), split_axis=0, concat_axis=0, tile...  6.55 us
    all_to_all x1, waiting for transfers between devices, local(): lax.all_to_all(by_strip, 'lev', split_axis=0, concat_axis=0, tiled=True)  6.25 us
    all_to_all x1, starting transfers between devices, local(): lax.all_to_all(by_strip, 'lev', split_axis=0, concat_axis=0, tiled=True)  5.5 us
    all_to_all x1, starting transfers between devices, local(): lax.all_to_all(spec_grid, 'wave', split_axis=1, concat_axis=0, tiled=True)  4.24 us
    all_to_all x1, starting transfers between devices, local(): lax.all_to_all(copies, ('wave', 'cpl'), split_axis=0, concat_axis=0, tile...  3.42 us
    convert_element_type x1, other arithmetic, quarter_tables(): cos_tab.astype(jnp.bfloat16).reshape(slots, width)  3.35 us
    dot_general x1, matrix products, local(): r_all = jnp.dot(lhs_cos, cos_tab, preferred_element_type=jnp.float32)  2.84 us
  transfers between devices with their start and end apart: 3, of which 3 were waited for; matrix products, arithmetic and copies ran while one was open for 7% of the time, Pallas kernels for 0%

profile of v11, /device:TPU:0, one launch (start us, length us, event | category | flops | bytes accessed | tf_op | source)
XLA Modules:
  0.0 65.3 jit_solution(4543833976458158793)
XLA Ops:
  0.0 0.0 copy-start
  0.0 19.1 %shard_map.64 = bf16[320,8,48]{2,1,0:T(8,128)(2,1)} custom-call(s32[1]{0:T(128)} %bitcast.offset_ref, s32[1280]{0:T(1024)} %waves_ref.1, bf16[320,2,6,4,1280]{4,3,2,1,0:T(4,128)(2,1)} %bitcast.41, bf16[320,8,1280]{2,1,0:T(8,128)(2,1)} %table_ref.1), custom_call_target="tpu_custom_call" | custom-call | flops 314572800 | bytes 45875200 | tf_op jit(solution)/shard_map/pallas_call | solution.py:86
  19.1 1.7 %copy.19 = bf16[320,8,48]{0,1,2:T(8,128)(2,1)S(1)} copy(bf16[320,8,48]{2,1,0:T(8,128)(2,1)} %shard_map.64) | data formatting | bytes 491520 | tf_op jit(solution)/shard_map/pallas_call | solution.py:86
  20.8 0.8 %copy.21 = bf16[320,8,48]{0,2,1:T(8,128)(2,1)} copy(bf16[320,8,48]{0,1,2:T(8,128)(2,1)S(1)} %bitcast.48) | data formatting | bytes 491520 | tf_op jit(solution)/shard_map/reshape | solution.py:124
  21.6 4.2 %all-to-all-start = ((bf16[320,8,48]{0,2,1:T(8,128)(2,1)}), bf16[320,8,48]{0,2,1:T(8,128)(2,1)S(1)}, u32[]{:S(2)}, u32[]{:S(2)}) async-start(bf16[320,8,48]{0,2,1:T(8,128)(2,1)} %copy.21), calls=%async_computation | async-start | bytes 589824 | tf_op jit(solution)/shard_map/all_to_all | solution.py:126
  25.8 0.0 copy-done
  25.8 0.3 fusion.15
  26.2 0.3 fusion.45
  26.5 0.4 cosine_multiply_fusion
  26.9 0.2 multiply_subtract_fusion
  27.1 3.4 %subtract_convert_fusion = (bf16[1280,9,128]{0,2,1:T(8,128)(2,1)}, bf16[1280,9,128]{0,2,1:T(8,128)(2,1)S(1)}) fusion(f32[1280,128]{0,1:T(8,128)S(1)} %bitcast.45, f32[1280,9]{0,1:T(8,128)S(1)} %get-tuple-element.27, f32[1280,128]{0,1:T(8,128)S(1)} %bitcast.44, f32[1280,9]{0,1:T(8,128)S(1)} %get-tuple-element.26), kind=kLoop, calls=%fused_computation.3 | loop fusion | flops 13271040 | bytes 7301120 | tf_op jit(solution)/shard_map/convert_element_type | solution.py:57
  30.4 1.8 %all-to-all-done = bf16[320,8,48]{0,2,1:T(8,128)(2,1)S(1)} async-done(((bf16[320,8,48]{0,2,1:T(8,128)(2,1)}), bf16[320,8,48]{0,2,1:T(8,128)(2,1)S(1)}, u32[]{:S(2)}, u32[]{:S(2)}) %all-to-all-start) | async-done | bytes 245792 | tf_op jit(solution)/shard_map/all_to_all | solution.py:126
  32.2 0.2 copy.26
  32.4 0.3 reshape.336
  32.7 2.8 %fusion = f32[96,1152]{1,0:T(8,128)S(1)} fusion(bf16[1280,1152]{0,1:T(8,128)(2,1)} %bitcast.43, bf16[48,1280]{1,0:T(8,128)(2,1)S(1)} %get-tuple-element.32, bf16[48,1280]{1,0:T(8,128)(2,1)S(1)} %bitcast.52), kind=kOutput, calls=%fused_computation.11 | convolution fusion | flops 283607040 | bytes 3637248 | tf_op jit(solution)/shard_map/dot_general | solution.py:140
  35.6 0.0 copy-start.1
  35.6 1.0 %fusion.4 = f32[96,1152]{1,0:T(8,128)S(1)} fusion(bf16[1280,1152]{0,1:T(8,128)(2,1)S(1)} %bitcast.42, bf16[48,1280]{1,0:T(8,128)(2,1)S(1)} %get-tuple-element.33, bf16[48,1280]{1,0:T(8,128)(2,1)S(1)} %bitcast.51), kind=kOutput, calls=%fused_computation.15 | convolution fusion | flops 283607040 | bytes 3637248 | tf_op jit(solution)/shard_map/dot_general | solution.py:141
  36.6 0.0 copy-start.2
  36.6 0.0 copy-start.3
  36.7 0.3 slice_subtract_fusion
  37.2 0.0 copy-done.1
  37.2 0.2 fusion.24
  37.3 0.1 multiply_reduce_fusion
  37.4 0.8 %reverse.1 = f32[2,4,1152]{2,1,0:T(4,128)S(1)} reverse(f32[2,4,1152]{2,1,0:T(4,128)S(1)} %bitcast.56), dimensions={2} | reverse | bytes 73728
  38.3 0.1 slice.163
  38.4 0.1 multiply_reduce_fusion.1
  38.5 0.1 multiply_reduce_fusion.2
  38.6 0.8 %reverse = f32[2,4,1152]{2,1,0:T(4,128)S(1)} reverse(f32[2,4,1152]{2,1,0:T(4,128)S(1)} %bitcast.57), dimensions={2} | reverse | bytes 73728
  39.4 0.1 slice.162
  39.5 0.1 multiply_reduce_fusion.3
  39.6 0.2 concatenate.11
  39.8 0.2 reshape.341
  40.0 0.7 %copy.23 = f32[4,2,4,1080]{3,2,1,0:T(4,128)} copy(f32[4,2,4,1080]{3,0,2,1:T(4,128)S(1)} %bitcast.53) | data formatting | bytes 276480 | tf_op jit(solution)/shard_map/transpose | solution.py:158
  40.7 5.5 %all-to-all-start.1 = ((f32[4,2,4,1080]{3,2,1,0:T(4,128)}), f32[4,2,4,1080]{3,2,1,0:T(4,128)S(1)}, u32[]{:S(2)}, u32[]{:S(2)}) async-start(f32[4,2,4,1080]{3,2,1,0:T(4,128)} %copy.23), calls=%async_computation.1 | async-start | bytes 294912 | tf_op jit(solution)/shard_map/all_to_all | solution.py:160
  46.2 6.2 %all-to-all-done.1 = f32[4,2,4,1080]{3,2,1,0:T(4,128)S(1)} async-done(((f32[4,2,4,1080]{3,2,1,0:T(4,128)}), f32[4,2,4,1080]{3,2,1,0:T(4,128)S(1)}, u32[]{:S(2)}, u32[]{:S(2)}) %all-to-all-start.1) | async-done | bytes 138272 | tf_op jit(solution)/shard_map/all_to_all | solution.py:160
  52.4 0.8 %broadcast_in_dim.18 = f32[8,2,4,1080]{3,2,1,0:T(4,128)} broadcast(f32[2,4,1080]{2,1,0:T(4,128)S(1)} %reduce_sum.49), dimensions={1,2,3} | broadcast | bytes 311040 | tf_op jit(solution)/shard_map/broadcast_in_dim | solution.py:162
  53.2 3.4 %all-to-all-start.2 = ((f32[8,2,4,1080]{3,2,1,0:T(4,128)}), f32[8,2,4,1080]{3,2,1,0:T(4,128)S(1)}, u32[]{:S(2)}, u32[]{:S(2)}) async-start(f32[8,2,4,1080]{3,2,1,0:T(4,128)} %broadcast_in_dim.18), calls=%async_computation.2 | async-start | bytes 589824 | tf_op jit(solution)/shard_map/all_to_all | solution.py:163
  56.6 0.0 copy-done.2
  56.6 0.1 broadcast_subtract_fusion
  56.7 0.0 copy-done.3
  56.7 0.1 compare_and_fusion.1
  56.8 6.5 %all-to-all-done.2 = f32[8,2,4,1080]{3,2,1,0:T(4,128)S(1)} async-done(((f32[8,2,4,1080]{3,2,1,0:T(4,128)}), f32[8,2,4,1080]{3,2,1,0:T(4,128)S(1)}, u32[]{:S(2)}, u32[]{:S(2)}) %all-to-all-start.2) | async-done | bytes 276512 | tf_op jit(solution)/shard_map/all_to_all | solution.py:163
  63.4 0.6 gather_fusion
  64.0 0.6 gather_fusion.1
  64.6 0.7 %fusion.47 = f32[2,4,1080]{2,1,0:T(4,128)} fusion(f32[2,4,1080]{2,1,0:T(4,128)S(1)} %gather_fusion.1, f32[2,4,1080]{2,1,0:T(4,128)S(1)} %gather_fusion, f32[2]{0:T(128)S(1)} %get-tuple-element.11, f32[2]{0:T(128)S(1)} %get-tuple-element.10, pred[2]{0:T(512)(128)(4,1)S(1)} %get-tuple-element.34, pred[2]{0:T(512)(128)(4,1)S(1)} %get-tuple-element.6), kind=kLoop, calls=%fused_computation.81 | loop fusion | flops 43200 | bytes 103700 | tf_op jit(solution)/shard_map/add | solution.py:34
  (16 shorter events, 0.4 us)
Async XLA Ops:
  0.0 25.8 %copy-start = (s32[1280]{0:T(1024)S(1)}, s32[1280]{0:T(1024)}, u32[]{:S(2)}) copy-start(s32[1280]{0:T(1024)} %waves_ref.1) | copy-start | bytes 15364
  21.6 10.6 %all-to-all-start = ((bf16[320,8,48]{0,2,1:T(8,128)(2,1)}), bf16[320,8,48]{0,2,1:T(8,128)(2,1)S(1)}, u32[]{:S(2)}, u32[]{:S(2)}) async-start(bf16[320,8,48]{0,2,1:T(8,128)(2,1)} %copy.21), calls=%async_computation | async-start | bytes 589824 | tf_op jit(solution)/shard_map/all_to_all | solution.py:126
  35.6 1.6 %copy-start.1 = (f32[6]{0:T(128)S(1)}, f32[6]{0:T(128)}, u32[]{:S(2)}) copy-start(f32[6]{0:T(128)} %param.11) | copy-start | bytes 76
  36.6 20.0 %copy-start.2 = (f32[16]{0:T(128)S(1)}, f32[16]{0:T(128)}, u32[]{:S(2)}) copy-start(f32[16]{0:T(128)} %param.13) | copy-start | bytes 196
  36.6 20.1 %copy-start.3 = (s32[16]{0:T(128)S(1)}, s32[16]{0:T(128)}, u32[]{:S(2)}) copy-start(s32[16]{0:T(128)} %param.12) | copy-start | bytes 196
  40.7 11.8 %all-to-all-start.1 = ((f32[4,2,4,1080]{3,2,1,0:T(4,128)}), f32[4,2,4,1080]{3,2,1,0:T(4,128)S(1)}, u32[]{:S(2)}, u32[]{:S(2)}) async-start(f32[4,2,4,1080]{3,2,1,0:T(4,128)} %copy.23), calls=%async_computation.1 | async-start | bytes 294912 | tf_op jit(solution)/shard_map/all_to_all | solution.py:160
  53.2 10.2 %all-to-all-start.2 = ((f32[8,2,4,1080]{3,2,1,0:T(4,128)}), f32[8,2,4,1080]{3,2,1,0:T(4,128)S(1)}, u32[]{:S(2)}, u32[]{:S(2)}) async-start(f32[8,2,4,1080]{3,2,1,0:T(4,128)} %broadcast_in_dim.18), calls=%async_computation.2 | async-start | bytes 589824 | tf_op jit(solution)/shard_map/all_to_all | solution.py:163

commit v12 on v11

--- a/solution.py
+++ b/solution.py
@@ -17,8 +17,8 @@
 
 
 def surface_flux(grid_vals, level_weight):
-    wind_speed = jnp.sqrt(grid_vals[:, 0] ** 2 + grid_vals[:, 1] ** 2 + 0.25)
-    return jnp.sum(level_weight[:, None] * wind_speed[:, None] * grid_vals, axis=2)
+    wind_speed = jnp.sqrt(grid_vals[:, :, 0] ** 2 + grid_vals[:, :, 1] ** 2 + 0.25)
+    return jnp.sum(level_weight[:, None, None] * wind_speed[:, :, None] * grid_vals, axis=1)
 
 
 def latitude_order(gathered, wave_count, cpl_count, lat_dev):
@@ -115,13 +115,8 @@
     wave_at = lax.axis_index("wave")
     cpl_at = lax.axis_index("cpl")
     stored = jnp.transpose(spectral, (0, 1, 3, 2, 4))
-    spec_grid = (
-        legendre_transform(
-            stored, legendre, wavenumber, (wave_at * slot_count).astype(jnp.int32).reshape(1)
-        )
-        .reshape(slot_count, legendre.shape[1], 2, levels, fields)
-        .transpose(0, 1, 2, 4, 3)
-        .reshape(slot_count, legendre.shape[1], channels)
+    spec_grid = legendre_transform(
+        stored, legendre, wavenumber, (wave_at * slot_count).astype(jnp.int32).reshape(1)
     )
     by_latitude = lax.all_to_all(spec_grid, "wave", split_axis=1, concat_axis=0, tiled=True)
     total_slots = by_latitude.shape[0]
@@ -143,7 +138,7 @@
     q1, q2 = q_all[:rows], q_all[rows:]
 
     def flux_of(grid_rows):
-        return surface_flux(grid_rows.reshape(lat_dev, fields, levels, quarter), level_weight)
+        return surface_flux(grid_rows.reshape(lat_dev, levels, fields, quarter), level_weight)
 
     strip0 = flux_of((r1 + q1)[:, :quarter])
     strip1 = jnp.flip(flux_of((r2 - q2)[:, 1 : quarter + 1]), axis=-1)

time: 65.8 us -> 66.1 us (level)
  no operation moved by 1% of the time
where the time goes in v12:
time: 66.1 us; the launch traced here: 65.6 us
  Pallas kernels  19.1 us (29%)
  waiting for transfers between devices  14.6 us (22%)
  starting transfers between devices  13.2 us (20%)
  local copies, waits for them, and re-layouts  8.1 us (12%)
  other arithmetic  6.49 us (10%)
  matrix products  3.85 us (6%)
    pallas_call x1, Pallas kernels, legendre_transform(): pl.pallas_call(legendre_kernel, out_shape=jax.ShapeDtypeStruct((slots, la...  19.1 us
    all_to_all x1, waiting for transfers between devices, local(): lax.all_to_all(copies, ('wave', 'cpl'), split_axis=0, concat_axis=0, tile...  6.55 us
    all_to_all x1, waiting for transfers between devices, local(): lax.all_to_all(by_strip, 'lev', split_axis=0, concat_axis=0, tiled=True)  6.25 us
    all_to_all x1, starting transfers between devices, local(): lax.all_to_all(by_strip, 'lev', split_axis=0, concat_axis=0, tiled=True)  5.5 us
    all_to_all x1, starting transfers between devices, local(): lax.all_to_all(spec_grid, 'wave', split_axis=1, concat_axis=0, tiled=True)  4.24 us
    all_to_all x1, starting transfers between devices, local(): lax.all_to_all(copies, ('wave', 'cpl'), split_axis=0, concat_axis=0, tile...  3.42 us
    convert_element_type x1, other arithmetic, quarter_tables(): cos_tab.astype(jnp.bfloat16).reshape(slots, width)  3.33 us
    dot_general x1, matrix products, local(): r_all = jnp.dot(lhs_cos, cos_tab, preferred_element_type=jnp.float32)  2.84 us
  transfers between devices with their start and end apart: 3, of which 3 were waited for; matrix products, arithmetic and copies ran while one was open for 7% of the time, Pallas kernels for 0%

profile of v12, /device:TPU:0, one launch (start us, length us, event | category | flops | bytes accessed | tf_op | source)
XLA Modules:
  0.0 65.6 jit_solution(18337678206692541284)
XLA Ops:
  0.0 19.1 %shard_map.64 = bf16[320,8,48]{2,1,0:T(8,128)(2,1)} custom-call(s32[1]{0:T(128)} %bitcast.offset_ref, s32[1280]{0:T(1024)} %waves_ref.1, bf16[320,2,6,4,1280]{4,3,2,1,0:T(4,128)(2,1)} %bitcast.37, bf16[320,8,1280]{2,1,0:T(8,128)(2,1)} %table_ref.1), custom_call_target="tpu_custom_call" | custom-call | flops 314572800 | bytes 45875200 | tf_op jit(solution)/shard_map/pallas_call | solution.py:86
  19.1 2.1 %copy.49 = bf16[320,8,48]{0,2,1:T(8,128)(2,1)} copy(bf16[320,8,48]{2,1,0:T(8,128)(2,1)} %shard_map.64) | data formatting | bytes 491520 | tf_op jit(solution)/shard_map/pallas_call | solution.py:86
  21.2 4.2 %all-to-all-start = ((bf16[320,8,48]{0,2,1:T(8,128)(2,1)}), bf16[320,8,48]{0,2,1:T(8,128)(2,1)S(1)}, u32[]{:S(2)}, u32[]{:S(2)}) async-start(bf16[320,8,48]{0,2,1:T(8,128)(2,1)} %copy.49), calls=%async_computation | async-start | bytes 589824 | tf_op jit(solution)/shard_map/all_to_all | solution.py:121
  25.5 0.0 copy-done
  25.5 0.3 fusion.15
  25.9 0.3 fusion.37
  26.1 0.4 cosine_multiply_fusion
  26.5 0.2 multiply_subtract_fusion
  26.7 3.3 %subtract_convert_fusion = (bf16[1280,9,128]{0,2,1:T(8,128)(2,1)}, bf16[1280,9,128]{0,2,1:T(8,128)(2,1)S(1)}) fusion(f32[1280,128]{0,1:T(8,128)S(1)} %bitcast.41, f32[1280,9]{0,1:T(8,128)S(1)} %get-tuple-element.35, f32[1280,128]{0,1:T(8,128)S(1)} %bitcast.40, f32[1280,9]{0,1:T(8,128)S(1)} %get-tuple-element.34), kind=kLoop, calls=%fused_computation.3 | loop fusion | flops 13271040 | bytes 7301120 | tf_op jit(solution)/shard_map/convert_element_type | solution.py:57
  30.1 1.8 %all-to-all-done = bf16[320,8,48]{0,2,1:T(8,128)(2,1)S(1)} async-done(((bf16[320,8,48]{0,2,1:T(8,128)(2,1)}), bf16[320,8,48]{0,2,1:T(8,128)(2,1)S(1)}, u32[]{:S(2)}, u32[]{:S(2)}) %all-to-all-start) | async-done | bytes 245792 | tf_op jit(solution)/shard_map/all_to_all | solution.py:121
  31.9 0.2 copy.130
  32.0 0.3 reshape.328
  32.4 2.8 %fusion = f32[96,1152]{1,0:T(8,128)S(1)} fusion(bf16[1280,1152]{0,1:T(8,128)(2,1)} %bitcast.39, bf16[48,1280]{1,0:T(8,128)(2,1)S(1)} %get-tuple-element.40, bf16[48,1280]{1,0:T(8,128)(2,1)S(1)} %bitcast.46), kind=kOutput, calls=%fused_computation.7 | convolution fusion | flops 283607040 | bytes 3637248 | tf_op jit(solution)/shard_map/dot_general | solution.py:135
  35.2 0.0 copy-start.1
  35.3 1.0 %fusion.4 = f32[96,1152]{1,0:T(8,128)S(1)} fusion(bf16[1280,1152]{0,1:T(8,128)(2,1)S(1)} %bitcast.38, bf16[48,1280]{1,0:T(8,128)(2,1)S(1)} %get-tuple-element.41, bf16[48,1280]{1,0:T(8,128)(2,1)S(1)} %bitcast.45), kind=kOutput, calls=%fused_computation.11 | convolution fusion | flops 283607040 | bytes 3637248 | tf_op jit(solution)/shard_map/dot_general | solution.py:136
  36.3 0.0 copy-start.2
  36.3 0.0 copy-start.3
  36.3 0.3 slice_subtract_fusion
  36.7 0.1 reshape.332
  36.7 0.1 fusion.45
  36.8 0.1 reshape.331
  36.9 0.1 fusion.46
  37.0 0.1 reshape.330
  37.1 0.1 fusion.47
  37.2 0.1 reshape.329
  37.2 0.1 fusion.48
  37.3 0.4 multiply_bitcast_fusion
  37.8 0.1 multiply_reduce_fusion
  37.8 0.8 %reverse.1 = f32[2,4,1152]{2,1,0:T(4,128)S(1)} reverse(f32[2,4,1152]{2,1,0:T(4,128)S(1)} %bitcast.50), dimensions={2} | reverse | bytes 73728
  38.6 0.1 slice.107
  38.8 0.1 multiply_reduce_fusion.1
  38.9 0.1 multiply_reduce_fusion.2
  38.9 0.8 %reverse = f32[2,4,1152]{2,1,0:T(4,128)S(1)} reverse(f32[2,4,1152]{2,1,0:T(4,128)S(1)} %bitcast.51), dimensions={2} | reverse | bytes 73728
  39.7 0.1 slice.106
  39.9 0.1 multiply_reduce_fusion.3
  39.9 0.2 concatenate.11
  40.1 0.2 reshape.333
  40.3 0.7 %copy.63 = f32[4,2,4,1080]{3,2,1,0:T(4,128)} copy(f32[4,2,4,1080]{3,0,2,1:T(4,128)S(1)} %bitcast.47) | data formatting | bytes 276480 | tf_op jit(solution)/shard_map/transpose | solution.py:153
  41.0 5.5 %all-to-all-start.1 = ((f32[4,2,4,1080]{3,2,1,0:T(4,128)}), f32[4,2,4,1080]{3,2,1,0:T(4,128)S(1)}, u32[]{:S(2)}, u32[]{:S(2)}) async-start(f32[4,2,4,1080]{3,2,1,0:T(4,128)} %copy.63), calls=%async_computation.1 | async-start | bytes 294912 | tf_op jit(solution)/shard_map/all_to_all | solution.py:155
  46.5 6.2 %all-to-all-done.1 = f32[4,2,4,1080]{3,2,1,0:T(4,128)S(1)} async-done(((f32[4,2,4,1080]{3,2,1,0:T(4,128)}), f32[4,2,4,1080]{3,2,1,0:T(4,128)S(1)}, u32[]{:S(2)}, u32[]{:S(2)}) %all-to-all-start.1) | async-done | bytes 138272 | tf_op jit(solution)/shard_map/all_to_all | solution.py:155
  52.8 0.8 %broadcast_in_dim.18 = f32[8,2,4,1080]{3,2,1,0:T(4,128)} broadcast(f32[2,4,1080]{2,1,0:T(4,128)S(1)} %reduce_sum.49), dimensions={1,2,3} | broadcast | bytes 311040 | tf_op jit(solution)/shard_map/broadcast_in_dim | solution.py:157
  53.5 3.4 %all-to-all-start.2 = ((f32[8,2,4,1080]{3,2,1,0:T(4,128)}), f32[8,2,4,1080]{3,2,1,0:T(4,128)S(1)}, u32[]{:S(2)}, u32[]{:S(2)}) async-start(f32[8,2,4,1080]{3,2,1,0:T(4,128)} %broadcast_in_dim.18), calls=%async_computation.2 | async-start | bytes 589824 | tf_op jit(solution)/shard_map/all_to_all | solution.py:158
  57.0 0.1 broadcast_subtract_fusion
  57.1 0.1 compare_and_fusion.1
  57.2 6.5 %all-to-all-done.2 = f32[8,2,4,1080]{3,2,1,0:T(4,128)S(1)} async-done(((f32[8,2,4,1080]{3,2,1,0:T(4,128)}), f32[8,2,4,1080]{3,2,1,0:T(4,128)S(1)}, u32[]{:S(2)}, u32[]{:S(2)}) %all-to-all-start.2) | async-done | bytes 276512 | tf_op jit(solution)/shard_map/all_to_all | solution.py:158
  63.7 0.6 gather_fusion
  64.3 0.6 gather_fusion.1
  64.9 0.7 %fusion.39 = f32[2,4,1080]{2,1,0:T(4,128)} fusion(f32[2,4,1080]{2,1,0:T(4,128)S(1)} %gather_fusion.1, f32[2,4,1080]{2,1,0:T(4,128)S(1)} %gather_fusion, f32[2]{0:T(128)S(1)} %get-tuple-element.11, f32[2]{0:T(128)S(1)} %get-tuple-element.10, pred[2]{0:T(512)(128)(4,1)S(1)} %get-tuple-element.42, pred[2]{0:T(512)(128)(4,1)S(1)} %get-tuple-element.6), kind=kLoop, calls=%fused_computation.77 | loop fusion | flops 43200 | bytes 103700 | tf_op jit(solution)/shard_map/add | solution.py:34
  (19 shorter events, 0.3 us)
Async XLA Ops:
  0.0 25.5 %copy-start = (s32[1280]{0:T(1024)S(1)}, s32[1280]{0:T(1024)}, u32[]{:S(2)}) copy-start(s32[1280]{0:T(1024)} %waves_ref.1) | copy-start | bytes 15364
  21.2 10.6 %all-to-all-start = ((bf16[320,8,48]{0,2,1:T(8,128)(2,1)}), bf16[320,8,48]{0,2,1:T(8,128)(2,1)S(1)}, u32[]{:S(2)}, u32[]{:S(2)}) async-start(bf16[320,8,48]{0,2,1:T(8,128)(2,1)} %copy.49), calls=%async_computation | async-start | bytes 589824 | tf_op jit(solution)/shard_map/all_to_all | solution.py:121
  35.2 2.1 %copy-start.1 = (f32[6]{0:T(128)S(1)}, f32[6]{0:T(128)}, u32[]{:S(2)}) copy-start(f32[6]{0:T(128)} %param.11) | copy-start | bytes 76
  36.3 20.7 %copy-start.2 = (f32[16]{0:T(128)S(1)}, f32[16]{0:T(128)}, u32[]{:S(2)}) copy-start(f32[16]{0:T(128)} %param.13) | copy-start | bytes 196
  36.3 20.8 %copy-start.3 = (s32[16]{0:T(128)S(1)}, s32[16]{0:T(128)}, u32[]{:S(2)}) copy-start(s32[16]{0:T(128)} %param.12) | copy-start | bytes 196
  41.0 11.8 %all-to-all-start.1 = ((f32[4,2,4,1080]{3,2,1,0:T(4,128)}), f32[4,2,4,1080]{3,2,1,0:T(4,128)S(1)}, u32[]{:S(2)}, u32[]{:S(2)}) async-start(f32[4,2,4,1080]{3,2,1,0:T(4,128)} %copy.63), calls=%async_computation.1 | async-start | bytes 294912 | tf_op jit(solution)/shard_map/all_to_all | solution.py:155
  53.5 10.2 %all-to-all-start.2 = ((f32[8,2,4,1080]{3,2,1,0:T(4,128)}), f32[8,2,4,1080]{3,2,1,0:T(4,128)S(1)}, u32[]{:S(2)}, u32[]{:S(2)}) async-start(f32[8,2,4,1080]{3,2,1,0:T(4,128)} %broadcast_in_dim.18), calls=%async_computation.2 | async-start | bytes 589824 | tf_op jit(solution)/shard_map/all_to_all | solution.py:158

commit v13 on v11

--- a/solution.py
+++ b/solution.py
@@ -149,13 +149,17 @@
     strip1 = jnp.flip(flux_of((r2 - q2)[:, 1 : quarter + 1]), axis=-1)
     strip2 = flux_of((r2 + q2)[:, :quarter])
     strip3 = jnp.flip(flux_of((r1 - q1)[:, 1 : quarter + 1]), axis=-1)
-    partial_value = jnp.concatenate([strip0, strip1, strip2, strip3], axis=-1)
+    quarters = [strip0, strip1, strip2, strip3]
 
     own_first = (wave_at * cpl_count + cpl_at) * lat_dev
     source = lax.dynamic_slice_in_dim(source_row, own_first, lat_dev)
     weight_hi = lax.dynamic_slice_in_dim(row_weight, own_first, lat_dev)
     strip_width = NLON // lev_count
-    by_strip = partial_value.reshape(lat_dev, fields, lev_count, strip_width).transpose(2, 0, 1, 3)
+    if lev_count == len(quarters):
+        by_strip = jnp.stack(quarters)
+    else:
+        partial_value = jnp.concatenate(quarters, axis=-1)
+        by_strip = partial_value.reshape(lat_dev, fields, lev_count, strip_width).transpose(2, 0, 1, 3)
     summed = jnp.sum(
         lax.all_to_all(by_strip, "lev", split_axis=0, concat_axis=0, tiled=True), axis=0
     )

time: 65.8 us -> 65.4 us (level)
  local copies, waits for them, and re-layouts: 7.88 us -> 6.84 us
  other arithmetic: 6.43 us -> 7.12 us
    another operation x0 -> x1, other arithmetic: none -> 0.69 us  [local(): by_strip = jnp.stack(quarters)]
    transpose x1 -> x0, local copies, waits for them, and re-layouts: 0.68 us -> none  [local(): partial_value.reshape(lat_dev, fields, lev_count, strip_width)]
    unnamed x12 -> x10, local copies, waits for them, and re-layouts: 1.82 us -> 1.65 us
where the time goes in v13:
time: 65.4 us; the launch traced here: 64.9 us
  Pallas kernels  19.1 us (29%)
  waiting for transfers between devices  14.6 us (22%)
  starting transfers between devices  13.2 us (20%)
  other arithmetic  7.12 us (11%)
  local copies, waits for them, and re-layouts  6.84 us (10%)
  matrix products  3.85 us (6%)
    pallas_call x1, Pallas kernels, legendre_transform(): pl.pallas_call(legendre_kernel, out_shape=jax.ShapeDtypeStruct((slots, la...  19.1 us
    all_to_all x1, waiting for transfers between devices, local(): lax.all_to_all(copies, ('wave', 'cpl'), split_axis=0, concat_axis=0, tile...  6.55 us
    all_to_all x1, waiting for transfers between devices, local(): lax.all_to_all(by_strip, 'lev', split_axis=0, concat_axis=0, tiled=True)  6.25 us
    all_to_all x1, starting transfers between devices, local(): lax.all_to_all(by_strip, 'lev', split_axis=0, concat_axis=0, tiled=True)  5.5 us
    all_to_all x1, starting transfers between devices, local(): lax.all_to_all(spec_grid, 'wave', split_axis=1, concat_axis=0, tiled=True)  4.24 us
    all_to_all x1, starting transfers between devices, local(): lax.all_to_all(copies, ('wave', 'cpl'), split_axis=0, concat_axis=0, tile...  3.42 us
    convert_element_type x1, other arithmetic, quarter_tables(): cos_tab.astype(jnp.bfloat16).reshape(slots, width)  3.35 us
    dot_general x1, matrix products, local(): r_all = jnp.dot(lhs_cos, cos_tab, preferred_element_type=jnp.float32)  2.84 us
  transfers between devices with their start and end apart: 3, of which 3 were waited for; matrix products, arithmetic and copies ran while one was open for 7% of the time, Pallas kernels for 0%

profile of v13, /device:TPU:0, one launch (start us, length us, event | category | flops | bytes accessed | tf_op | source)
XLA Modules:
  0.0 64.9 jit_solution(3528324339930160588)
XLA Ops:
  0.0 0.0 copy-start
  0.0 19.1 %shard_map.64 = bf16[320,8,48]{2,1,0:T(8,128)(2,1)} custom-call(s32[1]{0:T(128)} %bitcast.offset_ref, s32[1280]{0:T(1024)} %waves_ref.1, bf16[320,2,6,4,1280]{4,3,2,1,0:T(4,128)(2,1)} %bitcast.46, bf16[320,8,1280]{2,1,0:T(8,128)(2,1)} %table_ref.1), custom_call_target="tpu_custom_call" | custom-call | flops 314572800 | bytes 45875200 | tf_op jit(solution)/shard_map/pallas_call | solution.py:86
  19.1 1.7 %copy.19 = bf16[320,8,48]{0,1,2:T(8,128)(2,1)S(1)} copy(bf16[320,8,48]{2,1,0:T(8,128)(2,1)} %shard_map.64) | data formatting | bytes 491520 | tf_op jit(solution)/shard_map/pallas_call | solution.py:86
  20.8 0.8 %copy.21 = bf16[320,8,48]{0,2,1:T(8,128)(2,1)} copy(bf16[320,8,48]{0,1,2:T(8,128)(2,1)S(1)} %bitcast.53) | data formatting | bytes 491520 | tf_op jit(solution)/shard_map/reshape | solution.py:124
  21.6 4.2 %all-to-all-start = ((bf16[320,8,48]{0,2,1:T(8,128)(2,1)}), bf16[320,8,48]{0,2,1:T(8,128)(2,1)S(1)}, u32[]{:S(2)}, u32[]{:S(2)}) async-start(bf16[320,8,48]{0,2,1:T(8,128)(2,1)} %copy.21), calls=%async_computation | async-start | bytes 589824 | tf_op jit(solution)/shard_map/all_to_all | solution.py:126
  25.8 0.0 copy-done
  25.8 0.3 fusion.15
  26.2 0.3 fusion.45
  26.5 0.4 cosine_multiply_fusion
  26.9 0.2 multiply_subtract_fusion
  27.1 3.4 %subtract_convert_fusion = (bf16[1280,9,128]{0,2,1:T(8,128)(2,1)}, bf16[1280,9,128]{0,2,1:T(8,128)(2,1)S(1)}) fusion(f32[1280,128]{0,1:T(8,128)S(1)} %bitcast.50, f32[1280,9]{0,1:T(8,128)S(1)} %get-tuple-element.27, f32[1280,128]{0,1:T(8,128)S(1)} %bitcast.49, f32[1280,9]{0,1:T(8,128)S(1)} %get-tuple-element.26), kind=kLoop, calls=%fused_computation.3 | loop fusion | flops 13271040 | bytes 7301120 | tf_op jit(solution)/shard_map/convert_element_type | solution.py:57
  30.4 1.8 %all-to-all-done = bf16[320,8,48]{0,2,1:T(8,128)(2,1)S(1)} async-done(((bf16[320,8,48]{0,2,1:T(8,128)(2,1)}), bf16[320,8,48]{0,2,1:T(8,128)(2,1)S(1)}, u32[]{:S(2)}, u32[]{:S(2)}) %all-to-all-start) | async-done | bytes 245792 | tf_op jit(solution)/shard_map/all_to_all | solution.py:126
  32.2 0.2 copy.25
  32.4 0.3 reshape.333
  32.7 2.8 %fusion = f32[96,1152]{1,0:T(8,128)S(1)} fusion(bf16[1280,1152]{0,1:T(8,128)(2,1)} %bitcast.48, bf16[48,1280]{1,0:T(8,128)(2,1)S(1)} %get-tuple-element.32, bf16[48,1280]{1,0:T(8,128)(2,1)S(1)} %bitcast.57), kind=kOutput, calls=%fused_computation.11 | convolution fusion | flops 283607040 | bytes 3637248 | tf_op jit(solution)/shard_map/dot_general | solution.py:140
  35.6 0.0 copy-start.1
  35.6 1.0 %fusion.4 = f32[96,1152]{1,0:T(8,128)S(1)} fusion(bf16[1280,1152]{0,1:T(8,128)(2,1)S(1)} %bitcast.47, bf16[48,1280]{1,0:T(8,128)(2,1)S(1)} %get-tuple-element.33, bf16[48,1280]{1,0:T(8,128)(2,1)S(1)} %bitcast.56), kind=kOutput, calls=%fused_computation.15 | convolution fusion | flops 283607040 | bytes 3637248 | tf_op jit(solution)/shard_map/dot_general | solution.py:141
  36.6 0.0 copy-start.2
  36.6 0.0 copy-start.3
  36.7 0.3 slice_subtract_fusion.1
  37.2 0.0 copy-done.1
  37.2 0.2 fusion.39
  37.3 0.1 multiply_reduce_fusion.3
  37.5 0.1 multiply_reduce_fusion.2
  37.6 0.8 %reverse.1 = f32[2,4,1152]{2,1,0:T(4,128)S(1)} reverse(f32[2,4,1152]{2,1,0:T(4,128)S(1)} %bitcast.62), dimensions={2} | reverse | bytes 73728
  38.4 0.1 slice_bitcast_fusion
  38.5 0.1 multiply_reduce_fusion.1
  38.6 0.1 multiply_reduce_fusion
  38.7 0.8 %reverse = f32[2,4,1152]{2,1,0:T(4,128)S(1)} reverse(f32[2,4,1152]{2,1,0:T(4,128)S(1)} %bitcast.63), dimensions={2} | reverse | bytes 73728
  39.5 0.1 slice_bitcast_fusion.1
  39.6 0.7 %pad_maximum_fusion = f32[4,2,4,1080]{3,2,1,0:T(4,128)} fusion(f32[1,2,4,1080]{3,2,1,0:T(4,128)S(1)} %slice_bitcast_fusion.1, f32[1,2,4,1080]{3,2,1,0:T(4,128)S(1)} %bitcast.61, f32[1,2,4,1080]{3,2,1,0:T(4,128)S(1)} %slice_bitcast_fusion, f32[1,2,4,1080]{3,2,1,0:T(4,128)S(1)} %bitcast.60), kind=kLoop, calls=%fused_computation.23 | loop fusion | flops 103680 | bytes 276480 | tf_op jit(solution)/shard_map/stack | solution.py:159
  40.3 5.5 %all-to-all-start.1 = ((f32[4,2,4,1080]{3,2,1,0:T(4,128)}), f32[4,2,4,1080]{3,2,1,0:T(4,128)S(1)}, u32[]{:S(2)}, u32[]{:S(2)}) async-start(f32[4,2,4,1080]{3,2,1,0:T(4,128)} %pad_maximum_fusion), calls=%async_computation.1 | async-start | bytes 294912 | tf_op jit(solution)/shard_map/all_to_all | solution.py:164
  45.8 6.2 %all-to-all-done.1 = f32[4,2,4,1080]{3,2,1,0:T(4,128)S(1)} async-done(((f32[4,2,4,1080]{3,2,1,0:T(4,128)}), f32[4,2,4,1080]{3,2,1,0:T(4,128)S(1)}, u32[]{:S(2)}, u32[]{:S(2)}) %all-to-all-start.1) | async-done | bytes 138272 | tf_op jit(solution)/shard_map/all_to_all | solution.py:164
  52.1 0.8 %broadcast_in_dim.18 = f32[8,2,4,1080]{3,2,1,0:T(4,128)} broadcast(f32[2,4,1080]{2,1,0:T(4,128)S(1)} %reduce_sum.49), dimensions={1,2,3} | broadcast | bytes 311040 | tf_op jit(solution)/shard_map/broadcast_in_dim | solution.py:166
  52.8 3.4 %all-to-all-start.2 = ((f32[8,2,4,1080]{3,2,1,0:T(4,128)}), f32[8,2,4,1080]{3,2,1,0:T(4,128)S(1)}, u32[]{:S(2)}, u32[]{:S(2)}) async-start(f32[8,2,4,1080]{3,2,1,0:T(4,128)} %broadcast_in_dim.18), calls=%async_computation.2 | async-start | bytes 589824 | tf_op jit(solution)/shard_map/all_to_all | solution.py:167
  56.3 0.0 copy-done.2
  56.3 0.1 broadcast_subtract_fusion
  56.4 0.0 copy-done.3
  56.4 0.1 compare_and_fusion.1
  56.5 6.5 %all-to-all-done.2 = f32[8,2,4,1080]{3,2,1,0:T(4,128)S(1)} async-done(((f32[8,2,4,1080]{3,2,1,0:T(4,128)}), f32[8,2,4,1080]{3,2,1,0:T(4,128)S(1)}, u32[]{:S(2)}, u32[]{:S(2)}) %all-to-all-start.2) | async-done | bytes 276512 | tf_op jit(solution)/shard_map/all_to_all | solution.py:167
  63.0 0.6 gather_fusion
  63.6 0.6 gather_fusion.1
  64.2 0.7 %fusion.47 = f32[2,4,1080]{2,1,0:T(4,128)} fusion(f32[2,4,1080]{2,1,0:T(4,128)S(1)} %gather_fusion.1, f32[2,4,1080]{2,1,0:T(4,128)S(1)} %gather_fusion, f32[2]{0:T(128)S(1)} %get-tuple-element.11, f32[2]{0:T(128)S(1)} %get-tuple-element.10, pred[2]{0:T(512)(128)(4,1)S(1)} %get-tuple-element.34, pred[2]{0:T(512)(128)(4,1)S(1)} %get-tuple-element.6), kind=kLoop, calls=%fused_computation.82 | loop fusion | flops 43200 | bytes 103700 | tf_op jit(solution)/shard_map/add | solution.py:34
  (16 shorter events, 0.4 us)
Async XLA Ops:
  0.0 25.8 %copy-start = (s32[1280]{0:T(1024)S(1)}, s32[1280]{0:T(1024)}, u32[]{:S(2)}) copy-start(s32[1280]{0:T(1024)} %waves_ref.1) | copy-start | bytes 15364
  21.6 10.6 %all-to-all-start = ((bf16[320,8,48]{0,2,1:T(8,128)(2,1)}), bf16[320,8,48]{0,2,1:T(8,128)(2,1)S(1)}, u32[]{:S(2)}, u32[]{:S(2)}) async-start(bf16[320,8,48]{0,2,1:T(8,128)(2,1)} %copy.21), calls=%async_computation | async-start | bytes 589824 | tf_op jit(solution)/shard_map/all_to_all | solution.py:126
  35.6 1.6 %copy-start.1 = (f32[6]{0:T(128)S(1)}, f32[6]{0:T(128)}, u32[]{:S(2)}) copy-start(f32[6]{0:T(128)} %param.11) | copy-start | bytes 76
  36.6 19.6 %copy-start.2 = (f32[16]{0:T(128)S(1)}, f32[16]{0:T(128)}, u32[]{:S(2)}) copy-start(f32[16]{0:T(128)} %param.13) | copy-start | bytes 196
  36.6 19.7 %copy-start.3 = (s32[16]{0:T(128)S(1)}, s32[16]{0:T(128)}, u32[]{:S(2)}) copy-start(s32[16]{0:T(128)} %param.12) | copy-start | bytes 196
  40.3 11.8 %all-to-all-start.1 = ((f32[4,2,4,1080]{3,2,1,0:T(4,128)}), f32[4,2,4,1080]{3,2,1,0:T(4,128)S(1)}, u32[]{:S(2)}, u32[]{:S(2)}) async-start(f32[4,2,4,1080]{3,2,1,0:T(4,128)} %pad_maximum_fusion), calls=%async_computation.1 | async-start | bytes 294912 | tf_op jit(solution)/shard_map/all_to_all | solution.py:164
  52.8 10.2 %all-to-all-start.2 = ((f32[8,2,4,1080]{3,2,1,0:T(4,128)}), f32[8,2,4,1080]{3,2,1,0:T(4,128)S(1)}, u32[]{:S(2)}, u32[]{:S(2)}) async-start(f32[8,2,4,1080]{3,2,1,0:T(4,128)} %broadcast_in_dim.18), calls=%async_computation.2 | async-start | bytes 589824 | tf_op jit(solution)/shard_map/all_to_all | solution.py:167

commit v14 on v13

--- a/solution.py
+++ b/solution.py
@@ -146,17 +146,17 @@
         return surface_flux(grid_rows.reshape(lat_dev, fields, levels, quarter), level_weight)
 
     strip0 = flux_of((r1 + q1)[:, :quarter])
-    strip1 = jnp.flip(flux_of((r2 - q2)[:, 1 : quarter + 1]), axis=-1)
+    mirror1 = flux_of((r2 - q2)[:, 1 : quarter + 1])
     strip2 = flux_of((r2 + q2)[:, :quarter])
-    strip3 = jnp.flip(flux_of((r1 - q1)[:, 1 : quarter + 1]), axis=-1)
-    quarters = [strip0, strip1, strip2, strip3]
+    mirror3 = flux_of((r1 - q1)[:, 1 : quarter + 1])
+    quarters = [strip0, jnp.flip(mirror1, axis=-1), strip2, jnp.flip(mirror3, axis=-1)]
 
     own_first = (wave_at * cpl_count + cpl_at) * lat_dev
     source = lax.dynamic_slice_in_dim(source_row, own_first, lat_dev)
     weight_hi = lax.dynamic_slice_in_dim(row_weight, own_first, lat_dev)
     strip_width = NLON // lev_count
     if lev_count == len(quarters):
-        by_strip = jnp.stack(quarters)
+        by_strip = jnp.stack([strip0, mirror1, strip2, mirror3])
     else:
         partial_value = jnp.concatenate(quarters, axis=-1)
         by_strip = partial_value.reshape(lat_dev, fields, lev_count, strip_width).transpose(2, 0, 1, 3)
@@ -167,7 +167,11 @@
     gathered = lax.all_to_all(copies, ("wave", "cpl"), split_axis=0, concat_axis=0, tiled=True)
     gathered = gathered.reshape((wave_count * cpl_count * lat_dev,) + summed.shape[1:])
     gathered = latitude_order(gathered, wave_count, cpl_count, lat_dev)
-    return interpolate(gathered, source, weight_hi)
+    result = interpolate(gathered, source, weight_hi)
+    if lev_count == len(quarters):
+        mirrored = lax.axis_index("lev") % 2 == 1
+        result = jnp.where(mirrored, jnp.flip(result, axis=-1), result)
+    return result
 
 
 def solution(mesh):

time: 65.4 us -> 64.5 us (0.986)
  local copies, waits for them, and re-layouts: 6.84 us -> 5.86 us
    unnamed x10 -> x9, local copies, waits for them, and re-layouts: 1.65 us -> 0.84 us
    select_n x0 -> x1, other arithmetic: none -> 0.72 us  [local(): result = jnp.where(mirrored, jnp.flip(result, axis=-1), result)]
where the time goes in v14:
time: 64.5 us; the launch traced here: 64 us
  Pallas kernels  19.1 us (30%)
  waiting for transfers between devices  14.6 us (23%)
  starting transfers between devices  13.2 us (20%)
  other arithmetic  7.2 us (11%)
  local copies, waits for them, and re-layouts  5.86 us (9%)
  matrix products  3.85 us (6%)
    pallas_call x1, Pallas kernels, legendre_transform(): pl.pallas_call(legendre_kernel, out_shape=jax.ShapeDtypeStruct((slots, la...  19.1 us
    all_to_all x1, waiting for transfers between devices, local(): lax.all_to_all(copies, ('wave', 'cpl'), split_axis=0, concat_axis=0, tile...  6.55 us
    all_to_all x1, waiting for transfers between devices, local(): lax.all_to_all(by_strip, 'lev', split_axis=0, concat_axis=0, tiled=True)  6.25 us
    all_to_all x1, starting transfers between devices, local(): lax.all_to_all(by_strip, 'lev', split_axis=0, concat_axis=0, tiled=True)  5.5 us
    all_to_all x1, starting transfers between devices, local(): lax.all_to_all(spec_grid, 'wave', split_axis=1, concat_axis=0, tiled=True)  4.24 us
    all_to_all x1, starting transfers between devices, local(): lax.all_to_all(copies, ('wave', 'cpl'), split_axis=0, concat_axis=0, tile...  3.42 us
    convert_element_type x1, other arithmetic, quarter_tables(): cos_tab.astype(jnp.bfloat16).reshape(slots, width)  3.35 us
    dot_general x1, matrix products, local(): r_all = jnp.dot(lhs_cos, cos_tab, preferred_element_type=jnp.float32)  2.84 us
  transfers between devices with their start and end apart: 3, of which 3 were waited for; matrix products, arithmetic and copies ran while one was open for 7% of the time, Pallas kernels for 0%

profile of v14, /device:TPU:0, one launch (start us, length us, event | category | flops | bytes accessed | tf_op | source)
XLA Modules:
  0.0 64.0 jit_solution(109718697461163350)
XLA Ops:
  0.0 0.0 copy-start
  0.0 19.1 %shard_map.64 = bf16[320,8,48]{2,1,0:T(8,128)(2,1)} custom-call(s32[1]{0:T(128)} %bitcast.offset_ref, s32[1280]{0:T(1024)} %waves_ref.1, bf16[320,2,6,4,1280]{4,3,2,1,0:T(4,128)(2,1)} %bitcast.43, bf16[320,8,1280]{2,1,0:T(8,128)(2,1)} %table_ref.1), custom_call_target="tpu_custom_call" | custom-call | flops 314572800 | bytes 45875200 | tf_op jit(solution)/shard_map/pallas_call | solution.py:86
  19.1 1.7 %copy.19 = bf16[320,8,48]{0,1,2:T(8,128)(2,1)S(1)} copy(bf16[320,8,48]{2,1,0:T(8,128)(2,1)} %shard_map.64) | data formatting | bytes 491520 | tf_op jit(solution)/shard_map/pallas_call | solution.py:86
  20.8 0.8 %copy.21 = bf16[320,8,48]{0,2,1:T(8,128)(2,1)} copy(bf16[320,8,48]{0,1,2:T(8,128)(2,1)S(1)} %bitcast.50) | data formatting | bytes 491520 | tf_op jit(solution)/shard_map/reshape | solution.py:124
  21.6 4.2 %all-to-all-start = ((bf16[320,8,48]{0,2,1:T(8,128)(2,1)}), bf16[320,8,48]{0,2,1:T(8,128)(2,1)S(1)}, u32[]{:S(2)}, u32[]{:S(2)}) async-start(bf16[320,8,48]{0,2,1:T(8,128)(2,1)} %copy.21), calls=%async_computation | async-start | bytes 589824 | tf_op jit(solution)/shard_map/all_to_all | solution.py:126
  25.8 0.0 copy-done
  25.8 0.3 fusion.15
  26.2 0.3 fusion.45
  26.5 0.4 cosine_multiply_fusion
  26.9 0.2 multiply_subtract_fusion
  27.1 3.4 %subtract_convert_fusion = (bf16[1280,9,128]{0,2,1:T(8,128)(2,1)}, bf16[1280,9,128]{0,2,1:T(8,128)(2,1)S(1)}) fusion(f32[1280,128]{0,1:T(8,128)S(1)} %bitcast.47, f32[1280,9]{0,1:T(8,128)S(1)} %get-tuple-element.27, f32[1280,128]{0,1:T(8,128)S(1)} %bitcast.46, f32[1280,9]{0,1:T(8,128)S(1)} %get-tuple-element.26), kind=kLoop, calls=%fused_computation.3 | loop fusion | flops 13271040 | bytes 7301120 | tf_op jit(solution)/shard_map/convert_element_type | solution.py:57
  30.4 1.8 %all-to-all-done = bf16[320,8,48]{0,2,1:T(8,128)(2,1)S(1)} async-done(((bf16[320,8,48]{0,2,1:T(8,128)(2,1)}), bf16[320,8,48]{0,2,1:T(8,128)(2,1)S(1)}, u32[]{:S(2)}, u32[]{:S(2)}) %all-to-all-start) | async-done | bytes 245792 | tf_op jit(solution)/shard_map/all_to_all | solution.py:126
  32.2 0.2 copy.25
  32.4 0.3 reshape.333
  32.7 2.8 %fusion = f32[96,1152]{1,0:T(8,128)S(1)} fusion(bf16[1280,1152]{0,1:T(8,128)(2,1)} %bitcast.45, bf16[48,1280]{1,0:T(8,128)(2,1)S(1)} %get-tuple-element.32, bf16[48,1280]{1,0:T(8,128)(2,1)S(1)} %bitcast.54), kind=kOutput, calls=%fused_computation.11 | convolution fusion | flops 283607040 | bytes 3637248 | tf_op jit(solution)/shard_map/dot_general | solution.py:140
  35.6 0.0 copy-start.1
  35.6 0.0 copy-start.2
  35.6 0.0 copy-start.3
  35.6 1.0 %fusion.4 = f32[96,1152]{1,0:T(8,128)S(1)} fusion(bf16[1280,1152]{0,1:T(8,128)(2,1)S(1)} %bitcast.44, bf16[48,1280]{1,0:T(8,128)(2,1)S(1)} %get-tuple-element.33, bf16[48,1280]{1,0:T(8,128)(2,1)S(1)} %bitcast.53), kind=kOutput, calls=%fused_computation.15 | convolution fusion | flops 283607040 | bytes 3637248 | tf_op jit(solution)/shard_map/dot_general | solution.py:141
  36.7 0.3 slice_subtract_fusion.1
  37.2 0.0 copy-done.1
  37.2 0.2 fusion.39
  37.3 0.1 multiply_reduce_fusion.3
  37.5 0.1 multiply_reduce_fusion.2
  37.6 0.1 multiply_reduce_fusion.1
  37.7 0.1 multiply_reduce_fusion
  37.8 0.7 %pad_maximum_fusion = f32[4,2,4,1080]{3,2,1,0:T(4,128)} fusion(f32[1,2,4,1080]{3,2,1,0:T(4,128)S(1)} %bitcast.61, f32[1,2,4,1080]{3,2,1,0:T(4,128)S(1)} %bitcast.60, f32[1,2,4,1080]{3,2,1,0:T(4,128)S(1)} %bitcast.59, f32[1,2,4,1080]{3,2,1,0:T(4,128)S(1)} %bitcast.58), kind=kLoop, calls=%fused_computation.23 | loop fusion | flops 103680 | bytes 276480 | tf_op jit(solution)/shard_map/stack | solution.py:159
  38.5 5.5 %all-to-all-start.1 = ((f32[4,2,4,1080]{3,2,1,0:T(4,128)}), f32[4,2,4,1080]{3,2,1,0:T(4,128)S(1)}, u32[]{:S(2)}, u32[]{:S(2)}) async-start(f32[4,2,4,1080]{3,2,1,0:T(4,128)} %pad_maximum_fusion), calls=%async_computation.1 | async-start | bytes 294912 | tf_op jit(solution)/shard_map/all_to_all | solution.py:164
  44.0 6.2 %all-to-all-done.1 = f32[4,2,4,1080]{3,2,1,0:T(4,128)S(1)} async-done(((f32[4,2,4,1080]{3,2,1,0:T(4,128)}), f32[4,2,4,1080]{3,2,1,0:T(4,128)S(1)}, u32[]{:S(2)}, u32[]{:S(2)}) %all-to-all-start.1) | async-done | bytes 138272 | tf_op jit(solution)/shard_map/all_to_all | solution.py:164
  50.3 0.8 %broadcast_in_dim.18 = f32[8,2,4,1080]{3,2,1,0:T(4,128)} broadcast(f32[2,4,1080]{2,1,0:T(4,128)S(1)} %reduce_sum.49), dimensions={1,2,3} | broadcast | bytes 311040 | tf_op jit(solution)/shard_map/broadcast_in_dim | solution.py:166
  51.0 3.4 %all-to-all-start.2 = ((f32[8,2,4,1080]{3,2,1,0:T(4,128)}), f32[8,2,4,1080]{3,2,1,0:T(4,128)S(1)}, u32[]{:S(2)}, u32[]{:S(2)}) async-start(f32[8,2,4,1080]{3,2,1,0:T(4,128)} %broadcast_in_dim.18), calls=%async_computation.2 | async-start | bytes 589824 | tf_op jit(solution)/shard_map/all_to_all | solution.py:167
  54.4 0.0 copy-done.2
  54.5 0.1 broadcast_subtract_fusion
  54.5 0.0 copy-done.3
  54.5 0.1 compare_and_fusion.1
  54.6 6.5 %all-to-all-done.2 = f32[8,2,4,1080]{3,2,1,0:T(4,128)S(1)} async-done(((f32[8,2,4,1080]{3,2,1,0:T(4,128)}), f32[8,2,4,1080]{3,2,1,0:T(4,128)S(1)}, u32[]{:S(2)}, u32[]{:S(2)}) %all-to-all-start.2) | async-done | bytes 276512 | tf_op jit(solution)/shard_map/all_to_all | solution.py:167
  61.2 0.6 gather_fusion
  61.8 0.6 gather_fusion.1
  62.4 0.1 fusion.47
  62.5 0.8 %reverse = f32[2,4,1152]{2,1,0:T(4,128)S(1)} reverse(f32[2,4,1152]{2,1,0:T(4,128)S(1)} %bitcast.57), dimensions={2} | reverse | bytes 73728
  63.3 0.7 %broadcast_select_fusion = f32[2,4,1080]{2,1,0:T(4,128)} fusion(f32[2,4,1080]{2,1,0:T(4,128)S(1)} %fusion.47, pred[]{:T(512)S(6)} %eq.17, f32[2,4,1152]{2,1,0:T(4,128)S(1)} %reverse), kind=kLoop, calls=%fused_computation.84 | loop fusion | flops 8640 | bytes 103681 | tf_op jit(solution)/shard_map/jit(_where)/select_n | solution.py:173
  (16 shorter events, 0.4 us)
Async XLA Ops:
  0.0 25.8 %copy-start = (s32[1280]{0:T(1024)S(1)}, s32[1280]{0:T(1024)}, u32[]{:S(2)}) copy-start(s32[1280]{0:T(1024)} %waves_ref.1) | copy-start | bytes 15364
  21.6 10.6 %all-to-all-start = ((bf16[320,8,48]{0,2,1:T(8,128)(2,1)}), bf16[320,8,48]{0,2,1:T(8,128)(2,1)S(1)}, u32[]{:S(2)}, u32[]{:S(2)}) async-start(bf16[320,8,48]{0,2,1:T(8,128)(2,1)} %copy.21), calls=%async_computation | async-start | bytes 589824 | tf_op jit(solution)/shard_map/all_to_all | solution.py:126
  35.6 1.6 %copy-start.1 = (f32[6]{0:T(128)S(1)}, f32[6]{0:T(128)}, u32[]{:S(2)}) copy-start(f32[6]{0:T(128)} %param.11) | copy-start | bytes 76
  35.6 18.8 %copy-start.2 = (f32[16]{0:T(128)S(1)}, f32[16]{0:T(128)}, u32[]{:S(2)}) copy-start(f32[16]{0:T(128)} %param.13) | copy-start | bytes 196
  35.6 18.9 %copy-start.3 = (s32[16]{0:T(128)S(1)}, s32[16]{0:T(128)}, u32[]{:S(2)}) copy-start(s32[16]{0:T(128)} %param.12) | copy-start | bytes 196
  38.5 11.8 %all-to-all-start.1 = ((f32[4,2,4,1080]{3,2,1,0:T(4,128)}), f32[4,2,4,1080]{3,2,1,0:T(4,128)S(1)}, u32[]{:S(2)}, u32[]{:S(2)}) async-start(f32[4,2,4,1080]{3,2,1,0:T(4,128)} %pad_maximum_fusion), calls=%async_computation.1 | async-start | bytes 294912 | tf_op jit(solution)/shard_map/all_to_all | solution.py:164
  51.0 10.2 %all-to-all-start.2 = ((f32[8,2,4,1080]{3,2,1,0:T(4,128)}), f32[8,2,4,1080]{3,2,1,0:T(4,128)S(1)}, u32[]{:S(2)}, u32[]{:S(2)}) async-start(f32[8,2,4,1080]{3,2,1,0:T(4,128)} %broadcast_in_dim.18), calls=%async_computation.2 | async-start | bytes 589824 | tf_op jit(solution)/shard_map/all_to_all | solution.py:167

commit v15 on v14

--- a/solution.py
+++ b/solution.py
@@ -9,7 +9,7 @@
 
 NLON = 4320
 LANE = 128
-SLOT_BLOCK = 64
+SLOT_BLOCK = 80
 
 
 def phase_angle(phase, lon_total):

time: 64.5 us -> 64.4 us (level)
  no operation moved by 1% of the time
where the time goes in v15:
time: 64.4 us; the launch traced here: 63.8 us
  Pallas kernels  19 us (30%)
  waiting for transfers between devices  14.6 us (23%)
  starting transfers between devices  13.2 us (20%)
  other arithmetic  7.2 us (11%)
  local copies, waits for them, and re-layouts  5.86 us (9%)
  matrix products  3.85 us (6%)
    pallas_call x1, Pallas kernels, legendre_transform(): pl.pallas_call(legendre_kernel, out_shape=jax.ShapeDtypeStruct((slots, la...  19 us
    all_to_all x1, waiting for transfers between devices, local(): lax.all_to_all(copies, ('wave', 'cpl'), split_axis=0, concat_axis=0, tile...  6.55 us
    all_to_all x1, waiting for transfers between devices, local(): lax.all_to_all(by_strip, 'lev', split_axis=0, concat_axis=0, tiled=True)  6.25 us
    all_to_all x1, starting transfers between devices, local(): lax.all_to_all(by_strip, 'lev', split_axis=0, concat_axis=0, tiled=True)  5.5 us
    all_to_all x1, starting transfers between devices, local(): lax.all_to_all(spec_grid, 'wave', split_axis=1, concat_axis=0, tiled=True)  4.24 us
    all_to_all x1, starting transfers between devices, local(): lax.all_to_all(copies, ('wave', 'cpl'), split_axis=0, concat_axis=0, tile...  3.42 us
    convert_element_type x1, other arithmetic, quarter_tables(): cos_tab.astype(jnp.bfloat16).reshape(slots, width)  3.35 us
    dot_general x1, matrix products, local(): r_all = jnp.dot(lhs_cos, cos_tab, preferred_element_type=jnp.float32)  2.84 us
  transfers between devices with their start and end apart: 3, of which 3 were waited for; matrix products, arithmetic and copies ran while one was open for 7% of the time, Pallas kernels for 0%

profile of v15, /device:TPU:0, one launch (start us, length us, event | category | flops | bytes accessed | tf_op | source)
XLA Modules:
  0.0 63.8 jit_solution(7253933350736290748)
XLA Ops:
  0.0 0.0 copy-start
  0.0 19.0 %shard_map.64 = bf16[320,8,48]{2,1,0:T(8,128)(2,1)} custom-call(s32[1]{0:T(128)} %bitcast.offset_ref, s32[1280]{0:T(1024)} %waves_ref.1, bf16[320,2,6,4,1280]{4,3,2,1,0:T(4,128)(2,1)} %bitcast.43, bf16[320,8,1280]{2,1,0:T(8,128)(2,1)} %table_ref.1), custom_call_target="tpu_custom_call" | custom-call | flops 314572800 | bytes 45875200 | tf_op jit(solution)/shard_map/pallas_call | solution.py:86
  19.0 1.7 %copy.19 = bf16[320,8,48]{0,1,2:T(8,128)(2,1)S(1)} copy(bf16[320,8,48]{2,1,0:T(8,128)(2,1)} %shard_map.64) | data formatting | bytes 491520 | tf_op jit(solution)/shard_map/pallas_call | solution.py:86
  20.7 0.8 %copy.21 = bf16[320,8,48]{0,2,1:T(8,128)(2,1)} copy(bf16[320,8,48]{0,1,2:T(8,128)(2,1)S(1)} %bitcast.50) | data formatting | bytes 491520 | tf_op jit(solution)/shard_map/reshape | solution.py:124
  21.5 4.2 %all-to-all-start = ((bf16[320,8,48]{0,2,1:T(8,128)(2,1)}), bf16[320,8,48]{0,2,1:T(8,128)(2,1)S(1)}, u32[]{:S(2)}, u32[]{:S(2)}) async-start(bf16[320,8,48]{0,2,1:T(8,128)(2,1)} %copy.21), calls=%async_computation | async-start | bytes 589824 | tf_op jit(solution)/shard_map/all_to_all | solution.py:126
  25.7 0.0 copy-done
  25.7 0.3 fusion.15
  26.1 0.3 fusion.45
  26.3 0.4 cosine_multiply_fusion
  26.7 0.2 multiply_subtract_fusion
  26.9 3.4 %subtract_convert_fusion = (bf16[1280,9,128]{0,2,1:T(8,128)(2,1)}, bf16[1280,9,128]{0,2,1:T(8,128)(2,1)S(1)}) fusion(f32[1280,128]{0,1:T(8,128)S(1)} %bitcast.47, f32[1280,9]{0,1:T(8,128)S(1)} %get-tuple-element.27, f32[1280,128]{0,1:T(8,128)S(1)} %bitcast.46, f32[1280,9]{0,1:T(8,128)S(1)} %get-tuple-element.26), kind=kLoop, calls=%fused_computation.3 | loop fusion | flops 13271040 | bytes 7301120 | tf_op jit(solution)/shard_map/convert_element_type | solution.py:57
  30.3 1.8 %all-to-all-done = bf16[320,8,48]{0,2,1:T(8,128)(2,1)S(1)} async-done(((bf16[320,8,48]{0,2,1:T(8,128)(2,1)}), bf16[320,8,48]{0,2,1:T(8,128)(2,1)S(1)}, u32[]{:S(2)}, u32[]{:S(2)}) %all-to-all-start) | async-done | bytes 245792 | tf_op jit(solution)/shard_map/all_to_all | solution.py:126
  32.1 0.2 copy.25
  32.2 0.3 reshape.333
  32.6 2.8 %fusion = f32[96,1152]{1,0:T(8,128)S(1)} fusion(bf16[1280,1152]{0,1:T(8,128)(2,1)} %bitcast.45, bf16[48,1280]{1,0:T(8,128)(2,1)S(1)} %get-tuple-element.32, bf16[48,1280]{1,0:T(8,128)(2,1)S(1)} %bitcast.54), kind=kOutput, calls=%fused_computation.11 | convolution fusion | flops 283607040 | bytes 3637248 | tf_op jit(solution)/shard_map/dot_general | solution.py:140
  35.4 0.0 copy-start.1
  35.5 0.0 copy-start.2
  35.5 0.0 copy-start.3
  35.5 1.0 %fusion.4 = f32[96,1152]{1,0:T(8,128)S(1)} fusion(bf16[1280,1152]{0,1:T(8,128)(2,1)S(1)} %bitcast.44, bf16[48,1280]{1,0:T(8,128)(2,1)S(1)} %get-tuple-element.33, bf16[48,1280]{1,0:T(8,128)(2,1)S(1)} %bitcast.53), kind=kOutput, calls=%fused_computation.15 | convolution fusion | flops 283607040 | bytes 3637248 | tf_op jit(solution)/shard_map/dot_general | solution.py:141
  36.5 0.3 slice_subtract_fusion.1
  37.0 0.0 copy-done.1
  37.0 0.2 fusion.39
  37.2 0.1 multiply_reduce_fusion.3
  37.3 0.1 multiply_reduce_fusion.2
  37.4 0.1 multiply_reduce_fusion.1
  37.5 0.1 multiply_reduce_fusion
  37.6 0.7 %pad_maximum_fusion = f32[4,2,4,1080]{3,2,1,0:T(4,128)} fusion(f32[1,2,4,1080]{3,2,1,0:T(4,128)S(1)} %bitcast.61, f32[1,2,4,1080]{3,2,1,0:T(4,128)S(1)} %bitcast.60, f32[1,2,4,1080]{3,2,1,0:T(4,128)S(1)} %bitcast.59, f32[1,2,4,1080]{3,2,1,0:T(4,128)S(1)} %bitcast.58), kind=kLoop, calls=%fused_computation.23 | loop fusion | flops 103680 | bytes 276480 | tf_op jit(solution)/shard_map/stack | solution.py:159
  38.3 5.5 %all-to-all-start.1 = ((f32[4,2,4,1080]{3,2,1,0:T(4,128)}), f32[4,2,4,1080]{3,2,1,0:T(4,128)S(1)}, u32[]{:S(2)}, u32[]{:S(2)}) async-start(f32[4,2,4,1080]{3,2,1,0:T(4,128)} %pad_maximum_fusion), calls=%async_computation.1 | async-start | bytes 294912 | tf_op jit(solution)/shard_map/all_to_all | solution.py:164
  43.8 6.2 %all-to-all-done.1 = f32[4,2,4,1080]{3,2,1,0:T(4,128)S(1)} async-done(((f32[4,2,4,1080]{3,2,1,0:T(4,128)}), f32[4,2,4,1080]{3,2,1,0:T(4,128)S(1)}, u32[]{:S(2)}, u32[]{:S(2)}) %all-to-all-start.1) | async-done | bytes 138272 | tf_op jit(solution)/shard_map/all_to_all | solution.py:164
  50.1 0.8 %broadcast_in_dim.18 = f32[8,2,4,1080]{3,2,1,0:T(4,128)} broadcast(f32[2,4,1080]{2,1,0:T(4,128)S(1)} %reduce_sum.49), dimensions={1,2,3} | broadcast | bytes 311040 | tf_op jit(solution)/shard_map/broadcast_in_dim | solution.py:166
  50.9 3.4 %all-to-all-start.2 = ((f32[8,2,4,1080]{3,2,1,0:T(4,128)}), f32[8,2,4,1080]{3,2,1,0:T(4,128)S(1)}, u32[]{:S(2)}, u32[]{:S(2)}) async-start(f32[8,2,4,1080]{3,2,1,0:T(4,128)} %broadcast_in_dim.18), calls=%async_computation.2 | async-start | bytes 589824 | tf_op jit(solution)/shard_map/all_to_all | solution.py:167
  54.3 0.0 copy-done.2
  54.3 0.1 broadcast_subtract_fusion
  54.4 0.0 copy-done.3
  54.4 0.1 compare_and_fusion.1
  54.5 6.5 %all-to-all-done.2 = f32[8,2,4,1080]{3,2,1,0:T(4,128)S(1)} async-done(((f32[8,2,4,1080]{3,2,1,0:T(4,128)}), f32[8,2,4,1080]{3,2,1,0:T(4,128)S(1)}, u32[]{:S(2)}, u32[]{:S(2)}) %all-to-all-start.2) | async-done | bytes 276512 | tf_op jit(solution)/shard_map/all_to_all | solution.py:167
  61.1 0.6 gather_fusion
  61.6 0.6 gather_fusion.1
  62.2 0.1 fusion.47
  62.3 0.8 %reverse = f32[2,4,1152]{2,1,0:T(4,128)S(1)} reverse(f32[2,4,1152]{2,1,0:T(4,128)S(1)} %bitcast.57), dimensions={2} | reverse | bytes 73728
  63.1 0.7 %broadcast_select_fusion = f32[2,4,1080]{2,1,0:T(4,128)} fusion(f32[2,4,1080]{2,1,0:T(4,128)S(1)} %fusion.47, pred[]{:T(512)S(6)} %eq.17, f32[2,4,1152]{2,1,0:T(4,128)S(1)} %reverse), kind=kLoop, calls=%fused_computation.84 | loop fusion | flops 8640 | bytes 103681 | tf_op jit(solution)/shard_map/jit(_where)/select_n | solution.py:173
  (16 shorter events, 0.4 us)
Async XLA Ops:
  0.0 25.7 %copy-start = (s32[1280]{0:T(1024)S(1)}, s32[1280]{0:T(1024)}, u32[]{:S(2)}) copy-start(s32[1280]{0:T(1024)} %waves_ref.1) | copy-start | bytes 15364
  21.5 10.6 %all-to-all-start = ((bf16[320,8,48]{0,2,1:T(8,128)(2,1)}), bf16[320,8,48]{0,2,1:T(8,128)(2,1)S(1)}, u32[]{:S(2)}, u32[]{:S(2)}) async-start(bf16[320,8,48]{0,2,1:T(8,128)(2,1)} %copy.21), calls=%async_computation | async-start | bytes 589824 | tf_op jit(solution)/shard_map/all_to_all | solution.py:126
  35.4 1.6 %copy-start.1 = (f32[6]{0:T(128)S(1)}, f32[6]{0:T(128)}, u32[]{:S(2)}) copy-start(f32[6]{0:T(128)} %param.11) | copy-start | bytes 76
  35.5 18.8 %copy-start.2 = (f32[16]{0:T(128)S(1)}, f32[16]{0:T(128)}, u32[]{:S(2)}) copy-start(f32[16]{0:T(128)} %param.13) | copy-start | bytes 196
  35.5 18.9 %copy-start.3 = (s32[16]{0:T(128)S(1)}, s32[16]{0:T(128)}, u32[]{:S(2)}) copy-start(s32[16]{0:T(128)} %param.12) | copy-start | bytes 196
  38.3 11.8 %all-to-all-start.1 = ((f32[4,2,4,1080]{3,2,1,0:T(4,128)}), f32[4,2,4,1080]{3,2,1,0:T(4,128)S(1)}, u32[]{:S(2)}, u32[]{:S(2)}) async-start(f32[4,2,4,1080]{3,2,1,0:T(4,128)} %pad_maximum_fusion), calls=%async_computation.1 | async-start | bytes 294912 | tf_op jit(solution)/shard_map/all_to_all | solution.py:164
  50.9 10.2 %all-to-all-start.2 = ((f32[8,2,4,1080]{3,2,1,0:T(4,128)}), f32[8,2,4,1080]{3,2,1,0:T(4,128)S(1)}, u32[]{:S(2)}, u32[]{:S(2)}) async-start(f32[8,2,4,1080]{3,2,1,0:T(4,128)} %broadcast_in_dim.18), calls=%async_computation.2 | async-start | bytes 589824 | tf_op jit(solution)/shard_map/all_to_all | solution.py:167
